TPU v7x, 512 devices: a whole 4x8x8 slice. The times are simulated.
512 devices in a mesh: tm: 32 (over y, x), rows: 16 (over z, core).
Axes of the slice: x: 4, y: 8, z: 8, core: 2. Of those that a mesh axis runs over, the one named last changes fastest.
Arguments:
- features: bfloat16 [64, 16, 40, 384], P('tm', 'rows'), may hold values from -6 to 6
- gain_one: float32 [384], replicated, may hold values from 0.1 to 1.9
- weight_one: bfloat16 [384, 3, 3, 3, 384], P('rows'), may hold values from -0.0625 to 0.0625
- bias_one: float32 [384], replicated, may hold values from -3 to 3
- gain_two: float32 [384], replicated, may hold values from 0.1 to 1.9
- weight_two: bfloat16 [384, 3, 3, 3, 384], P('rows'), may hold values from -0.0625 to 0.0625
- bias_two: float32 [384], replicated, may hold values from -3 to 3
Outputs:
- block_out: bfloat16 [64, 16, 40, 384], P('tm', 'rows')
All inputs are finite; a program needn't handle non-finite values.
Results may differ from a plain program's by a relative error of at most 0.0049.
Values may be sent and summed in bfloat16 or wider, within the bound.
No kernel may reach another device: no remote copies, remote signals or barrier semaphores. Data moves between devices by JAX's collectives and lax.ppermute only.
A program may use at most 64 MiB of HBM per device.

v0:
```python
import jax
import jax.numpy as jnp
from jax import lax
from jax.sharding import PartitionSpec as P


def passed_along(x, axis, by):
    peers = lax.axis_size(axis)
    pairs = [(i, i + by) for i in range(peers) if 0 <= i + by < peers]
    return lax.ppermute(x, axis, pairs)


def norm_silu(values, norm_gain):
    values = values.astype(jnp.float32)
    mean_square = jnp.mean(values * values, axis=-1, keepdims=True)
    scaled = values * lax.rsqrt(mean_square + 1e-06) * norm_gain
    return jax.nn.silu(scaled).astype(jnp.bfloat16)


def causal_conv(extended, kernel, bias_part):
    frames = extended.shape[0] - 2
    height = extended.shape[1]
    columns = extended.shape[2]
    channels = extended.shape[3]
    part_width = kernel.shape[0]
    folded = 9 * part_width
    padded_width = (folded + 127) // 128 * 128
    padded = jnp.pad(extended, ((0, 0), (1, 1), (1, 1), (0, 0)))
    summed = jnp.zeros((frames, height, columns, part_width), jnp.float32)
    for tap_time in range(3):
        slab = padded[tap_time : tap_time + frames]
        taps = jnp.transpose(kernel[:, tap_time], (1, 2, 0, 3)).reshape(folded, channels)
        taps = jnp.pad(taps, ((0, padded_width - folded), (0, 0)))
        product = lax.dot_general(
            slab.reshape(-1, channels),
            taps,
            (((1,), (1,)), ((), ())),
            preferred_element_type=jnp.float32,
        )
        product = product[:, :folded].reshape(frames, height + 2, columns + 2, 3, 3, part_width)
        for tap_row in range(3):
            for tap_col in range(3):
                summed = (
                    summed
                    + product[
                        :, tap_row : tap_row + height, tap_col : tap_col + columns, tap_row, tap_col
                    ]
                )
    return summed + bias_part


def shards(features, gain_one, weight_one, bias_one, gain_two, weight_two, bias_two):
    part_width = weight_one.shape[0]
    offset = lax.axis_index("rows") * part_width
    bias_first = lax.dynamic_slice_in_dim(bias_one, offset, part_width, 0)
    bias_second = lax.dynamic_slice_in_dim(bias_two, offset, part_width, 0)
    normed_one = norm_silu(features, gain_one)
    prior_one = passed_along(normed_one, "tm", 1)
    extended_one = jnp.concatenate([prior_one, normed_one], 0)
    full_one = lax.all_gather(extended_one, "rows", axis=1, tiled=True)
    conv_one = causal_conv(full_one, weight_one, bias_first).astype(jnp.bfloat16)
    own_rows = lax.all_to_all(conv_one, "rows", split_axis=1, concat_axis=3, tiled=True)
    normed_two = norm_silu(own_rows, gain_two)
    prior_two = passed_along(normed_two, "tm", 1)
    extended_two = jnp.concatenate([prior_two, normed_two], 0)
    full_two = lax.all_gather(extended_two, "rows", axis=1, tiled=True)
    conv_two = causal_conv(full_two, weight_two, bias_second)
    returned = lax.all_to_all(conv_two, "rows", split_axis=1, concat_axis=3, tiled=True)
    return (features.astype(jnp.float32) + returned).astype(jnp.bfloat16)


def solution(mesh):
    in_specs = (
        P("tm", "rows", None, None),
        P(),
        P("rows", None, None, None, None),
        P(),
        P(),
        P("rows", None, None, None, None),
        P(),
    )
    out_specs = P("tm", "rows", None, None)
    return jax.shard_map(shards, mesh=mesh, in_specs=in_specs, out_specs=out_specs, check_vma=False)
```

profile of v0, /device:TPU:1, one launch (start us, length us, event | category | flops | bytes accessed | tf_op | source)
XLA Modules:
  0.0 217.8 jit_solution(14636832090744077345)
XLA Ops:
  8.4 3.9 %collective-permute-start = (bf16[2,1,40,384]{3,2,1,0:T(8,128)(2,1)S(1)}, bf16[2,1,40,384]{3,2,1,0:T(8,128)(2,1)S(1)}, u32[]{:S(2)}, u32[]{:S(2)}) collective-permute-start(bf16[2,1,40,384]{3,2,1,0:T(8,128)(2,1)S(1)} %fusion.32), channel_id=1, source_target_pairs={{0,16},{16,32},{32,48},{48,64},{64,80},{80,96},{96,112},{112,128},... | collective-permute-start | bytes 184328 | tf_op jit(solution)/shard_map/ppermute | solution.py:10
  16.3 48.9 %all-gather.3.cloned.1.call-done = bf16[4,16,40,384]{3,2,0,1:T(8,128)(2,1)} async-done(((bf16[4,1,40,384]{3,2,0,1:T(8,128)(2,1)}), bf16[4,16,40,384]{3,2,0,1:T(8,128)(2,1)}) %all-gather.3.cloned.1.call-update) | async-done | bytes 1966096 | tf_op jit(solution)/shard_map/all_gather | solution.py:60
  65.2 4.8 %pad_slice_fusion.5 = (bf16[2,18,42,384]{3,2,0,1:T(8,128)(2,1)S(1)}, bf16[2,18,42,384]{3,2,0,1:T(8,128)(2,1)}, bf16[2,18,42,384]{3,2,0,1:T(8,128)(2,1)S(1)}) fusion(bf16[4,16,40,384]{3,2,0,1:T(8,128)(2,1)} %all-gather.3.cloned.1.call-done), kind=kLoop, calls=%fused_computation.5 | loop fusion | bytes 5449728 | tf_op jit(solution)/shard_map/slice | solution.py:31
  71.5 1.9 fusion.38
  73.4 4.3 %reshape.156 = f32[2,18,42,3,3,24]{2,1,0,5,4,3:T(8,128)} reshape(f32[1512,216]{0,1:T(8,128)S(1)} %fusion.38) | data formatting | bytes 2612736 | tf_op jit(solution)/shard_map/reshape | solution.py:40
  77.7 1.5 copy.58
  79.2 1.4 reshape.151
  80.5 1.9 fusion.37
  82.4 4.4 %reshape.153 = f32[2,18,42,3,3,24]{2,1,0,5,4,3:T(8,128)} reshape(f32[1512,216]{0,1:T(8,128)S(1)} %fusion.37) | data formatting | bytes 2612736 | tf_op jit(solution)/shard_map/reshape | solution.py:40
  87.9 4.3 %reshape.150 = f32[2,18,42,3,3,24]{2,1,0,5,4,3:T(8,128)} reshape(f32[1512,216]{0,1:T(8,128)S(1)} %fusion.36) | data formatting | bytes 2612736 | tf_op jit(solution)/shard_map/reshape | solution.py:40
  92.2 7.0 %fusion.14 = bf16[2,16,40,24]{2,1,0,3:T(8,128)(2,1)S(1)} fusion(f32[2,18,42,3,3,24]{2,1,0,5,4,3:T(8,128)} %reshape.156, f32[2,18,42,3,3,24]{2,1,0,5,4,3:T(8,128)} %reshape.153, f32[2,18,42,3,3,24]{2,1,0,5,4,3:T(8,128)} %reshape.150, f32[24]{0:T(128)S(1)} %dynamic_slice.6), kind=kLoop, calls=%fused_computation.47 | loop fusion | flops 860160 | bytes 3379296 | tf_op jit(solution)/shard_map/convert_element_type | solution.py:61
  99.6 12.0 %all_to_all.27 = bf16[16,2,960]{2,1,0:T(2,128)(2,1)S(1)} all-to-all(bf16[16,2,960]{2,1,0:T(2,128)(2,1)S(1)} %reshape.192), channel_id=1, replica_groups=mesh['tm'=32,'rows'=16] {'rows'}, dimensions={0} | all-to-all | bytes 122880 | tf_op jit(solution)/shard_map/all_to_all | solution.py:62
  112.7 3.3 %collective-permute-start.1 = (bf16[2,1,40,384]{3,2,1,0:T(8,128)(2,1)S(1)}, bf16[2,1,40,384]{3,2,1,0:T(8,128)(2,1)S(1)}, u32[]{:S(2)}, u32[]{:S(2)}) collective-permute-start(bf16[2,1,40,384]{3,2,1,0:T(8,128)(2,1)S(1)} %multiply_convert_fusion), channel_id=1, source_target_pairs={{0,16},{16,32},{32,48},{48,64},{64,80},{80,96},{96,112},{112,128},... | collective-permute-start | bytes 184328 | tf_op jit(solution)/shard_map/ppermute | solution.py:10
  118.6 41.3 %all-gather.5.cloned.1.call-done = bf16[4,16,40,384]{3,2,0,1:T(8,128)(2,1)} async-done(((bf16[4,1,40,384]{3,2,0,1:T(8,128)(2,1)}), bf16[4,16,40,384]{3,2,0,1:T(8,128)(2,1)}) %all-gather.5.cloned.1.call-update) | async-done | bytes 1966096 | tf_op jit(solution)/shard_map/all_gather | solution.py:66
  159.9 4.8 %pad_slice_fusion.2 = (bf16[2,18,42,384]{3,2,0,1:T(8,128)(2,1)S(1)}, bf16[2,18,42,384]{3,2,0,1:T(8,128)(2,1)}, bf16[2,18,42,384]{3,2,0,1:T(8,128)(2,1)S(1)}) fusion(bf16[4,16,40,384]{3,2,0,1:T(8,128)(2,1)} %all-gather.5.cloned.1.call-done), kind=kLoop, calls=%fused_computation.2 | loop fusion | bytes 5449728 | tf_op jit(solution)/shard_map/slice | solution.py:31
  166.1 1.9 fusion.41
  168.0 4.3 %reshape.165 = f32[2,18,42,3,3,24]{2,1,0,5,4,3:T(8,128)} reshape(f32[1512,216]{0,1:T(8,128)S(1)} %fusion.41) | data formatting | bytes 2612736 | tf_op jit(solution)/shard_map/reshape | solution.py:40
  172.4 1.5 copy.65
  173.8 1.4 reshape.160
  175.2 1.9 fusion.40
  177.1 4.4 %reshape.162 = f32[2,18,42,3,3,24]{2,1,0,5,4,3:T(8,128)} reshape(f32[1512,216]{0,1:T(8,128)S(1)} %fusion.40) | data formatting | bytes 2612736 | tf_op jit(solution)/shard_map/reshape | solution.py:40
  182.5 4.3 %reshape.159 = f32[2,18,42,3,3,24]{2,1,0,5,4,3:T(8,128)} reshape(f32[1512,216]{0,1:T(8,128)S(1)} %fusion.39) | data formatting | bytes 2612736 | tf_op jit(solution)/shard_map/reshape | solution.py:40
  186.8 7.0 %fusion.1 = f32[2,16,40,24]{2,1,0,3:T(8,128)S(1)} fusion(f32[2,18,42,3,3,24]{2,1,0,5,4,3:T(8,128)} %reshape.165, f32[2,18,42,3,3,24]{2,1,0,5,4,3:T(8,128)} %reshape.162, f32[2,18,42,3,3,24]{2,1,0,5,4,3:T(8,128)} %reshape.159, f32[24]{0:T(128)S(1)} %dynamic_slice.7), kind=kLoop, calls=%fused_computation.8 | loop fusion | flops 829440 | bytes 3440736 | tf_op jit(solution)/shard_map/add | solution.py:49
  194.8 13.2 %all_to_all.28 = f32[16,1,1920]{2,1,0:T(1,128)S(1)} all-to-all(f32[16,1,1920]{2,1,0:T(1,128)S(1)} %reshape.194), channel_id=1, replica_groups=mesh['tm'=32,'rows'=16] {'rows'}, dimensions={0} | all-to-all | bytes 245760 | tf_op jit(solution)/shard_map/all_to_all | solution.py:68
  (46 shorter events, 18.7 us)
Async XLA Ops:
  6.5 58.7 %all-gather.3.cloned.1.call-start = ((), (), s32[]{:S(2)}) async-start(), calls=%async_computation.2 | async-start | bytes 2088960 | tf_op jit(solution)/shard_map/all_gather | solution.py:60
  8.4 5.2 %collective-permute-start = (bf16[2,1,40,384]{3,2,1,0:T(8,128)(2,1)S(1)}, bf16[2,1,40,384]{3,2,1,0:T(8,128)(2,1)S(1)}, u32[]{:S(2)}, u32[]{:S(2)}) collective-permute-start(bf16[2,1,40,384]{3,2,1,0:T(8,128)(2,1)S(1)} %fusion.32), channel_id=1, source_target_pairs={{0,16},{16,32},{32,48},{48,64},{64,80},{80,96},{96,112},{112,128},... | collective-permute-start | bytes 184328 | tf_op jit(solution)/shard_map/ppermute | solution.py:10
  14.3 145.5 %all-gather.5.cloned.1.call-start = ((), (), s32[]{:S(2)}) async-start(), calls=%async_computation.3 | async-start | bytes 2088960 | tf_op jit(solution)/shard_map/all_gather | solution.py:66
  99.2 13.4 %copy-start.2 = (f32[384]{0:T(512)S(1)}, f32[384]{0:T(512)}, u32[]{:S(2)}) copy-start(f32[384]{0:T(512)} %param.11) | copy-start | bytes 4612
  99.3 19.2 %copy-start.1 = (bf16[24,3,3,3,384]{4,0,3,2,1:T(8,128)(2,1)S(1)}, bf16[24,3,3,3,384]{4,0,3,2,1:T(8,128)(2,1)}, u32[]{:S(2)}) copy-start(bf16[24,3,3,3,384]{4,0,3,2,1:T(8,128)(2,1)} %param.12) | copy-start | bytes 1492996
  112.7 4.4 %collective-permute-start.1 = (bf16[2,1,40,384]{3,2,1,0:T(8,128)(2,1)S(1)}, bf16[2,1,40,384]{3,2,1,0:T(8,128)(2,1)S(1)}, u32[]{:S(2)}, u32[]{:S(2)}) collective-permute-start(bf16[2,1,40,384]{3,2,1,0:T(8,128)(2,1)S(1)} %multiply_convert_fusion), channel_id=1, source_target_pairs={{0,16},{16,32},{32,48},{48,64},{64,80},{80,96},{96,112},{112,128},... | collective-permute-start | bytes 184328 | tf_op jit(solution)/shard_map/ppermute | solution.py:10
  193.8 16.5 %copy-start = (bf16[2,1,40,384]{3,2,1,0:T(8,128)(2,1)S(1)}, bf16[2,1,40,384]{3,2,1,0:T(8,128)(2,1)}, u32[]{:S(2)}) copy-start(bf16[2,1,40,384]{3,2,1,0:T(8,128)(2,1)} %param.7) | copy-start | bytes 184324
Sparse Core Ops, SparseCore 0:
  14.5 50.7 all-gather.2
  117.9 41.9 all-gather.4
where the time goes:
time: 218 us
  waiting for transfers between devices  92.6 us (42%)
  local copies, waits for them, and re-layouts  50.8 us (23%)
  blocking collectives  25.2 us (12%)
  other arithmetic  19.4 us (9%)
  between operations  13.6 us (6%)
  matrix products  8.8 us (4%)
  starting transfers between devices  7.28 us (3%)
    all_gather x1, waiting for transfers between devices, shards(): full_one = lax.all_gather(extended_one, 'rows', axis=1, tiled=True)  48.9 us
    all_gather x1, waiting for transfers between devices, shards(): full_two = lax.all_gather(extended_two, 'rows', axis=1, tiled=True)  41.3 us
    reshape x6, local copies, waits for them, and re-layouts, causal_conv(): product[:, :folded]  25.9 us
    all_to_all x1, blocking collectives, shards(): lax.all_to_all(conv_two, 'rows', split_axis=1, concat_axis=3, tiled=True)  13.2 us
    slice x8, local copies, waits for them, and re-layouts, causal_conv(): slab = padded[tap_time:tap_time + frames]  13.1 us
    all_to_all x1, blocking collectives, shards(): lax.all_to_all(conv_one, 'rows', split_axis=1, concat_axis=3, tiled=True)  12 us
    dot_general x6, matrix products, causal_conv(): lax.dot_general(slab.reshape(-1, channels), taps, (((1,), (1,)), ((), ())...  8.8 us
    ppermute x2, starting transfers between devices, passed_along(): return lax.ppermute(x, axis, pairs)  7.24 us
  transfers between devices with their start and end apart: 4, of which 4 were waited for; matrix products, arithmetic and copies ran while one was open for 1% of the time, Pallas kernels for 0%

commit v1 on v0

v1 whole, which is shorter than its diff:
```python
import jax
import jax.numpy as jnp
from jax import lax
from jax.sharding import Mesh, PartitionSpec as P

CORES = 2


def passed_along(x, axis, by):
    peers = lax.axis_size(axis)
    pairs = [(i, i + by) for i in range(peers) if 0 <= i + by < peers]
    return lax.ppermute(x, axis, pairs)


def norm_silu(values, norm_gain):
    values = values.astype(jnp.float32)
    mean_square = jnp.mean(values * values, axis=-1, keepdims=True)
    scaled = values * lax.rsqrt(mean_square + 1e-06) * norm_gain
    return jax.nn.silu(scaled).astype(jnp.bfloat16)


def gather_rows(x):
    frames, _, columns, channels = x.shape
    along_z = lax.all_gather(x, "z", axis=1, tiled=True)
    both = lax.all_gather(along_z, "core", axis=2, tiled=False)
    return both.reshape(frames, -1, columns, channels)


def scatter_rows(y):
    frames, rows, columns, part_width = y.shape
    y = y.reshape(frames, rows // CORES, CORES, columns, part_width)
    y = lax.all_to_all(y, "z", split_axis=1, concat_axis=1, tiled=True)
    y = lax.all_to_all(y, "core", split_axis=2, concat_axis=2, tiled=True)
    y = jnp.transpose(y, (0, 3, 1, 2, 4))
    return y.reshape(frames, 1, columns, rows * part_width)


def causal_conv(extended, kernel, bias_part):
    out = lax.conv_general_dilated(
        extended[None],
        kernel,
        window_strides=(1, 1, 1),
        padding=((0, 0), (1, 1), (1, 1)),
        dimension_numbers=("NDHWC", "ODHWI", "NDHWC"),
        preferred_element_type=jnp.float32,
    )
    return out[0] + bias_part


def shards(features, gain_one, weight_one, bias_one, gain_two, weight_two, bias_two):
    part_width = weight_one.shape[0]
    index = lax.axis_index("z") * CORES + lax.axis_index("core")
    offset = index * part_width
    bias_first = lax.dynamic_slice_in_dim(bias_one, offset, part_width, 0)
    bias_second = lax.dynamic_slice_in_dim(bias_two, offset, part_width, 0)
    normed_one = norm_silu(features, gain_one)
    prior_one = passed_along(normed_one, "tm", 1)
    extended_one = jnp.concatenate([prior_one, normed_one], 0)
    full_one = gather_rows(extended_one)
    conv_one = causal_conv(full_one, weight_one, bias_first).astype(jnp.bfloat16)
    own_rows = scatter_rows(conv_one)
    normed_two = norm_silu(own_rows, gain_two)
    prior_two = passed_along(normed_two, "tm", 1)
    extended_two = jnp.concatenate([prior_two, normed_two], 0)
    full_two = gather_rows(extended_two)
    conv_two = causal_conv(full_two, weight_two, bias_second)
    returned = scatter_rows(conv_two)
    return (features.astype(jnp.float32) + returned).astype(jnp.bfloat16)


def solution(mesh):
    tm = mesh.shape["tm"]
    rows = mesh.shape["rows"]
    split = Mesh(mesh.devices.reshape(tm, rows // CORES, CORES), ("tm", "z", "core"))
    row_axes = ("z", "core")
    in_specs = (
        P("tm", row_axes, None, None),
        P(),
        P(row_axes, None, None, None, None),
        P(),
        P(),
        P(row_axes, None, None, None, None),
        P(),
    )
    out_specs = P("tm", row_axes, None, None)
    return jax.shard_map(shards, mesh=split, in_specs=in_specs, out_specs=out_specs, check_vma=False)
```

time: 218 us -> 199 us (0.913)
  blocking collectives: 25.2 us -> 89.9 us
  waiting for transfers between devices: 92.6 us -> 52.5 us
  local copies, waits for them, and re-layouts: 50.8 us -> 12.7 us
  other arithmetic: 19.4 us -> 4.95 us
  matrix products: 8.8 us -> 17.7 us
    all_gather x0 -> x2, blocking collectives: none -> 52.5 us  [gather_rows(): along_z = lax.all_gather(x, 'z', axis=1, tiled=True)]
    all_gather x2, waiting for transfers between devices: 90.2 us -> 49.9 us  [gather_rows(): both = lax.all_gather(along_z, 'core', axis=2, tiled=False)]
    reshape x12 -> x1, local copies, waits for them, and re-layouts: 31.9 us -> 0.14 us  [scatter_rows(): return y.reshape(frames, 1, columns, rows * part_width)]
    conv_general_dilated x0 -> x2, matrix products: none -> 17.7 us  [causal_conv(): lax.conv_general_dilated(extended[None], kernel, window_strides=(1, 1, 1)...]
    slice x10 -> x0, local copies, waits for them, and re-layouts: 14.3 us -> none  [the longest x8 13.1 us: causal_conv(): slab = padded[tap_time:tap_time + frames]]
    all_to_all x2 -> x4, blocking collectives: 25.2 us -> 37.4 us  [the longest x2 27 us: scatter_rows(): y = lax.all_to_all(y, 'z', split_axis=1, concat_axis=1, tiled=True)]
    dot_general x6 -> x0, matrix products: 8.8 us -> none  [causal_conv(): lax.dot_general(slab.reshape(-1, channels), taps, (((1,), (1,)), ((), ())...]
    convert_element_type x1 -> x0, other arithmetic: 6.99 us -> none  [shards(): causal_conv(full_one, weight_one, bias_first).astype(jnp.bfloat16)]
where the time goes in v1:
time: 199 us
  blocking collectives  89.9 us (45%)
  waiting for transfers between devices  52.5 us (26%)
  matrix products  17.7 us (9%)
  between operations  13.7 us (7%)
  local copies, waits for them, and re-layouts  12.7 us (6%)
  starting transfers between devices  7.09 us (4%)
  other arithmetic  4.95 us (2%)
    all_gather x2, blocking collectives, gather_rows(): along_z = lax.all_gather(x, 'z', axis=1, tiled=True)  52.5 us
    all_gather x2, waiting for transfers between devices, gather_rows(): both = lax.all_gather(along_z, 'core', axis=2, tiled=False)  49.9 us
    all_to_all x2, blocking collectives, scatter_rows(): y = lax.all_to_all(y, 'z', split_axis=1, concat_axis=1, tiled=True)  27 us
    conv_general_dilated x2, matrix products, causal_conv(): lax.conv_general_dilated(extended[None], kernel, window_strides=(1, 1, 1)...  17.7 us
    all_to_all x2, blocking collectives, scatter_rows(): y = lax.all_to_all(y, 'core', split_axis=2, concat_axis=2, tiled=True)  10.4 us
    ppermute x2, starting transfers between devices, passed_along(): return lax.ppermute(x, axis, pairs)  7.04 us
    unnamed x22, local copies, waits for them, and re-layouts  6.12 us
  transfers between devices with their start and end apart: 4, of which 4 were waited for; matrix products, arithmetic and copies ran while one was open for 1% of the time, Pallas kernels for 0%

profile of v1, /device:TPU:1, one launch (start us, length us, event | category | flops | bytes accessed | tf_op | source)
XLA Modules:
  0.0 198.5 jit_solution(11436423002637607309)
XLA Ops:
  6.5 1.0 fusion.25
  7.5 0.9 fusion.32
  8.5 3.9 %collective-permute-start = (bf16[2,1,40,384]{3,2,1,0:T(8,128)(2,1)S(1)}, bf16[2,1,40,384]{3,2,1,0:T(8,128)(2,1)S(1)}, u32[]{:S(2)}, u32[]{:S(2)}) collective-permute-start(bf16[2,1,40,384]{3,2,1,0:T(8,128)(2,1)S(1)} %fusion.32), channel_id=1, source_target_pairs={{0,16},{16,32},{32,48},{48,64},{64,80},{80,96},{96,112},{112,128},... | collective-permute-start | bytes 184328 | tf_op jit(solution)/shard_map/ppermute | solution.py:12
  12.4 1.3 collective-permute-done
  13.7 29.2 %all_gather.18 = bf16[4,8,40,384]{3,2,1,0:T(8,128)(2,1)} all-gather(bf16[4,1,40,384]{3,2,1,0:T(8,128)(2,1)S(1)} %pad_maximum_fusion), channel_id=1, replica_groups=mesh['tm'=32,'z'=8,'core'=2] {'z'}, dimensions={1}, use_global_device_ids=true | all-gather | bytes 1105920 | tf_op jit(solution)/shard_map/all_gather | solution.py:24
  43.0 0.8 dynamic_slice.6
  43.8 26.1 %all-gather.5.cloned.1.call-done = bf16[4,8,80,384]{3,2,1,0:T(8,128)(2,1)} async-done(((bf16[4,8,40,384]{3,2,1,0:T(8,128)(2,1)}), bf16[4,8,80,384]{3,2,1,0:T(8,128)(2,1)}) %all-gather.5.cloned.1.call-update) | async-done | bytes 1966096 | tf_op jit(solution)/shard_map/all_gather | solution.py:25
  69.8 1.8 copy.46
  71.9 0.9 copy.32
  73.0 8.9 %fusion.21 = f32[2,16,8,6,24]{4,2,3,1,0:T(8,128)S(1)} fusion(bf16[24,3,3,3,384]{4,0,3,2,1:T(8,128)(2,1)S(1)} %copy-done, bf16[4,16,1,7,2,384]{5,3,4,1,0,2:T(8,128)(2,1)S(1)} %slice.4, bf16[4,16,1,8,6,384]{5,3,4,1,0,2:T(8,128)(2,1)S(1)} %copy.32, pred[8,6]{0,1:T(8,128)(4,1)S(1)} %copy-done.4), kind=kOutput, calls=%fused_computation.18 | convolution fusion | flops 742035456 | bytes 3692592 | tf_op jit(solution)/shard_map/conv_general_dilated | solution.py:39
  83.0 13.1 %all_to_all.20 = bf16[8,2,1920]{2,1,0:T(2,128)(2,1)S(1)} all-to-all(bf16[8,2,1920]{2,1,0:T(2,128)(2,1)S(1)} %reshape.124), channel_id=1, replica_groups=mesh['tm'=32,'z'=8,'core'=2] {'z'}, dimensions={0} | all-to-all | bytes 122880 | tf_op jit(solution)/shard_map/all_to_all | solution.py:32
  96.7 5.1 %all_to_all.21 = bf16[2,2,7680]{2,1,0:T(2,128)(2,1)S(1)} all-to-all(bf16[2,2,7680]{2,1,0:T(2,128)(2,1)S(1)} %reshape.126), channel_id=1, replica_groups=mesh['tm'=32,'z'=8,'core'=2] {'core'}, dimensions={0} | all-to-all | bytes 122880 | tf_op jit(solution)/shard_map/all_to_all | solution.py:33
  102.6 3.1 %collective-permute-start.1 = (bf16[2,1,40,384]{3,2,1,0:T(8,128)(2,1)S(1)}, bf16[2,1,40,384]{3,2,1,0:T(8,128)(2,1)S(1)}, u32[]{:S(2)}, u32[]{:S(2)}) collective-permute-start(bf16[2,1,40,384]{3,2,1,0:T(8,128)(2,1)S(1)} %multiply_convert_fusion), channel_id=1, source_target_pairs={{0,16},{16,32},{32,48},{48,64},{64,80},{80,96},{96,112},{112,128},... | collective-permute-start | bytes 184328 | tf_op jit(solution)/shard_map/ppermute | solution.py:12
  105.7 1.3 collective-permute-done.1
  107.0 23.3 %all_gather.21 = bf16[4,8,40,384]{3,2,1,0:T(8,128)(2,1)} all-gather(bf16[4,1,40,384]{3,2,1,0:T(8,128)(2,1)S(1)} %pad_maximum_fusion.1), channel_id=1, replica_groups=mesh['tm'=32,'z'=8,'core'=2] {'z'}, dimensions={1}, use_global_device_ids=true | all-gather | bytes 1105920 | tf_op jit(solution)/shard_map/all_gather | solution.py:24
  130.3 0.8 dynamic_slice.7
  131.0 23.8 %all-gather.7.cloned.1.call-done = bf16[4,8,80,384]{3,2,1,0:T(8,128)(2,1)} async-done(((bf16[4,8,40,384]{3,2,1,0:T(8,128)(2,1)}), bf16[4,8,80,384]{3,2,1,0:T(8,128)(2,1)}) %all-gather.7.cloned.1.call-update) | async-done | bytes 1966096 | tf_op jit(solution)/shard_map/all_gather | solution.py:25
  154.9 1.8 copy.47
  156.9 0.9 copy.40
  158.0 8.9 %fusion.18 = f32[2,16,8,6,24]{4,2,3,1,0:T(8,128)S(1)} fusion(bf16[24,3,3,3,384]{4,0,3,2,1:T(8,128)(2,1)S(1)} %copy-done.3, bf16[4,16,1,7,2,384]{5,3,4,1,0,2:T(8,128)(2,1)S(1)} %slice.6, bf16[4,16,1,8,6,384]{5,3,4,1,0,2:T(8,128)(2,1)S(1)} %copy.40, pred[8,6]{0,1:T(8,128)(4,1)S(1)} %copy-done.4), kind=kOutput, calls=%fused_computation.17 | convolution fusion | flops 742035456 | bytes 3692592 | tf_op jit(solution)/shard_map/conv_general_dilated | solution.py:39
  168.1 13.9 %all_to_all.22 = f32[8,1,3840]{2,1,0:T(1,128)S(1)} all-to-all(f32[8,1,3840]{2,1,0:T(1,128)S(1)} %reshape.128), channel_id=1, replica_groups=mesh['tm'=32,'z'=8,'core'=2] {'z'}, dimensions={0} | all-to-all | bytes 245760 | tf_op jit(solution)/shard_map/all_to_all | solution.py:32
  182.6 0.9 reduce.3
  184.2 5.3 %all_to_all.23 = f32[2,1,15360]{2,1,0:T(1,128)S(1)} all-to-all(f32[2,1,15360]{2,1,0:T(1,128)S(1)} %reshape.130), channel_id=1, replica_groups=mesh['tm'=32,'z'=8,'core'=2] {'core'}, dimensions={0} | all-to-all | bytes 245760 | tf_op jit(solution)/shard_map/all_to_all | solution.py:33
  189.5 1.0 reduce.4
  (50 shorter events, 6.9 us)
Async XLA Ops:
  6.5 66.4 %copy-start = (bf16[24,3,3,3,384]{4,0,3,2,1:T(8,128)(2,1)S(1)}, bf16[24,3,3,3,384]{4,0,3,2,1:T(8,128)(2,1)}, u32[]{:S(2)}) copy-start(bf16[24,3,3,3,384]{4,0,3,2,1:T(8,128)(2,1)} %param.9) | copy-start | bytes 1492996
  6.5 63.3 %all-gather.5.cloned.1.call-start = ((), (), s32[]{:S(2)}) async-start(), calls=%async_computation.4 | async-start | bytes 2949120 | tf_op jit(solution)/shard_map/all_gather | solution.py:25
  8.5 5.2 %collective-permute-start = (bf16[2,1,40,384]{3,2,1,0:T(8,128)(2,1)S(1)}, bf16[2,1,40,384]{3,2,1,0:T(8,128)(2,1)S(1)}, u32[]{:S(2)}, u32[]{:S(2)}) collective-permute-start(bf16[2,1,40,384]{3,2,1,0:T(8,128)(2,1)S(1)} %fusion.32), channel_id=1, source_target_pairs={{0,16},{16,32},{32,48},{48,64},{64,80},{80,96},{96,112},{112,128},... | collective-permute-start | bytes 184328 | tf_op jit(solution)/shard_map/ppermute | solution.py:12
  43.0 111.9 %all-gather.7.cloned.1.call-start = ((), (), s32[]{:S(2)}) async-start(), calls=%async_computation.5 | async-start | bytes 2949120 | tf_op jit(solution)/shard_map/all_gather | solution.py:25
  71.9 1.1 copy-start.4
  82.7 19.8 %copy-start.2 = (f32[384]{0:T(512)S(1)}, f32[384]{0:T(512)}, u32[]{:S(2)}) copy-start(f32[384]{0:T(512)} %param.11) | copy-start | bytes 4612
  102.6 4.4 %collective-permute-start.1 = (bf16[2,1,40,384]{3,2,1,0:T(8,128)(2,1)S(1)}, bf16[2,1,40,384]{3,2,1,0:T(8,128)(2,1)S(1)}, u32[]{:S(2)}, u32[]{:S(2)}) collective-permute-start(bf16[2,1,40,384]{3,2,1,0:T(8,128)(2,1)S(1)} %multiply_convert_fusion), channel_id=1, source_target_pairs={{0,16},{16,32},{32,48},{48,64},{64,80},{80,96},{96,112},{112,128},... | collective-permute-start | bytes 184328 | tf_op jit(solution)/shard_map/ppermute | solution.py:12
  156.9 1.1 copy-start.3
  183.5 7.5 %copy-start.1 = (bf16[2,1,40,384]{3,2,1,0:T(8,128)(2,1)S(1)}, bf16[2,1,40,384]{3,2,1,0:T(8,128)(2,1)}, u32[]{:S(2)}) copy-start(bf16[2,1,40,384]{3,2,1,0:T(8,128)(2,1)} %param.7) | copy-start | bytes 184324
Sparse Core Ops, SparseCore 0:
  43.1 26.7 all-gather.4
  130.4 24.4 all-gather.6

commit v2 on v1

--- a/solution.py
+++ b/solution.py
@@ -4,6 +4,7 @@
 from jax.sharding import Mesh, PartitionSpec as P
 
 CORES = 2
+ROW_AXES = ("z", "core")
 
 
 def passed_along(x, axis, by):
@@ -19,20 +20,48 @@
     return jax.nn.silu(scaled).astype(jnp.bfloat16)
 
 
+def rotated(stacked, start):
+    n = stacked.shape[0]
+    doubled = jnp.concatenate([stacked, stacked], 0)
+    return lax.dynamic_slice_in_dim(doubled, start, n, 0)
+
+
 def gather_rows(x):
-    frames, _, columns, channels = x.shape
-    along_z = lax.all_gather(x, "z", axis=1, tiled=True)
-    both = lax.all_gather(along_z, "core", axis=2, tiled=False)
-    return both.reshape(frames, -1, columns, channels)
+    n = lax.axis_size("z")
+    z = lax.axis_index("z")
+    core = lax.axis_index("core")
+    forward = [(i, (i + 1) % n) for i in range(n)]
+    backward = [(i, (i - 1) % n) for i in range(n)]
+    got = {0: x[:, 0]}
+    ahead = behind = x[:, 0]
+    for step in range(1, n // 2 + 1):
+        behind = lax.ppermute(behind, "z", forward)
+        got[-step] = behind
+        if step < n - step:
+            ahead = lax.ppermute(ahead, "z", backward)
+            got[step] = ahead
+    half = n // 2
+    relative = jnp.stack([got[k - half] for k in range(n)], 0)
+    mine = rotated(relative, (half - z) % n)
+    other = lax.ppermute(mine, "core", [(0, 1), (1, 0)])
+    first = jnp.where(core == 0, mine, other)
+    second = jnp.where(core == 0, other, mine)
+    both = jnp.stack([first, second], 1)
+    return jnp.transpose(both, (2, 0, 1, 3, 4)).reshape(x.shape[0], n * CORES, x.shape[2], x.shape[3])
 
 
 def scatter_rows(y):
     frames, rows, columns, part_width = y.shape
-    y = y.reshape(frames, rows // CORES, CORES, columns, part_width)
-    y = lax.all_to_all(y, "z", split_axis=1, concat_axis=1, tiled=True)
-    y = lax.all_to_all(y, "core", split_axis=2, concat_axis=2, tiled=True)
-    y = jnp.transpose(y, (0, 3, 1, 2, 4))
-    return y.reshape(frames, 1, columns, rows * part_width)
+    me = lax.axis_index("z") * CORES + lax.axis_index("core")
+    pieces = []
+    for shift in range(rows):
+        piece = lax.dynamic_index_in_dim(y, (me + shift) % rows, 1, keepdims=False)
+        if shift:
+            piece = lax.ppermute(piece, ROW_AXES, [(i, (i + shift) % rows) for i in range(rows)])
+        pieces.append(piece)
+    stacked = jnp.stack(pieces[::-1], 0)
+    ordered = rotated(stacked, (rows - 1 - me) % rows)
+    return jnp.transpose(ordered, (1, 2, 0, 3)).reshape(frames, 1, columns, rows * part_width)
 
 
 def causal_conv(extended, kernel, bias_part):
@@ -71,16 +100,15 @@
 def solution(mesh):
     tm = mesh.shape["tm"]
     rows = mesh.shape["rows"]
-    split = Mesh(mesh.devices.reshape(tm, rows // CORES, CORES), ("tm", "z", "core"))
-    row_axes = ("z", "core")
+    split = Mesh(mesh.devices.reshape(tm, rows // CORES, CORES), ("tm",) + ROW_AXES)
     in_specs = (
-        P("tm", row_axes, None, None),
+        P("tm", ROW_AXES, None, None),
         P(),
-        P(row_axes, None, None, None, None),
+        P(ROW_AXES, None, None, None, None),
         P(),
         P(),
-        P(row_axes, None, None, None, None),
+        P(ROW_AXES, None, None, None, None),
         P(),
     )
-    out_specs = P("tm", row_axes, None, None)
+    out_specs = P("tm", ROW_AXES, None, None)
     return jax.shard_map(shards, mesh=split, in_specs=in_specs, out_specs=out_specs, check_vma=False)

time: 199 us -> 247 us (1.24)
  the two profiles are of different devices: /device:TPU:1 before, /device:TPU:33 now
where the time goes in v2:
time: 247 us; the launch traced here: 245 us
  starting transfers between devices  170 us (69%)
  waiting for transfers between devices  39.2 us (16%)
  matrix products  17.7 us (7%)
  local copies, waits for them, and re-layouts  12 us (5%)
  other arithmetic  4.13 us (2%)
    ppermute x30, starting transfers between devices, scatter_rows(): lax.ppermute(piece, ROW_AXES, [(i, (i + shift) % rows) for i in range(row...  103 us
    ppermute x6, starting transfers between devices, gather_rows(): ahead = lax.ppermute(ahead, 'z', backward)  27.4 us
    conv_general_dilated x2, matrix products, causal_conv(): lax.conv_general_dilated(extended[None], kernel, window_strides=(1, 1, 1)...  17.7 us
    ppermute x8, starting transfers between devices, gather_rows(): behind = lax.ppermute(behind, 'z', forward)  17.4 us
    ppermute x2, starting transfers between devices, gather_rows(): other = lax.ppermute(mine, 'core', [(0, 1), (1, 0)])  17.2 us
    ppermute x8, waiting for transfers between devices, gather_rows(): behind = lax.ppermute(behind, 'z', forward)  15.7 us
    ppermute x2, waiting for transfers between devices, passed_along(): return lax.ppermute(x, axis, pairs)  11.5 us
    ppermute x30, waiting for transfers between devices, scatter_rows(): lax.ppermute(piece, ROW_AXES, [(i, (i + shift) % rows) for i in range(row...  6.33 us
  transfers between devices with their start and end apart: 48, of which 16 were waited for; matrix products, arithmetic and copies ran while one was open for 2% of the time, Pallas kernels for 0%

profile of v2, /device:TPU:33, one launch (start us, length us, event | category | flops | bytes accessed | tf_op | source)
XLA Modules:
  0.0 245.2 jit_solution(8929119786304640530)
XLA Ops:
  5.1 5.2 %collective-permute-done = bf16[2,1,40,384]{3,2,0,1:T(8,128)(2,1)S(1)} collective-permute-done((bf16[2,1,40,384]{3,2,0,1:T(8,128)(2,1)S(1)}, bf16[2,1,40,384]{3,2,0,1:T(8,128)(2,1)S(1)}, u32[]{:S(2)}, u32[]{:S(2)}) %collective-permute-start) | collective-permute-done | bytes 61472 | tf_op jit(solution)/shard_map/ppermute | solution.py:13
  14.3 8.9 %collective-permute-done.1 = bf16[4,40,384]{2,1,0:T(8,128)(2,1)S(1)} collective-permute-done((bf16[4,40,384]{2,1,0:T(8,128)(2,1)S(1)}, bf16[4,40,384]{2,1,0:T(8,128)(2,1)S(1)}, u32[]{:S(2)}, u32[]{:S(2)}) %collective-permute-start.1) | collective-permute-done | bytes 122912 | tf_op jit(solution)/shard_map/ppermute | solution.py:38
  25.1 4.6 %collective-permute-start.5 = (bf16[4,40,384]{2,1,0:T(8,128)(2,1)S(1)}, bf16[4,40,384]{2,1,0:T(8,128)(2,1)S(1)}, u32[]{:S(2)}, u32[]{:S(2)}) collective-permute-start(bf16[4,40,384]{2,1,0:T(8,128)(2,1)S(1)} %fusion.39), channel_id=1, source_target_pairs={{0,14},{2,0},{4,2},{6,4},{8,6},{10,8},{12,10},{14,12},{1,15},{3,1}... | collective-permute-start | bytes 368648 | tf_op jit(solution)/shard_map/ppermute | solution.py:41
  31.9 4.6 %collective-permute-start.6 = (bf16[4,40,384]{2,1,0:T(8,128)(2,1)S(1)}, bf16[4,40,384]{2,1,0:T(8,128)(2,1)S(1)}, u32[]{:S(2)}, u32[]{:S(2)}) collective-permute-start(bf16[4,40,384]{2,1,0:T(8,128)(2,1)S(1)} %collective-permute-done.5), channel_id=1, source_target_pairs={{0,14},{2,0},{4,2},{6,4},{8,6},{10,8},{12,10},{14,12},{1,15},{3,1}... | collective-permute-start | bytes 368648 | tf_op jit(solution)/shard_map/ppermute | solution.py:41
  46.7 8.0 %collective-permute-start.8 = (bf16[8,4,40,384]{3,2,0,1:T(8,128)(2,1)}, bf16[8,4,40,384]{3,2,0,1:T(8,128)(2,1)S(1)}, u32[]{:S(2)}, u32[]{:S(2)}) collective-permute-start(bf16[8,4,40,384]{3,2,0,1:T(8,128)(2,1)} %copy.104), channel_id=1, source_target_pairs={{0,1},{1,0},{2,3},{3,2},{4,5},{5,4},{6,7},{7,6},{8,9},{9,8},{10,11... | collective-permute-start | bytes 2949128 | tf_op jit(solution)/shard_map/ppermute | solution.py:46
  59.4 8.9 %fusion.21 = f32[2,16,8,6,24]{4,2,3,1,0:T(8,128)S(1)} fusion(bf16[24,3,3,3,384]{4,0,3,2,1:T(8,128)(2,1)S(1)} %copy-done, bf16[4,16,1,7,2,384]{5,3,4,1,0,2:T(8,128)(2,1)S(1)} %slice.4, bf16[4,16,1,8,6,384]{5,3,4,1,0,2:T(8,128)(2,1)S(1)} %copy.46, pred[8,6]{0,1:T(8,128)(4,1)S(1)} %copy-done.4), kind=kOutput, calls=%fused_computation.20 | convolution fusion | flops 742035456 | bytes 3692592 | tf_op jit(solution)/shard_map/conv_general_dilated | solution.py:68
  70.0 5.3 %collective-permute-start.10 = (bf16[2,40,24]{1,2,0:T(8,128)(2,1)S(1)}, bf16[2,40,24]{1,2,0:T(8,128)(2,1)S(1)}, u32[]{:S(2)}, u32[]{:S(2)}) collective-permute-start(bf16[2,40,24]{1,2,0:T(8,128)(2,1)S(1)} %bitcast.283), channel_id=1, source_target_pairs={{0,14},{1,15},{2,0},{3,1},{4,2},{5,3},{6,4},{7,5},{8,6},{9,7},{10,... | collective-permute-start | bytes 11528 | tf_op jit(solution)/shard_map/ppermute | solution.py:60
  77.3 5.6 %collective-permute-start.12 = (bf16[2,40,24]{1,2,0:T(8,128)(2,1)S(1)}, bf16[2,40,24]{1,2,0:T(8,128)(2,1)S(1)}, u32[]{:S(2)}, u32[]{:S(2)}) collective-permute-start(bf16[2,40,24]{1,2,0:T(8,128)(2,1)S(1)} %bitcast.281), channel_id=1, source_target_pairs={{0,12},{1,13},{2,14},{3,15},{4,0},{5,1},{6,2},{7,3},{8,4},{9,5},{1... | collective-permute-start | bytes 11528 | tf_op jit(solution)/shard_map/ppermute | solution.py:60
  86.1 4.7 %collective-permute-start.14 = (bf16[2,40,24]{1,2,0:T(8,128)(2,1)S(1)}, bf16[2,40,24]{1,2,0:T(8,128)(2,1)S(1)}, u32[]{:S(2)}, u32[]{:S(2)}) collective-permute-start(bf16[2,40,24]{1,2,0:T(8,128)(2,1)S(1)} %bitcast.279), channel_id=1, source_target_pairs={{0,10},{1,11},{2,12},{3,13},{4,14},{5,15},{6,0},{7,1},{8,2},{9,3},... | collective-permute-start | bytes 11528 | tf_op jit(solution)/shard_map/ppermute | solution.py:60
  90.8 5.1 %collective-permute-start.15 = (bf16[2,40,24]{1,2,0:T(8,128)(2,1)S(1)}, bf16[2,40,24]{1,2,0:T(8,128)(2,1)S(1)}, u32[]{:S(2)}, u32[]{:S(2)}) collective-permute-start(bf16[2,40,24]{1,2,0:T(8,128)(2,1)S(1)} %bitcast.278), channel_id=1, source_target_pairs={{0,9},{1,10},{2,11},{3,12},{4,13},{5,14},{6,15},{7,0},{8,1},{9,2},... | collective-permute-start | bytes 11528 | tf_op jit(solution)/shard_map/ppermute | solution.py:60
  100.3 5.2 %collective-permute-start.17 = (bf16[2,40,24]{1,2,0:T(8,128)(2,1)S(1)}, bf16[2,40,24]{1,2,0:T(8,128)(2,1)S(1)}, u32[]{:S(2)}, u32[]{:S(2)}) collective-permute-start(bf16[2,40,24]{1,2,0:T(8,128)(2,1)S(1)} %bitcast.275), channel_id=1, source_target_pairs={{0,7},{1,8},{2,9},{3,10},{4,11},{5,12},{6,13},{7,14},{8,15},{9,0},... | collective-permute-start | bytes 11528 | tf_op jit(solution)/shard_map/ppermute | solution.py:60
  107.5 6.0 %collective-permute-start.19 = (bf16[2,40,24]{1,2,0:T(8,128)(2,1)S(1)}, bf16[2,40,24]{1,2,0:T(8,128)(2,1)S(1)}, u32[]{:S(2)}, u32[]{:S(2)}) collective-permute-start(bf16[2,40,24]{1,2,0:T(8,128)(2,1)S(1)} %bitcast.273), channel_id=1, source_target_pairs={{0,5},{1,6},{2,7},{3,8},{4,9},{5,10},{6,11},{7,12},{8,13},{9,14},{... | collective-permute-start | bytes 11528 | tf_op jit(solution)/shard_map/ppermute | solution.py:60
  115.5 5.2 %collective-permute-start.21 = (bf16[2,40,24]{1,2,0:T(8,128)(2,1)S(1)}, bf16[2,40,24]{1,2,0:T(8,128)(2,1)S(1)}, u32[]{:S(2)}, u32[]{:S(2)}) collective-permute-start(bf16[2,40,24]{1,2,0:T(8,128)(2,1)S(1)} %bitcast.271), channel_id=1, source_target_pairs={{0,3},{1,4},{2,5},{3,6},{4,7},{5,8},{6,9},{7,10},{8,11},{9,12},{10... | collective-permute-start | bytes 11528 | tf_op jit(solution)/shard_map/ppermute | solution.py:60
  128.9 6.4 %collective-permute-done.24 = bf16[2,1,40,384]{3,2,0,1:T(8,128)(2,1)S(1)} collective-permute-done((bf16[2,1,40,384]{3,2,0,1:T(8,128)(2,1)S(1)}, bf16[2,1,40,384]{3,2,0,1:T(8,128)(2,1)S(1)}, u32[]{:S(2)}, u32[]{:S(2)}) %collective-permute-start.24) | collective-permute-done | bytes 61472 | tf_op jit(solution)/shard_map/ppermute | solution.py:13
  137.3 4.9 %collective-permute-done.25 = bf16[4,40,384]{2,1,0:T(8,128)(2,1)S(1)} collective-permute-done((bf16[4,40,384]{2,1,0:T(8,128)(2,1)S(1)}, bf16[4,40,384]{2,1,0:T(8,128)(2,1)S(1)}, u32[]{:S(2)}, u32[]{:S(2)}) %collective-permute-start.25) | collective-permute-done | bytes 122912 | tf_op jit(solution)/shard_map/ppermute | solution.py:38
  164.7 9.2 %collective-permute-start.32 = (bf16[8,4,40,384]{3,2,0,1:T(8,128)(2,1)S(1)}, bf16[8,4,40,384]{3,2,0,1:T(8,128)(2,1)S(1)}, u32[]{:S(2)}, u32[]{:S(2)}) collective-permute-start(bf16[8,4,40,384]{3,2,0,1:T(8,128)(2,1)S(1)} %constant_dynamic-slice_fusion.16), channel_id=1, source_target_pairs={{0,1},{1,0},{2,3},{3,2},{4,5},{5,4},{6,7},{7,6},{8,9},{9,8},{10,11... | collective-permute-start | bytes 2949128 | tf_op jit(solution)/shard_map/ppermute | solution.py:46
  178.3 8.9 %fusion.18 = f32[2,16,8,6,24]{4,2,3,1,0:T(8,128)S(1)} fusion(bf16[24,3,3,3,384]{4,0,3,2,1:T(8,128)(2,1)S(1)} %copy-done.3, bf16[4,16,1,7,2,384]{5,3,4,1,0,2:T(8,128)(2,1)S(1)} %slice.6, bf16[4,16,1,8,6,384]{5,3,4,1,0,2:T(8,128)(2,1)S(1)} %copy.83, pred[8,6]{0,1:T(8,128)(4,1)S(1)} %copy-done.4), kind=kOutput, calls=%fused_computation.19 | convolution fusion | flops 742035456 | bytes 3692592 | tf_op jit(solution)/shard_map/conv_general_dilated | solution.py:68
  188.5 5.3 %collective-permute-start.34 = (f32[2,40,24]{1,2,0:T(8,128)S(1)}, f32[2,40,24]{1,2,0:T(8,128)S(1)}, u32[]{:S(2)}, u32[]{:S(2)}) collective-permute-start(f32[2,40,24]{1,2,0:T(8,128)S(1)} %bitcast.267), channel_id=1, source_target_pairs={{0,14},{1,15},{2,0},{3,1},{4,2},{5,3},{6,4},{7,5},{8,6},{9,7},{10,... | collective-permute-start | bytes 23048 | tf_op jit(solution)/shard_map/ppermute | solution.py:60
  195.9 5.1 %collective-permute-start.36 = (f32[2,40,24]{1,2,0:T(8,128)S(1)}, f32[2,40,24]{1,2,0:T(8,128)S(1)}, u32[]{:S(2)}, u32[]{:S(2)}) collective-permute-start(f32[2,40,24]{1,2,0:T(8,128)S(1)} %bitcast.265), channel_id=1, source_target_pairs={{0,12},{1,13},{2,14},{3,15},{4,0},{5,1},{6,2},{7,3},{8,4},{9,5},{1... | collective-permute-start | bytes 23048 | tf_op jit(solution)/shard_map/ppermute | solution.py:60
  203.7 5.2 %collective-permute-start.38 = (f32[2,40,24]{1,2,0:T(8,128)S(1)}, f32[2,40,24]{1,2,0:T(8,128)S(1)}, u32[]{:S(2)}, u32[]{:S(2)}) collective-permute-start(f32[2,40,24]{1,2,0:T(8,128)S(1)} %bitcast.263), channel_id=1, source_target_pairs={{0,10},{1,11},{2,12},{3,13},{4,14},{5,15},{6,0},{7,1},{8,2},{9,3},... | collective-permute-start | bytes 23048 | tf_op jit(solution)/shard_map/ppermute | solution.py:60
  213.5 4.9 %collective-permute-start.40 = (f32[2,40,24]{1,2,0:T(8,128)S(1)}, f32[2,40,24]{1,2,0:T(8,128)S(1)}, u32[]{:S(2)}, u32[]{:S(2)}) collective-permute-start(f32[2,40,24]{1,2,0:T(8,128)S(1)} %bitcast.261), channel_id=1, source_target_pairs={{0,8},{1,9},{2,10},{3,11},{4,12},{5,13},{6,14},{7,15},{8,0},{9,1},... | collective-permute-start | bytes 23048 | tf_op jit(solution)/shard_map/ppermute | solution.py:60
  218.4 4.7 %collective-permute-start.41 = (f32[2,40,24]{1,2,0:T(8,128)S(1)}, f32[2,40,24]{1,2,0:T(8,128)S(1)}, u32[]{:S(2)}, u32[]{:S(2)}) collective-permute-start(f32[2,40,24]{1,2,0:T(8,128)S(1)} %bitcast.260), channel_id=1, source_target_pairs={{0,7},{1,8},{2,9},{3,10},{4,11},{5,12},{6,13},{7,14},{8,15},{9,0},... | collective-permute-start | bytes 23048 | tf_op jit(solution)/shard_map/ppermute | solution.py:60
  225.6 6.0 %collective-permute-start.43 = (f32[2,40,24]{1,2,0:T(8,128)S(1)}, f32[2,40,24]{1,2,0:T(8,128)S(1)}, u32[]{:S(2)}, u32[]{:S(2)}) collective-permute-start(f32[2,40,24]{1,2,0:T(8,128)S(1)} %bitcast.258), channel_id=1, source_target_pairs={{0,5},{1,6},{2,7},{3,8},{4,9},{5,10},{6,11},{7,12},{8,13},{9,14},{... | collective-permute-start | bytes 23048 | tf_op jit(solution)/shard_map/ppermute | solution.py:60
  233.6 4.7 %collective-permute-start.45 = (f32[2,40,24]{1,2,0:T(8,128)S(1)}, f32[2,40,24]{1,2,0:T(8,128)S(1)}, u32[]{:S(2)}, u32[]{:S(2)}) collective-permute-start(f32[2,40,24]{1,2,0:T(8,128)S(1)} %bitcast.256), channel_id=1, source_target_pairs={{0,3},{1,4},{2,5},{3,6},{4,7},{5,8},{6,9},{7,10},{8,11},{9,12},{10... | collective-permute-start | bytes 23048 | tf_op jit(solution)/shard_map/ppermute | solution.py:60
  (251 shorter events, 101.4 us)
Async XLA Ops:
  10.3 12.9 %collective-permute-start.1 = (bf16[4,40,384]{2,1,0:T(8,128)(2,1)S(1)}, bf16[4,40,384]{2,1,0:T(8,128)(2,1)S(1)}, u32[]{:S(2)}, u32[]{:S(2)}) collective-permute-start(bf16[4,40,384]{2,1,0:T(8,128)(2,1)S(1)} %fusion.39), channel_id=1, source_target_pairs={{0,2},{2,4},{4,6},{6,8},{8,10},{10,12},{12,14},{14,0},{1,3},{3,5},... | collective-permute-start | bytes 368648 | tf_op jit(solution)/shard_map/ppermute | solution.py:38
  69.5 16.6 %collective-permute-start.9 = (bf16[2,40,24]{1,2,0:T(8,128)(2,1)S(1)}, bf16[2,40,24]{1,2,0:T(8,128)(2,1)S(1)}, u32[]{:S(2)}, u32[]{:S(2)}) collective-permute-start(bf16[2,40,24]{1,2,0:T(8,128)(2,1)S(1)} %bitcast.277), channel_id=1, source_target_pairs={{0,15},{1,0},{2,1},{3,2},{4,3},{5,4},{6,5},{7,6},{8,7},{9,8},{10,9... | collective-permute-start | bytes 11528 | tf_op jit(solution)/shard_map/ppermute | solution.py:60
  70.0 20.8 %collective-permute-start.10 = (bf16[2,40,24]{1,2,0:T(8,128)(2,1)S(1)}, bf16[2,40,24]{1,2,0:T(8,128)(2,1)S(1)}, u32[]{:S(2)}, u32[]{:S(2)}) collective-permute-start(bf16[2,40,24]{1,2,0:T(8,128)(2,1)S(1)} %bitcast.283), channel_id=1, source_target_pairs={{0,14},{1,15},{2,0},{3,1},{4,2},{5,3},{6,4},{7,5},{8,6},{9,7},{10,... | collective-permute-start | bytes 11528 | tf_op jit(solution)/shard_map/ppermute | solution.py:60
  75.3 20.6 %collective-permute-start.11 = (bf16[2,40,24]{1,2,0:T(8,128)(2,1)S(1)}, bf16[2,40,24]{1,2,0:T(8,128)(2,1)S(1)}, u32[]{:S(2)}, u32[]{:S(2)}) collective-permute-start(bf16[2,40,24]{1,2,0:T(8,128)(2,1)S(1)} %bitcast.282), channel_id=1, source_target_pairs={{0,13},{1,14},{2,15},{3,0},{4,1},{5,2},{6,3},{7,4},{8,5},{9,6},{10... | collective-permute-start | bytes 11528 | tf_op jit(solution)/shard_map/ppermute | solution.py:60
  77.3 22.9 %collective-permute-start.12 = (bf16[2,40,24]{1,2,0:T(8,128)(2,1)S(1)}, bf16[2,40,24]{1,2,0:T(8,128)(2,1)S(1)}, u32[]{:S(2)}, u32[]{:S(2)}) collective-permute-start(bf16[2,40,24]{1,2,0:T(8,128)(2,1)S(1)} %bitcast.281), channel_id=1, source_target_pairs={{0,12},{1,13},{2,14},{3,15},{4,0},{5,1},{6,2},{7,3},{8,4},{9,5},{1... | collective-permute-start | bytes 11528 | tf_op jit(solution)/shard_map/ppermute | solution.py:60
  83.0 22.5 %collective-permute-start.13 = (bf16[2,40,24]{1,2,0:T(8,128)(2,1)S(1)}, bf16[2,40,24]{1,2,0:T(8,128)(2,1)S(1)}, u32[]{:S(2)}, u32[]{:S(2)}) collective-permute-start(bf16[2,40,24]{1,2,0:T(8,128)(2,1)S(1)} %bitcast.280), channel_id=1, source_target_pairs={{0,11},{1,12},{2,13},{3,14},{4,15},{5,0},{6,1},{7,2},{8,3},{9,4},{... | collective-permute-start | bytes 11528 | tf_op jit(solution)/shard_map/ppermute | solution.py:60
  86.1 21.3 %collective-permute-start.14 = (bf16[2,40,24]{1,2,0:T(8,128)(2,1)S(1)}, bf16[2,40,24]{1,2,0:T(8,128)(2,1)S(1)}, u32[]{:S(2)}, u32[]{:S(2)}) collective-permute-start(bf16[2,40,24]{1,2,0:T(8,128)(2,1)S(1)} %bitcast.279), channel_id=1, source_target_pairs={{0,10},{1,11},{2,12},{3,13},{4,14},{5,15},{6,0},{7,1},{8,2},{9,3},... | collective-permute-start | bytes 11528 | tf_op jit(solution)/shard_map/ppermute | solution.py:60
  90.8 22.7 %collective-permute-start.15 = (bf16[2,40,24]{1,2,0:T(8,128)(2,1)S(1)}, bf16[2,40,24]{1,2,0:T(8,128)(2,1)S(1)}, u32[]{:S(2)}, u32[]{:S(2)}) collective-permute-start(bf16[2,40,24]{1,2,0:T(8,128)(2,1)S(1)} %bitcast.278), channel_id=1, source_target_pairs={{0,9},{1,10},{2,11},{3,12},{4,13},{5,14},{6,15},{7,0},{8,1},{9,2},... | collective-permute-start | bytes 11528 | tf_op jit(solution)/shard_map/ppermute | solution.py:60
  95.9 19.6 %collective-permute-start.16 = (bf16[2,40,24]{1,2,0:T(8,128)(2,1)S(1)}, bf16[2,40,24]{1,2,0:T(8,128)(2,1)S(1)}, u32[]{:S(2)}, u32[]{:S(2)}) collective-permute-start(bf16[2,40,24]{1,2,0:T(8,128)(2,1)S(1)} %bitcast.276), channel_id=1, source_target_pairs={{0,8},{1,9},{2,10},{3,11},{4,12},{5,13},{6,14},{7,15},{8,0},{9,1},... | collective-permute-start | bytes 11528 | tf_op jit(solution)/shard_map/ppermute | solution.py:60
  100.3 20.4 %collective-permute-start.17 = (bf16[2,40,24]{1,2,0:T(8,128)(2,1)S(1)}, bf16[2,40,24]{1,2,0:T(8,128)(2,1)S(1)}, u32[]{:S(2)}, u32[]{:S(2)}) collective-permute-start(bf16[2,40,24]{1,2,0:T(8,128)(2,1)S(1)} %bitcast.275), channel_id=1, source_target_pairs={{0,7},{1,8},{2,9},{3,10},{4,11},{5,12},{6,13},{7,14},{8,15},{9,0},... | collective-permute-start | bytes 11528 | tf_op jit(solution)/shard_map/ppermute | solution.py:60
  105.5 17.2 %collective-permute-start.18 = (bf16[2,40,24]{1,2,0:T(8,128)(2,1)S(1)}, bf16[2,40,24]{1,2,0:T(8,128)(2,1)S(1)}, u32[]{:S(2)}, u32[]{:S(2)}) collective-permute-start(bf16[2,40,24]{1,2,0:T(8,128)(2,1)S(1)} %bitcast.274), channel_id=1, source_target_pairs={{0,6},{1,7},{2,8},{3,9},{4,10},{5,11},{6,12},{7,13},{8,14},{9,15},... | collective-permute-start | bytes 11528 | tf_op jit(solution)/shard_map/ppermute | solution.py:60
  107.5 15.8 %collective-permute-start.19 = (bf16[2,40,24]{1,2,0:T(8,128)(2,1)S(1)}, bf16[2,40,24]{1,2,0:T(8,128)(2,1)S(1)}, u32[]{:S(2)}, u32[]{:S(2)}) collective-permute-start(bf16[2,40,24]{1,2,0:T(8,128)(2,1)S(1)} %bitcast.273), channel_id=1, source_target_pairs={{0,5},{1,6},{2,7},{3,8},{4,9},{5,10},{6,11},{7,12},{8,13},{9,14},{... | collective-permute-start | bytes 11528 | tf_op jit(solution)/shard_map/ppermute | solution.py:60
  164.7 11.3 %collective-permute-start.32 = (bf16[8,4,40,384]{3,2,0,1:T(8,128)(2,1)S(1)}, bf16[8,4,40,384]{3,2,0,1:T(8,128)(2,1)S(1)}, u32[]{:S(2)}, u32[]{:S(2)}) collective-permute-start(bf16[8,4,40,384]{3,2,0,1:T(8,128)(2,1)S(1)} %constant_dynamic-slice_fusion.16), channel_id=1, source_target_pairs={{0,1},{1,0},{2,3},{3,2},{4,5},{5,4},{6,7},{7,6},{8,9},{9,8},{10,11... | collective-permute-start | bytes 2949128 | tf_op jit(solution)/shard_map/ppermute | solution.py:46
  188.1 15.6 %collective-permute-start.33 = (f32[2,40,24]{1,2,0:T(8,128)S(1)}, f32[2,40,24]{1,2,0:T(8,128)S(1)}, u32[]{:S(2)}, u32[]{:S(2)}) collective-permute-start(f32[2,40,24]{1,2,0:T(8,128)S(1)} %bitcast.268), channel_id=1, source_target_pairs={{0,15},{1,0},{2,1},{3,2},{4,3},{5,4},{6,5},{7,6},{8,7},{9,8},{10,9... | collective-permute-start | bytes 23048 | tf_op jit(solution)/shard_map/ppermute | solution.py:60
  188.5 20.4 %collective-permute-start.34 = (f32[2,40,24]{1,2,0:T(8,128)S(1)}, f32[2,40,24]{1,2,0:T(8,128)S(1)}, u32[]{:S(2)}, u32[]{:S(2)}) collective-permute-start(f32[2,40,24]{1,2,0:T(8,128)S(1)} %bitcast.267), channel_id=1, source_target_pairs={{0,14},{1,15},{2,0},{3,1},{4,2},{5,3},{6,4},{7,5},{8,6},{9,7},{10,... | collective-permute-start | bytes 23048 | tf_op jit(solution)/shard_map/ppermute | solution.py:60
  193.9 19.6 %collective-permute-start.35 = (f32[2,40,24]{1,2,0:T(8,128)S(1)}, f32[2,40,24]{1,2,0:T(8,128)S(1)}, u32[]{:S(2)}, u32[]{:S(2)}) collective-permute-start(f32[2,40,24]{1,2,0:T(8,128)S(1)} %bitcast.266), channel_id=1, source_target_pairs={{0,13},{1,14},{2,15},{3,0},{4,1},{5,2},{6,3},{7,4},{8,5},{9,6},{10... | collective-permute-start | bytes 23048 | tf_op jit(solution)/shard_map/ppermute | solution.py:60
  195.9 22.5 %collective-permute-start.36 = (f32[2,40,24]{1,2,0:T(8,128)S(1)}, f32[2,40,24]{1,2,0:T(8,128)S(1)}, u32[]{:S(2)}, u32[]{:S(2)}) collective-permute-start(f32[2,40,24]{1,2,0:T(8,128)S(1)} %bitcast.265), channel_id=1, source_target_pairs={{0,12},{1,13},{2,14},{3,15},{4,0},{5,1},{6,2},{7,3},{8,4},{9,5},{1... | collective-permute-start | bytes 23048 | tf_op jit(solution)/shard_map/ppermute | solution.py:60
  201.0 22.1 %collective-permute-start.37 = (f32[2,40,24]{1,2,0:T(8,128)S(1)}, f32[2,40,24]{1,2,0:T(8,128)S(1)}, u32[]{:S(2)}, u32[]{:S(2)}) collective-permute-start(f32[2,40,24]{1,2,0:T(8,128)S(1)} %bitcast.264), channel_id=1, source_target_pairs={{0,11},{1,12},{2,13},{3,14},{4,15},{5,0},{6,1},{7,2},{8,3},{9,4},{... | collective-permute-start | bytes 23048 | tf_op jit(solution)/shard_map/ppermute | solution.py:60
  203.7 21.8 %collective-permute-start.38 = (f32[2,40,24]{1,2,0:T(8,128)S(1)}, f32[2,40,24]{1,2,0:T(8,128)S(1)}, u32[]{:S(2)}, u32[]{:S(2)}) collective-permute-start(f32[2,40,24]{1,2,0:T(8,128)S(1)} %bitcast.263), channel_id=1, source_target_pairs={{0,10},{1,11},{2,12},{3,13},{4,14},{5,15},{6,0},{7,1},{8,2},{9,3},... | collective-permute-start | bytes 23048 | tf_op jit(solution)/shard_map/ppermute | solution.py:60
  208.9 22.7 %collective-permute-start.39 = (f32[2,40,24]{1,2,0:T(8,128)S(1)}, f32[2,40,24]{1,2,0:T(8,128)S(1)}, u32[]{:S(2)}, u32[]{:S(2)}) collective-permute-start(f32[2,40,24]{1,2,0:T(8,128)S(1)} %bitcast.262), channel_id=1, source_target_pairs={{0,9},{1,10},{2,11},{3,12},{4,13},{5,14},{6,15},{7,0},{8,1},{9,2},... | collective-permute-start | bytes 23048 | tf_op jit(solution)/shard_map/ppermute | solution.py:60
  213.5 20.1 %collective-permute-start.40 = (f32[2,40,24]{1,2,0:T(8,128)S(1)}, f32[2,40,24]{1,2,0:T(8,128)S(1)}, u32[]{:S(2)}, u32[]{:S(2)}) collective-permute-start(f32[2,40,24]{1,2,0:T(8,128)S(1)} %bitcast.261), channel_id=1, source_target_pairs={{0,8},{1,9},{2,10},{3,11},{4,12},{5,13},{6,14},{7,15},{8,0},{9,1},... | collective-permute-start | bytes 23048 | tf_op jit(solution)/shard_map/ppermute | solution.py:60
  218.4 19.9 %collective-permute-start.41 = (f32[2,40,24]{1,2,0:T(8,128)S(1)}, f32[2,40,24]{1,2,0:T(8,128)S(1)}, u32[]{:S(2)}, u32[]{:S(2)}) collective-permute-start(f32[2,40,24]{1,2,0:T(8,128)S(1)} %bitcast.260), channel_id=1, source_target_pairs={{0,7},{1,8},{2,9},{3,10},{4,11},{5,12},{6,13},{7,14},{8,15},{9,0},... | collective-permute-start | bytes 23048 | tf_op jit(solution)/shard_map/ppermute | solution.py:60
  223.1 17.1 %collective-permute-start.42 = (f32[2,40,24]{1,2,0:T(8,128)S(1)}, f32[2,40,24]{1,2,0:T(8,128)S(1)}, u32[]{:S(2)}, u32[]{:S(2)}) collective-permute-start(f32[2,40,24]{1,2,0:T(8,128)S(1)} %bitcast.259), channel_id=1, source_target_pairs={{0,6},{1,7},{2,8},{3,9},{4,10},{5,11},{6,12},{7,13},{8,14},{9,15},... | collective-permute-start | bytes 23048 | tf_op jit(solution)/shard_map/ppermute | solution.py:60
  225.6 15.3 %collective-permute-start.43 = (f32[2,40,24]{1,2,0:T(8,128)S(1)}, f32[2,40,24]{1,2,0:T(8,128)S(1)}, u32[]{:S(2)}, u32[]{:S(2)}) collective-permute-start(f32[2,40,24]{1,2,0:T(8,128)S(1)} %bitcast.258), channel_id=1, source_target_pairs={{0,5},{1,6},{2,7},{3,8},{4,9},{5,10},{6,11},{7,12},{8,13},{9,14},{... | collective-permute-start | bytes 23048 | tf_op jit(solution)/shard_map/ppermute | solution.py:60
  (29 other events, 328.3 us)

commit v3 on v0

v3 whole, which is shorter than its diff:
```python
import jax
import jax.numpy as jnp
from jax import lax
from jax.sharding import PartitionSpec as P


def passed_along(x, axis, by):
    peers = lax.axis_size(axis)
    pairs = [(i, i + by) for i in range(peers) if 0 <= i + by < peers]
    return lax.ppermute(x, axis, pairs)


def norm_silu(values, norm_gain):
    values = values.astype(jnp.float32)
    mean_square = jnp.mean(values * values, axis=-1, keepdims=True)
    scaled = values * lax.rsqrt(mean_square + 1e-06) * norm_gain
    return jax.nn.silu(scaled).astype(jnp.bfloat16)


def causal_conv(own, kernel, bias_part):
    part_width = kernel.shape[0]
    stacked = jnp.transpose(kernel, (1, 0, 2, 3, 4)).reshape(3 * part_width, 3, 3, kernel.shape[4])
    product = lax.conv_general_dilated(
        own,
        stacked,
        window_strides=(1, 1),
        padding=((1, 1), (1, 1)),
        dimension_numbers=("NHWC", "OHWI", "NHWC"),
        preferred_element_type=jnp.float32,
    )
    tap = [product[..., a * part_width : (a + 1) * part_width] for a in range(3)]
    onward = jnp.stack([tap[0][0] + tap[1][1], tap[0][1]], 0)
    kept = jnp.stack([tap[2][0], tap[1][0] + tap[2][1]], 0)
    arrived = passed_along(onward, "tm", 1)
    return kept + arrived + bias_part


def shards(features, gain_one, weight_one, bias_one, gain_two, weight_two, bias_two):
    part_width = weight_one.shape[0]
    offset = lax.axis_index("rows") * part_width
    bias_first = lax.dynamic_slice_in_dim(bias_one, offset, part_width, 0)
    bias_second = lax.dynamic_slice_in_dim(bias_two, offset, part_width, 0)
    normed_one = norm_silu(features, gain_one)
    full_one = lax.all_gather(normed_one, "rows", axis=1, tiled=True)
    conv_one = causal_conv(full_one, weight_one, bias_first).astype(jnp.bfloat16)
    own_rows = lax.all_to_all(conv_one, "rows", split_axis=1, concat_axis=3, tiled=True)
    normed_two = norm_silu(own_rows, gain_two)
    full_two = lax.all_gather(normed_two, "rows", axis=1, tiled=True)
    conv_two = causal_conv(full_two, weight_two, bias_second)
    returned = lax.all_to_all(conv_two, "rows", split_axis=1, concat_axis=3, tiled=True)
    return (features.astype(jnp.float32) + returned).astype(jnp.bfloat16)


def solution(mesh):
    in_specs = (
        P("tm", "rows", None, None),
        P(),
        P("rows", None, None, None, None),
        P(),
        P(),
        P("rows", None, None, None, None),
        P(),
    )
    out_specs = P("tm", "rows", None, None)
    return jax.shard_map(shards, mesh=mesh, in_specs=in_specs, out_specs=out_specs, check_vma=False)
```

time: 218 us -> 120 us (0.55)
  the two profiles are of different devices: /device:TPU:1 before, /device:TPU:33 now
where the time goes in v3:
time: 120 us; the launch traced here: 119 us
  blocking collectives  57.9 us (48%)
  waiting for transfers between devices  32.7 us (27%)
  starting transfers between devices  9.42 us (8%)
  local copies, waits for them, and re-layouts  7.49 us (6%)
  matrix products  6.95 us (6%)
  other arithmetic  4.51 us (4%)
    all_gather x1, blocking collectives, shards(): full_one = lax.all_gather(normed_one, 'rows', axis=1, tiled=True)  26.4 us
    ppermute x2, waiting for transfers between devices, passed_along(): return lax.ppermute(x, axis, pairs)  25 us
    all_gather x1, blocking collectives, shards(): full_two = lax.all_gather(normed_two, 'rows', axis=1, tiled=True)  17.5 us
    all_to_all x1, blocking collectives, shards(): lax.all_to_all(conv_two, 'rows', split_axis=1, concat_axis=3, tiled=True)  14 us
    all_to_all x1, waiting for transfers between devices, shards(): lax.all_to_all(conv_one, 'rows', split_axis=1, concat_axis=3, tiled=True)  7.76 us
    conv_general_dilated x2, matrix products, causal_conv(): lax.conv_general_dilated(own, stacked, window_strides=(1, 1), padding=((1...  6.95 us
    ppermute x2, starting transfers between devices, passed_along(): return lax.ppermute(x, axis, pairs)  5.17 us
    all_to_all x1, starting transfers between devices, shards(): lax.all_to_all(conv_one, 'rows', split_axis=1, concat_axis=3, tiled=True)  4.25 us
  transfers between devices with their start and end apart: 3, of which 3 were waited for; matrix products, arithmetic and copies ran while one was open for 1% of the time, Pallas kernels for 0%

profile of v3, /device:TPU:33, one launch (start us, length us, event | category | flops | bytes accessed | tf_op | source)
XLA Modules:
  0.0 119.4 jit_solution(10759477269598027484)
XLA Ops:
  0.0 0.9 fusion.20
  0.9 0.9 fusion.29
  1.9 26.4 %all_gather.6 = bf16[2,16,40,384]{3,2,0,1:T(8,128)(2,1)S(1)} all-gather(bf16[2,1,40,384]{3,2,0,1:T(8,128)(2,1)S(1)} %fusion.29), channel_id=1, replica_groups=mesh['tm'=32,'rows'=16] {'rows'}, dimensions={1}, use_global_device_ids=true | all-gather | bytes 1044480 | tf_op jit(solution)/shard_map/all_gather | solution.py:44
  28.9 0.8 copy-done.1
  29.8 3.5 %fusion.10 = f32[16,16,6,72]{3,1,2,0:T(8,128)S(1)} fusion(bf16[72,3,3,384]{3,0,2,1:T(8,128)(2,1)S(1)} %bitcast.66, bf16[16,2,8,8,384]{4,0,3,2,1:T(8,128)(2,1)S(1)} %fusion.2, pred[16,6]{0,1:T(8,128)(4,1)S(1)} %copy-done.4), kind=kOutput, calls=%fused_computation.11 | convolution fusion | flops 732672000 | bytes 2512992 | tf_op jit(solution)/shard_map/conv_general_dilated | solution.py:23
  33.3 0.5 copy.48
  33.8 0.4 copy.62
  34.3 3.2 %collective-permute-start = (f32[2,16,40,24]{2,3,1,0:T(8,128)S(1)}, f32[2,16,40,24]{2,3,1,0:T(8,128)S(1)}, u32[]{:S(2)}, u32[]{:S(2)}) collective-permute-start(f32[2,16,40,24]{2,3,1,0:T(8,128)S(1)} %pad_maximum_fusion), channel_id=1, source_target_pairs={{0,16},{16,32},{32,48},{48,64},{64,80},{80,96},{96,112},{112,128},... | collective-permute-start | bytes 368648 | tf_op jit(solution)/shard_map/ppermute | solution.py:10
  37.6 0.8 dynamic_slice.6
  38.3 11.9 %collective-permute-done = f32[2,16,40,24]{2,3,1,0:T(8,128)S(1)} collective-permute-done((f32[2,16,40,24]{2,3,1,0:T(8,128)S(1)}, f32[2,16,40,24]{2,3,1,0:T(8,128)S(1)}, u32[]{:S(2)}, u32[]{:S(2)}) %collective-permute-start) | collective-permute-done | bytes 122912 | tf_op jit(solution)/shard_map/ppermute | solution.py:10
  50.3 0.9 reshape.116
  51.2 4.2 %all-to-all-start = ((bf16[16,2,960]{2,1,0:T(2,128)(2,1)}), bf16[16,2,960]{2,1,0:T(2,128)(2,1)S(1)}, u32[]{:S(2)}, u32[]{:S(2)}) async-start(bf16[16,2,960]{2,1,0:T(2,128)(2,1)} %reshape.116), calls=%async_computation | async-start | bytes 131072 | tf_op jit(solution)/shard_map/all_to_all | solution.py:46
  55.5 7.8 %all-to-all-done = bf16[16,2,960]{2,1,0:T(2,128)(2,1)S(1)} async-done(((bf16[16,2,960]{2,1,0:T(2,128)(2,1)}), bf16[16,2,960]{2,1,0:T(2,128)(2,1)S(1)}, u32[]{:S(2)}, u32[]{:S(2)}) %all-to-all-start) | async-done | bytes 61472 | tf_op jit(solution)/shard_map/all_to_all | solution.py:46
  63.9 17.5 %all_gather.7 = bf16[2,16,40,384]{3,2,0,1:T(8,128)(2,1)S(1)} all-gather(bf16[2,1,40,384]{3,2,0,1:T(8,128)(2,1)S(1)} %fusion.30), channel_id=1, replica_groups=mesh['tm'=32,'rows'=16] {'rows'}, dimensions={1}, use_global_device_ids=true | all-gather | bytes 1044480 | tf_op jit(solution)/shard_map/all_gather | solution.py:48
  82.0 3.5 %fusion.13 = f32[16,16,6,72]{3,1,2,0:T(8,128)S(1)} fusion(bf16[72,3,3,384]{3,0,2,1:T(8,128)(2,1)S(1)} %bitcast.65, bf16[16,2,8,8,384]{4,0,3,2,1:T(8,128)(2,1)S(1)} %fusion.3, pred[16,6]{0,1:T(8,128)(4,1)S(1)} %copy-done.4), kind=kOutput, calls=%fused_computation.12 | convolution fusion | flops 732672000 | bytes 2512992 | tf_op jit(solution)/shard_map/conv_general_dilated | solution.py:23
  85.5 0.5 copy.57
  86.0 0.4 copy.63
  86.5 1.9 %collective-permute-start.1 = (f32[2,16,40,24]{2,3,1,0:T(8,128)S(1)}, f32[2,16,40,24]{2,3,1,0:T(8,128)S(1)}, u32[]{:S(2)}, u32[]{:S(2)}) collective-permute-start(f32[2,16,40,24]{2,3,1,0:T(8,128)S(1)} %pad_maximum_fusion.1), channel_id=1, source_target_pairs={{0,16},{16,32},{32,48},{48,64},{64,80},{80,96},{96,112},{112,128},... | collective-permute-start | bytes 368648 | tf_op jit(solution)/shard_map/ppermute | solution.py:10
  88.4 0.8 dynamic_slice.7
  89.2 13.1 %collective-permute-done.1 = f32[2,16,40,24]{2,3,1,0:T(8,128)S(1)} collective-permute-done((f32[2,16,40,24]{2,3,1,0:T(8,128)S(1)}, f32[2,16,40,24]{2,3,1,0:T(8,128)S(1)}, u32[]{:S(2)}, u32[]{:S(2)}) %collective-permute-start.1) | collective-permute-done | bytes 122912 | tf_op jit(solution)/shard_map/ppermute | solution.py:10
  102.8 14.0 %all_to_all.27 = f32[16,1,1920]{2,1,0:T(1,128)S(1)} all-to-all(f32[16,1,1920]{2,1,0:T(1,128)S(1)} %reshape.118), channel_id=1, replica_groups=mesh['tm'=32,'rows'=16] {'rows'}, dimensions={0} | all-to-all | bytes 245760 | tf_op jit(solution)/shard_map/all_to_all | solution.py:50
  116.8 0.5 broadcast.93
  117.3 0.9 reduce.5
  118.7 0.6 fusion.28
  (40 shorter events, 3.2 us)
Async XLA Ops:
  28.7 1.0 copy-start.1
  28.7 1.1 copy-start.4
  34.3 21.2 %copy-start.2 = (bf16[24,3,3,3,384]{4,0,3,2,1:T(8,128)(2,1)S(1)}, bf16[24,3,3,3,384]{4,0,3,2,1:T(8,128)(2,1)}, u32[]{:S(2)}) copy-start(bf16[24,3,3,3,384]{4,0,3,2,1:T(8,128)(2,1)} %param.12) | copy-start | bytes 1492996
  34.3 15.9 %collective-permute-start = (f32[2,16,40,24]{2,3,1,0:T(8,128)S(1)}, f32[2,16,40,24]{2,3,1,0:T(8,128)S(1)}, u32[]{:S(2)}, u32[]{:S(2)}) collective-permute-start(f32[2,16,40,24]{2,3,1,0:T(8,128)S(1)} %pad_maximum_fusion), channel_id=1, source_target_pairs={{0,16},{16,32},{32,48},{48,64},{64,80},{80,96},{96,112},{112,128},... | collective-permute-start | bytes 368648 | tf_op jit(solution)/shard_map/ppermute | solution.py:10
  51.2 12.1 %all-to-all-start = ((bf16[16,2,960]{2,1,0:T(2,128)(2,1)}), bf16[16,2,960]{2,1,0:T(2,128)(2,1)S(1)}, u32[]{:S(2)}, u32[]{:S(2)}) async-start(bf16[16,2,960]{2,1,0:T(2,128)(2,1)} %reshape.116), calls=%async_computation | async-start | bytes 131072 | tf_op jit(solution)/shard_map/all_to_all | solution.py:46
  55.4 8.4 %copy-start.3 = (f32[384]{0:T(512)S(1)}, f32[384]{0:T(512)}, u32[]{:S(2)}) copy-start(f32[384]{0:T(512)} %param.11) | copy-start | bytes 4612
  86.5 15.8 %collective-permute-start.1 = (f32[2,16,40,24]{2,3,1,0:T(8,128)S(1)}, f32[2,16,40,24]{2,3,1,0:T(8,128)S(1)}, u32[]{:S(2)}, u32[]{:S(2)}) collective-permute-start(f32[2,16,40,24]{2,3,1,0:T(8,128)S(1)} %pad_maximum_fusion.1), channel_id=1, source_target_pairs={{0,16},{16,32},{32,48},{48,64},{64,80},{80,96},{96,112},{112,128},... | collective-permute-start | bytes 368648 | tf_op jit(solution)/shard_map/ppermute | solution.py:10
  102.7 16.0 %copy-start = (bf16[2,1,40,384]{3,2,1,0:T(8,128)(2,1)S(1)}, bf16[2,1,40,384]{3,2,1,0:T(8,128)(2,1)}, u32[]{:S(2)}) copy-start(bf16[2,1,40,384]{3,2,1,0:T(8,128)(2,1)} %param.7) | copy-start | bytes 184324

commit v4 on v3

--- a/solution.py
+++ b/solution.py
@@ -43,9 +43,8 @@
     normed_one = norm_silu(features, gain_one)
     full_one = lax.all_gather(normed_one, "rows", axis=1, tiled=True)
     conv_one = causal_conv(full_one, weight_one, bias_first).astype(jnp.bfloat16)
-    own_rows = lax.all_to_all(conv_one, "rows", split_axis=1, concat_axis=3, tiled=True)
-    normed_two = norm_silu(own_rows, gain_two)
-    full_two = lax.all_gather(normed_two, "rows", axis=1, tiled=True)
+    every_channel = lax.all_gather(conv_one, "rows", axis=3, tiled=True)
+    full_two = norm_silu(every_channel, gain_two)
     conv_two = causal_conv(full_two, weight_two, bias_second)
     returned = lax.all_to_all(conv_two, "rows", split_axis=1, concat_axis=3, tiled=True)
     return (features.astype(jnp.float32) + returned).astype(jnp.bfloat16)

time: 120 us -> 124 us (1.033)
  blocking collectives: 57.9 us -> 67.9 us
  waiting for transfers between devices: 32.7 us -> 24.1 us
  local copies, waits for them, and re-layouts: 7.49 us -> 12.2 us
  starting transfers between devices: 9.42 us -> 5.18 us
  other arithmetic: 4.51 us -> 6.49 us
    all_gather x1, blocking collectives: 17.5 us -> 27.8 us  [shards(): every_channel = lax.all_gather(conv_one, 'rows', axis=3, tiled=True)]
    all_to_all x1 -> x0, waiting for transfers between devices: 7.76 us -> none  [shards(): lax.all_to_all(conv_one, 'rows', split_axis=1, concat_axis=3, tiled=True)]
    all_to_all x1 -> x0, starting transfers between devices: 4.25 us -> none  [shards(): lax.all_to_all(conv_one, 'rows', split_axis=1, concat_axis=3, tiled=True)]
    all_gather x2 -> x1, local copies, waits for them, and re-layouts: 0.31 us -> 4.52 us  [shards(): every_channel = lax.all_gather(conv_one, 'rows', axis=3, tiled=True)]
    reduce_sum x2, other arithmetic: 1 us -> 2.47 us  [norm_silu(): mean_square = jnp.mean(values * values, axis=-1, keepdims=True)]
    unnamed x18 -> x20, local copies, waits for them, and re-layouts: 3.39 us -> 3.91 us
  transfers between devices with their start and end apart: 3 -> 2, of which waited for: 3 -> 2; matrix products, arithmetic and copies ran while one was open for 1% -> 2% of each run, Pallas kernels for 0% -> 0%
where the time goes in v4:
time: 124 us; the launch traced here: 123 us
  blocking collectives  67.9 us (55%)
  waiting for transfers between devices  24.1 us (19%)
  local copies, waits for them, and re-layouts  12.2 us (10%)
  matrix products  6.93 us (6%)
  other arithmetic  6.49 us (5%)
  starting transfers between devices  5.18 us (4%)
    all_gather x1, blocking collectives, shards(): every_channel = lax.all_gather(conv_one, 'rows', axis=3, tiled=True)  27.8 us
    all_gather x1, blocking collectives, shards(): full_one = lax.all_gather(normed_one, 'rows', axis=1, tiled=True)  26.4 us
    ppermute x2, waiting for transfers between devices, passed_along(): return lax.ppermute(x, axis, pairs)  24.1 us
    all_to_all x1, blocking collectives, shards(): lax.all_to_all(conv_two, 'rows', split_axis=1, concat_axis=3, tiled=True)  13.7 us
    conv_general_dilated x2, matrix products, causal_conv(): lax.conv_general_dilated(own, stacked, window_strides=(1, 1), padding=((1...  6.93 us
    ppermute x2, starting transfers between devices, passed_along(): return lax.ppermute(x, axis, pairs)  5.18 us
    all_gather x1, local copies, waits for them, and re-layouts, shards(): every_channel = lax.all_gather(conv_one, 'rows', axis=3, tiled=True)  4.52 us
    unnamed x20, local copies, waits for them, and re-layouts  3.91 us
  transfers between devices with their start and end apart: 2, of which 2 were waited for; matrix products, arithmetic and copies ran while one was open for 2% of the time, Pallas kernels for 0%

profile of v4, /device:TPU:33, one launch (start us, length us, event | category | flops | bytes accessed | tf_op | source)
XLA Modules:
  0.0 123.1 jit_solution(11685712361366267448)
XLA Ops:
  0.0 0.9 fusion.28
  0.9 0.9 fusion.37
  1.9 26.4 %all_gather.6 = bf16[2,16,40,384]{3,2,0,1:T(8,128)(2,1)S(1)} all-gather(bf16[2,1,40,384]{3,2,0,1:T(8,128)(2,1)S(1)} %fusion.37), channel_id=1, replica_groups=mesh['tm'=32,'rows'=16] {'rows'}, dimensions={1}, use_global_device_ids=true | all-gather | bytes 1044480 | tf_op jit(solution)/shard_map/all_gather | solution.py:44
  28.9 0.8 copy-done.2
  29.8 3.5 %fusion.18 = f32[16,16,6,72]{3,1,2,0:T(8,128)S(1)} fusion(bf16[72,3,3,384]{3,0,2,1:T(8,128)(2,1)S(1)} %bitcast.51, bf16[16,2,8,8,384]{4,0,3,2,1:T(8,128)(2,1)S(1)} %fusion.10, pred[16,6]{0,1:T(8,128)(4,1)S(1)} %copy-done.6), kind=kOutput, calls=%fused_computation.21 | convolution fusion | flops 732672000 | bytes 2512992 | tf_op jit(solution)/shard_map/conv_general_dilated | solution.py:23
  33.3 0.5 copy.42
  34.3 3.3 %collective-permute-start = (f32[2,16,40,24]{2,3,1,0:T(8,128)S(1)}, f32[2,16,40,24]{2,3,1,0:T(8,128)S(1)}, u32[]{:S(2)}, u32[]{:S(2)}) collective-permute-start(f32[2,16,40,24]{2,3,1,0:T(8,128)S(1)} %pad_maximum_fusion), channel_id=1, source_target_pairs={{0,16},{16,32},{32,48},{48,64},{64,80},{80,96},{96,112},{112,128},... | collective-permute-start | bytes 368648 | tf_op jit(solution)/shard_map/ppermute | solution.py:10
  37.6 0.9 copy.47
  38.5 0.8 dynamic_slice.6
  39.2 11.0 %collective-permute-done = f32[2,16,40,24]{2,3,1,0:T(8,128)S(1)} collective-permute-done((f32[2,16,40,24]{2,3,1,0:T(8,128)S(1)}, f32[2,16,40,24]{2,3,1,0:T(8,128)S(1)}, u32[]{:S(2)}, u32[]{:S(2)}) %collective-permute-start) | collective-permute-done | bytes 122912 | tf_op jit(solution)/shard_map/ppermute | solution.py:10
  50.4 27.8 %all_gather.7 = bf16[2,16,40,384]{2,1,0,3:T(8,128)(2,1)S(1)} all-gather(bf16[2,16,40,24]{2,1,0,3:T(8,128)(2,1)S(1)} %copy.44), channel_id=1, replica_groups=mesh['tm'=32,'rows'=16] {'rows'}, dimensions={3}, use_global_device_ids=true | all-gather | bytes 1044480 | tf_op jit(solution)/shard_map/all_gather | solution.py:46
  78.1 4.5 %copy.45 = bf16[2,16,40,384]{3,1,2,0:T(8,128)(2,1)} copy(bf16[2,16,40,384]{2,1,0,3:T(8,128)(2,1)S(1)} %all_gather.7) | data formatting | bytes 1966080 | tf_op jit(solution)/shard_map/all_gather | solution.py:46
  82.7 1.5 %fusion.2 = f32[2,16,40]{1,2,0:T(8,128)S(1)} fusion(bf16[2,16,40,384]{3,1,2,0:T(8,128)(2,1)} %copy.45), kind=kLoop, calls=%fused_computation.5 | loop fusion | flops 1473280 | bytes 988160 | tf_op jit(solution)/shard_map/reduce_sum | solution.py:15
  84.3 0.6 fusion.24
  85.3 0.8 copy-done.4
  86.1 3.5 %fusion.21 = f32[16,16,6,72]{3,1,2,0:T(8,128)S(1)} fusion(bf16[72,3,3,384]{3,0,2,1:T(8,128)(2,1)S(1)} %bitcast.50, bf16[16,2,8,8,384]{4,0,3,2,1:T(8,128)(2,1)S(1)} %fusion.11, pred[16,6]{0,1:T(8,128)(4,1)S(1)} %copy-done.6), kind=kOutput, calls=%fused_computation.22 | convolution fusion | flops 732672000 | bytes 2512992 | tf_op jit(solution)/shard_map/conv_general_dilated | solution.py:23
  89.5 0.5 copy.48
  90.6 1.9 %collective-permute-start.1 = (f32[2,16,40,24]{2,3,1,0:T(8,128)S(1)}, f32[2,16,40,24]{2,3,1,0:T(8,128)S(1)}, u32[]{:S(2)}, u32[]{:S(2)}) collective-permute-start(f32[2,16,40,24]{2,3,1,0:T(8,128)S(1)} %pad_maximum_fusion.1), channel_id=1, source_target_pairs={{0,16},{16,32},{32,48},{48,64},{64,80},{80,96},{96,112},{112,128},... | collective-permute-start | bytes 368648 | tf_op jit(solution)/shard_map/ppermute | solution.py:10
  92.5 0.8 dynamic_slice.7
  93.3 13.1 %collective-permute-done.1 = f32[2,16,40,24]{2,3,1,0:T(8,128)S(1)} collective-permute-done((f32[2,16,40,24]{2,3,1,0:T(8,128)S(1)}, f32[2,16,40,24]{2,3,1,0:T(8,128)S(1)}, u32[]{:S(2)}, u32[]{:S(2)}) %collective-permute-start.1) | collective-permute-done | bytes 122912 | tf_op jit(solution)/shard_map/ppermute | solution.py:10
  106.8 13.7 %all_to_all.18 = f32[16,1,1920]{2,1,0:T(1,128)S(1)} all-to-all(f32[16,1,1920]{2,1,0:T(1,128)S(1)} %reshape.55), channel_id=1, replica_groups=mesh['tm'=32,'rows'=16] {'rows'}, dimensions={0} | all-to-all | bytes 245760 | tf_op jit(solution)/shard_map/all_to_all | solution.py:49
  120.5 0.5 broadcast.48
  121.0 0.9 reduce.1
  122.5 0.6 fusion.36
  (38 shorter events, 3.1 us)
Async XLA Ops:
  28.7 1.0 copy-start.2
  28.7 1.1 copy-start.6
  34.2 3.4 %copy-start.3 = (bf16[24,3,3,3,384]{4,0,3,2,1:T(8,128)(2,1)S(1)}, bf16[24,3,3,3,384]{4,0,3,2,1:T(8,128)(2,1)}, u32[]{:S(2)}) copy-start(bf16[24,3,3,3,384]{4,0,3,2,1:T(8,128)(2,1)} %param.12) | copy-start | bytes 1492996
  34.3 15.9 %collective-permute-start = (f32[2,16,40,24]{2,3,1,0:T(8,128)S(1)}, f32[2,16,40,24]{2,3,1,0:T(8,128)S(1)}, u32[]{:S(2)}, u32[]{:S(2)}) collective-permute-start(f32[2,16,40,24]{2,3,1,0:T(8,128)S(1)} %pad_maximum_fusion), channel_id=1, source_target_pairs={{0,16},{16,32},{32,48},{48,64},{64,80},{80,96},{96,112},{112,128},... | collective-permute-start | bytes 368648 | tf_op jit(solution)/shard_map/ppermute | solution.py:10
  78.1 6.1 %copy-start.5 = (f32[384]{0:T(512)S(1)}, f32[384]{0:T(512)}, u32[]{:S(2)}) copy-start(f32[384]{0:T(512)} %param.11) | copy-start | bytes 4612
  82.7 1.6 %copy-start = (bf16[2,16,40,384]{3,1,2,0:T(8,128)(2,1)S(1)}, bf16[2,16,40,384]{3,1,2,0:T(8,128)(2,1)}, u32[]{:S(2)}) copy-start(bf16[2,16,40,384]{3,1,2,0:T(8,128)(2,1)} %copy.45) | copy-start | bytes 2949124
  85.1 1.0 copy-start.4
  90.6 15.8 %collective-permute-start.1 = (f32[2,16,40,24]{2,3,1,0:T(8,128)S(1)}, f32[2,16,40,24]{2,3,1,0:T(8,128)S(1)}, u32[]{:S(2)}, u32[]{:S(2)}) collective-permute-start(f32[2,16,40,24]{2,3,1,0:T(8,128)S(1)} %pad_maximum_fusion.1), channel_id=1, source_target_pairs={{0,16},{16,32},{32,48},{48,64},{64,80},{80,96},{96,112},{112,128},... | collective-permute-start | bytes 368648 | tf_op jit(solution)/shard_map/ppermute | solution.py:10
  106.8 15.6 %copy-start.1 = (bf16[2,1,40,384]{3,2,1,0:T(8,128)(2,1)S(1)}, bf16[2,1,40,384]{3,2,1,0:T(8,128)(2,1)}, u32[]{:S(2)}) copy-start(bf16[2,1,40,384]{3,2,1,0:T(8,128)(2,1)} %param.7) | copy-start | bytes 184324

commit v5 on v4

--- a/solution.py
+++ b/solution.py
@@ -31,7 +31,7 @@
     tap = [product[..., a * part_width : (a + 1) * part_width] for a in range(3)]
     onward = jnp.stack([tap[0][0] + tap[1][1], tap[0][1]], 0)
     kept = jnp.stack([tap[2][0], tap[1][0] + tap[2][1]], 0)
-    arrived = passed_along(onward, "tm", 1)
+    arrived = passed_along(onward.reshape(onward.shape[0], -1), "tm", 1).reshape(onward.shape)
     return kept + arrived + bias_part
 
 
@@ -43,7 +43,10 @@
     normed_one = norm_silu(features, gain_one)
     full_one = lax.all_gather(normed_one, "rows", axis=1, tiled=True)
     conv_one = causal_conv(full_one, weight_one, bias_first).astype(jnp.bfloat16)
-    every_channel = lax.all_gather(conv_one, "rows", axis=3, tiled=True)
+    frames, height, columns, _ = conv_one.shape
+    blocks = lax.all_gather(conv_one.reshape(frames, -1), "rows", axis=0, tiled=False)
+    blocks = blocks.reshape(-1, frames, height, columns, part_width)
+    every_channel = jnp.transpose(blocks, (1, 2, 3, 0, 4)).reshape(frames, height, columns, -1)
     full_two = norm_silu(every_channel, gain_two)
     conv_two = causal_conv(full_two, weight_two, bias_second)
     returned = lax.all_to_all(conv_two, "rows", split_axis=1, concat_axis=3, tiled=True)

time: 124 us -> 122 us (0.984)
  local copies, waits for them, and re-layouts: 12.2 us -> 32.8 us
  waiting for transfers between devices: 24.1 us -> 12.4 us
  blocking collectives: 67.9 us -> 57.4 us
    convert_element_type x1 -> x3, local copies, waits for them, and re-layouts: 0.03 us -> 22.8 us  [norm_silu(): values = values.astype(jnp.float32)]
    ppermute x2, waiting for transfers between devices: 24.1 us -> 12.4 us  [passed_along(): return lax.ppermute(x, axis, pairs)]
    all_gather x1, blocking collectives: 27.8 us -> 18.3 us  [shards(): lax.all_gather(conv_one.reshape(frames, -1), 'rows', axis=0, tiled=False)]
    all_gather x1 -> x0, local copies, waits for them, and re-layouts: 4.52 us -> none  [shards(): every_channel = lax.all_gather(conv_one, 'rows', axis=3, tiled=True)]
    another operation x0 -> x6, local copies, waits for them, and re-layouts: none -> 1.49 us  [the longest x4 1 us: causal_conv(): onward = jnp.stack([tap[0][0] + tap[1][1], tap[0][1]], 0)]
    unnamed x20 -> x14, local copies, waits for them, and re-layouts: 3.91 us -> 2.68 us
where the time goes in v5:
time: 122 us; the launch traced here: 121 us
  blocking collectives  57.4 us (47%)
  local copies, waits for them, and re-layouts  32.8 us (27%)
  waiting for transfers between devices  12.4 us (10%)
  matrix products  6.95 us (6%)
  other arithmetic  6.42 us (5%)
  starting transfers between devices  5.04 us (4%)
    all_gather x1, blocking collectives, shards(): full_one = lax.all_gather(normed_one, 'rows', axis=1, tiled=True)  26.4 us
    convert_element_type x3, local copies, waits for them, and re-layouts, norm_silu(): values = values.astype(jnp.float32)  22.8 us
    all_gather x1, blocking collectives, shards(): lax.all_gather(conv_one.reshape(frames, -1), 'rows', axis=0, tiled=False)  18.3 us
    all_to_all x1, blocking collectives, shards(): lax.all_to_all(conv_two, 'rows', split_axis=1, concat_axis=3, tiled=True)  12.7 us
    ppermute x2, waiting for transfers between devices, passed_along(): return lax.ppermute(x, axis, pairs)  12.4 us
    conv_general_dilated x2, matrix products, causal_conv(): lax.conv_general_dilated(own, stacked, window_strides=(1, 1), padding=((1...  6.95 us
    ppermute x2, starting transfers between devices, passed_along(): return lax.ppermute(x, axis, pairs)  5.04 us
    unnamed x14, local copies, waits for them, and re-layouts  2.68 us
  transfers between devices with their start and end apart: 2, of which 2 were waited for; matrix products, arithmetic and copies ran while one was open for 2% of the time, Pallas kernels for 0%

profile of v5, /device:TPU:33, one launch (start us, length us, event | category | flops | bytes accessed | tf_op | source)
XLA Modules:
  0.0 121.3 jit_solution(14448465558925518558)
XLA Ops:
  0.0 0.9 fusion.18
  0.9 1.1 copy.55
  2.0 0.9 fusion.29
  3.0 26.4 %all_gather.6 = bf16[2,16,40,384]{3,2,0,1:T(8,128)(2,1)S(1)} all-gather(bf16[2,1,40,384]{3,2,0,1:T(8,128)(2,1)S(1)} %fusion.29), channel_id=1, replica_groups=mesh['tm'=32,'rows'=16] {'rows'}, dimensions={1}, use_global_device_ids=true | all-gather | bytes 1044480 | tf_op jit(solution)/shard_map/all_gather | solution.py:44
  30.4 3.5 %fusion.10 = f32[16,16,6,72]{3,1,2,0:T(8,128)S(1)} fusion(bf16[72,3,3,384]{3,0,2,1:T(8,128)(2,1)S(1)} %bitcast.71, bf16[16,2,8,8,384]{4,0,3,2,1:T(8,128)(2,1)S(1)} %fusion.2, pred[16,6]{0,1:T(8,128)(4,1)S(1)} %copy-done.3), kind=kOutput, calls=%fused_computation.13 | convolution fusion | flops 732672000 | bytes 2512992 | tf_op jit(solution)/shard_map/conv_general_dilated | solution.py:23
  35.7 3.1 %collective-permute-start = (f32[2,15360]{1,0:T(2,128)S(1)}, f32[2,15360]{1,0:T(2,128)S(1)}, u32[]{:S(2)}, u32[]{:S(2)}) collective-permute-start(f32[2,15360]{1,0:T(2,128)S(1)} %pad_maximum_fusion), channel_id=1, source_target_pairs={{0,16},{16,32},{32,48},{48,64},{64,80},{80,96},{96,112},{112,128},... | collective-permute-start | bytes 368648 | tf_op jit(solution)/shard_map/ppermute | solution.py:10
  38.8 0.8 dynamic_slice.6
  40.6 5.1 %collective-permute-done = f32[2,15360]{1,0:T(2,128)S(1)} collective-permute-done((f32[2,15360]{1,0:T(2,128)S(1)}, f32[2,15360]{1,0:T(2,128)S(1)}, u32[]{:S(2)}, u32[]{:S(2)}) %collective-permute-start) | collective-permute-done | bytes 122912 | tf_op jit(solution)/shard_map/ppermute | solution.py:10
  45.9 18.3 %all-gather.1 = bf16[16,2,15360]{2,1,0:T(2,128)(2,1)S(1)} all-gather(bf16[1,2,15360]{2,1,0:T(2,128)(2,1)S(1)} %fusion.30), channel_id=2, replica_groups=mesh['tm'=32,'rows'=16] {'rows'}, dimensions={0}, use_global_device_ids=true | all-gather | bytes 1044480 | tf_op jit(solution)/shard_map/all_gather | solution.py:47
  64.1 0.5 multiply_reduce_fusion
  64.8 0.5 reduce_sum.27
  65.6 9.2 %reshape.87 = f32[16,2,16,40,24]{4,3,2,0,1:T(8,128)} reshape(f32[16,2,15360]{2,0,1:T(8,128)S(1)} %copy_convert_fusion) | data formatting | bytes 3932160 | tf_op jit(solution)/shard_map/convert_element_type | solution.py:14
  74.8 9.2 %copy.62 = f32[2,16,40,16,24]{2,4,3,1,0:T(8,128)} copy(f32[2,16,40,16,24]{4,2,1,3,0:T(8,128)} %bitcast.59) | data formatting | bytes 3932160 | tf_op jit(solution)/shard_map/convert_element_type | solution.py:14
  84.0 4.4 %copy.63 = f32[2,16,40,384]{3,2,1,0:T(8,128)S(1)} copy(f32[2,16,40,384]{2,3,1,0:T(8,128)} %bitcast.60) | data formatting | bytes 3932160 | tf_op jit(solution)/shard_map/convert_element_type | solution.py:14
  88.3 0.6 fusion.16
  89.5 3.5 %fusion.13 = f32[16,16,6,72]{3,1,2,0:T(8,128)S(1)} fusion(bf16[72,3,3,384]{3,0,2,1:T(8,128)(2,1)S(1)} %bitcast.70, bf16[16,2,8,8,384]{4,0,3,2,1:T(8,128)(2,1)S(1)} %fusion.3, pred[16,6]{0,1:T(8,128)(4,1)S(1)} %copy-done.3), kind=kOutput, calls=%fused_computation.14 | convolution fusion | flops 732672000 | bytes 2512992 | tf_op jit(solution)/shard_map/conv_general_dilated | solution.py:23
  94.9 1.9 %collective-permute-start.1 = (f32[2,15360]{1,0:T(2,128)S(1)}, f32[2,15360]{1,0:T(2,128)S(1)}, u32[]{:S(2)}, u32[]{:S(2)}) collective-permute-start(f32[2,15360]{1,0:T(2,128)S(1)} %pad_maximum_fusion.1), channel_id=1, source_target_pairs={{0,16},{16,32},{32,48},{48,64},{64,80},{80,96},{96,112},{112,128},... | collective-permute-start | bytes 368648 | tf_op jit(solution)/shard_map/ppermute | solution.py:10
  96.9 0.8 dynamic_slice.7
  97.6 7.3 %collective-permute-done.1 = f32[2,15360]{1,0:T(2,128)S(1)} collective-permute-done((f32[2,15360]{1,0:T(2,128)S(1)}, f32[2,15360]{1,0:T(2,128)S(1)}, u32[]{:S(2)}, u32[]{:S(2)}) %collective-permute-start.1) | collective-permute-done | bytes 122912 | tf_op jit(solution)/shard_map/ppermute | solution.py:10
  104.9 0.5 reshape.65
  106.1 12.7 %all_to_all.18 = f32[16,1,1920]{2,1,0:T(1,128)S(1)} all-to-all(f32[16,1,1920]{2,1,0:T(1,128)S(1)} %reshape.99), channel_id=1, replica_groups=mesh['tm'=32,'rows'=16] {'rows'}, dimensions={0} | all-to-all | bytes 245760 | tf_op jit(solution)/shard_map/all_to_all | solution.py:52
  118.7 0.5 broadcast.51
  119.2 0.9 reduce.6
  120.7 0.6 fusion.26
  (52 shorter events, 7.8 us)
Async XLA Ops:
  29.7 0.7 copy-start.3
  34.8 5.0 %copy-start.1 = (bf16[24,3,3,3,384]{4,0,3,2,1:T(8,128)(2,1)S(1)}, bf16[24,3,3,3,384]{4,0,3,2,1:T(8,128)(2,1)}, u32[]{:S(2)}) copy-start(bf16[24,3,3,3,384]{4,0,3,2,1:T(8,128)(2,1)} %param.12) | copy-start | bytes 1492996
  35.7 10.0 %collective-permute-start = (f32[2,15360]{1,0:T(2,128)S(1)}, f32[2,15360]{1,0:T(2,128)S(1)}, u32[]{:S(2)}, u32[]{:S(2)}) collective-permute-start(f32[2,15360]{1,0:T(2,128)S(1)} %pad_maximum_fusion), channel_id=1, source_target_pairs={{0,16},{16,32},{32,48},{48,64},{64,80},{80,96},{96,112},{112,128},... | collective-permute-start | bytes 368648 | tf_op jit(solution)/shard_map/ppermute | solution.py:10
  83.9 4.4 %copy-start.2 = (f32[384]{0:T(512)S(1)}, f32[384]{0:T(512)}, u32[]{:S(2)}) copy-start(f32[384]{0:T(512)} %param.11) | copy-start | bytes 4612
  94.9 10.0 %collective-permute-start.1 = (f32[2,15360]{1,0:T(2,128)S(1)}, f32[2,15360]{1,0:T(2,128)S(1)}, u32[]{:S(2)}, u32[]{:S(2)}) collective-permute-start(f32[2,15360]{1,0:T(2,128)S(1)} %pad_maximum_fusion.1), channel_id=1, source_target_pairs={{0,16},{16,32},{32,48},{48,64},{64,80},{80,96},{96,112},{112,128},... | collective-permute-start | bytes 368648 | tf_op jit(solution)/shard_map/ppermute | solution.py:10
  105.7 14.9 %copy-start = (bf16[2,1,40,384]{3,2,1,0:T(8,128)(2,1)S(1)}, bf16[2,1,40,384]{3,2,1,0:T(8,128)(2,1)}, u32[]{:S(2)}) copy-start(bf16[2,1,40,384]{3,2,1,0:T(8,128)(2,1)} %param.7) | copy-start | bytes 184324

commit v6 on v3

--- a/solution.py
+++ b/solution.py
@@ -31,7 +31,7 @@
     tap = [product[..., a * part_width : (a + 1) * part_width] for a in range(3)]
     onward = jnp.stack([tap[0][0] + tap[1][1], tap[0][1]], 0)
     kept = jnp.stack([tap[2][0], tap[1][0] + tap[2][1]], 0)
-    arrived = passed_along(onward, "tm", 1)
+    arrived = passed_along(onward.reshape(onward.shape[0], -1), "tm", 1).reshape(onward.shape)
     return kept + arrived + bias_part
 
 

time: 120 us -> 112 us (0.933)
  waiting for transfers between devices: 32.7 us -> 21.1 us
  local copies, waits for them, and re-layouts: 7.49 us -> 10.5 us
    ppermute x2, waiting for transfers between devices: 25 us -> 13.4 us  [passed_along(): return lax.ppermute(x, axis, pairs)]
    reshape x0 -> x4, local copies, waits for them, and re-layouts: none -> 1.37 us  [causal_conv(): passed_along(onward.reshape(onward.shape[0], -1), 'tm', 1)]
where the time goes in v6:
time: 112 us; the launch traced here: 111 us
  blocking collectives  58.1 us (52%)
  waiting for transfers between devices  21.1 us (19%)
  local copies, waits for them, and re-layouts  10.5 us (9%)
  starting transfers between devices  9.3 us (8%)
  matrix products  6.96 us (6%)
  other arithmetic  4.71 us (4%)
    all_gather x1, blocking collectives, shards(): full_one = lax.all_gather(normed_one, 'rows', axis=1, tiled=True)  26.4 us
    all_gather x1, blocking collectives, shards(): full_two = lax.all_gather(normed_two, 'rows', axis=1, tiled=True)  17.6 us
    all_to_all x1, blocking collectives, shards(): lax.all_to_all(conv_two, 'rows', split_axis=1, concat_axis=3, tiled=True)  14.1 us
    ppermute x2, waiting for transfers between devices, passed_along(): return lax.ppermute(x, axis, pairs)  13.4 us
    all_to_all x1, waiting for transfers between devices, shards(): lax.all_to_all(conv_one, 'rows', split_axis=1, concat_axis=3, tiled=True)  7.76 us
    conv_general_dilated x2, matrix products, causal_conv(): lax.conv_general_dilated(own, stacked, window_strides=(1, 1), padding=((1...  6.96 us
    ppermute x2, starting transfers between devices, passed_along(): return lax.ppermute(x, axis, pairs)  5.05 us
    all_to_all x1, starting transfers between devices, shards(): lax.all_to_all(conv_one, 'rows', split_axis=1, concat_axis=3, tiled=True)  4.25 us
  transfers between devices with their start and end apart: 3, of which 3 were waited for; matrix products, arithmetic and copies ran while one was open for 1% of the time, Pallas kernels for 0%

profile of v6, /device:TPU:33, one launch (start us, length us, event | category | flops | bytes accessed | tf_op | source)
XLA Modules:
  0.0 111.1 jit_solution(11718824173448043643)
XLA Ops:
  0.0 0.9 fusion.20
  0.9 0.9 fusion.29
  1.9 26.4 %all_gather.6 = bf16[2,16,40,384]{3,2,0,1:T(8,128)(2,1)S(1)} all-gather(bf16[2,1,40,384]{3,2,0,1:T(8,128)(2,1)S(1)} %fusion.29), channel_id=1, replica_groups=mesh['tm'=32,'rows'=16] {'rows'}, dimensions={1}, use_global_device_ids=true | all-gather | bytes 1044480 | tf_op jit(solution)/shard_map/all_gather | solution.py:44
  28.9 0.8 copy-done.1
  29.8 3.5 %fusion.10 = f32[16,16,6,72]{3,1,2,0:T(8,128)S(1)} fusion(bf16[72,3,3,384]{3,0,2,1:T(8,128)(2,1)S(1)} %bitcast.74, bf16[16,2,8,8,384]{4,0,3,2,1:T(8,128)(2,1)S(1)} %fusion.2, pred[16,6]{0,1:T(8,128)(4,1)S(1)} %copy-done.4), kind=kOutput, calls=%fused_computation.11 | convolution fusion | flops 732672000 | bytes 2512992 | tf_op jit(solution)/shard_map/conv_general_dilated | solution.py:23
  33.3 0.5 copy.56
  35.2 3.1 %collective-permute-start = (f32[2,15360]{1,0:T(2,128)S(1)}, f32[2,15360]{1,0:T(2,128)S(1)}, u32[]{:S(2)}, u32[]{:S(2)}) collective-permute-start(f32[2,15360]{1,0:T(2,128)S(1)} %pad_maximum_fusion), channel_id=1, source_target_pairs={{0,16},{16,32},{32,48},{48,64},{64,80},{80,96},{96,112},{112,128},... | collective-permute-start | bytes 368648 | tf_op jit(solution)/shard_map/ppermute | solution.py:10
  38.4 0.8 dynamic_slice.6
  39.1 6.1 %collective-permute-done = f32[2,15360]{1,0:T(2,128)S(1)} collective-permute-done((f32[2,15360]{1,0:T(2,128)S(1)}, f32[2,15360]{1,0:T(2,128)S(1)}, u32[]{:S(2)}, u32[]{:S(2)}) %collective-permute-start) | collective-permute-done | bytes 122912 | tf_op jit(solution)/shard_map/ppermute | solution.py:10
  45.2 0.5 reshape.105
  46.0 0.9 reshape.130
  46.9 4.2 %all-to-all-start = ((bf16[16,2,960]{2,1,0:T(2,128)(2,1)}), bf16[16,2,960]{2,1,0:T(2,128)(2,1)S(1)}, u32[]{:S(2)}, u32[]{:S(2)}) async-start(bf16[16,2,960]{2,1,0:T(2,128)(2,1)} %reshape.130), calls=%async_computation | async-start | bytes 131072 | tf_op jit(solution)/shard_map/all_to_all | solution.py:46
  51.2 7.8 %all-to-all-done = bf16[16,2,960]{2,1,0:T(2,128)(2,1)S(1)} async-done(((bf16[16,2,960]{2,1,0:T(2,128)(2,1)}), bf16[16,2,960]{2,1,0:T(2,128)(2,1)S(1)}, u32[]{:S(2)}, u32[]{:S(2)}) %all-to-all-start) | async-done | bytes 61472 | tf_op jit(solution)/shard_map/all_to_all | solution.py:46
  59.6 17.6 %all_gather.7 = bf16[2,16,40,384]{3,2,0,1:T(8,128)(2,1)S(1)} all-gather(bf16[2,1,40,384]{3,2,0,1:T(8,128)(2,1)S(1)} %fusion.30), channel_id=1, replica_groups=mesh['tm'=32,'rows'=16] {'rows'}, dimensions={1}, use_global_device_ids=true | all-gather | bytes 1044480 | tf_op jit(solution)/shard_map/all_gather | solution.py:48
  77.9 3.5 %fusion.13 = f32[16,16,6,72]{3,1,2,0:T(8,128)S(1)} fusion(bf16[72,3,3,384]{3,0,2,1:T(8,128)(2,1)S(1)} %bitcast.73, bf16[16,2,8,8,384]{4,0,3,2,1:T(8,128)(2,1)S(1)} %fusion.3, pred[16,6]{0,1:T(8,128)(4,1)S(1)} %copy-done.4), kind=kOutput, calls=%fused_computation.12 | convolution fusion | flops 732672000 | bytes 2512992 | tf_op jit(solution)/shard_map/conv_general_dilated | solution.py:23
  81.4 0.5 copy.68
  83.3 1.9 %collective-permute-start.1 = (f32[2,15360]{1,0:T(2,128)S(1)}, f32[2,15360]{1,0:T(2,128)S(1)}, u32[]{:S(2)}, u32[]{:S(2)}) collective-permute-start(f32[2,15360]{1,0:T(2,128)S(1)} %pad_maximum_fusion.1), channel_id=1, source_target_pairs={{0,16},{16,32},{32,48},{48,64},{64,80},{80,96},{96,112},{112,128},... | collective-permute-start | bytes 368648 | tf_op jit(solution)/shard_map/ppermute | solution.py:10
  85.2 0.8 dynamic_slice.7
  86.0 7.3 %collective-permute-done.1 = f32[2,15360]{1,0:T(2,128)S(1)} collective-permute-done((f32[2,15360]{1,0:T(2,128)S(1)}, f32[2,15360]{1,0:T(2,128)S(1)}, u32[]{:S(2)}, u32[]{:S(2)}) %collective-permute-start.1) | collective-permute-done | bytes 122912 | tf_op jit(solution)/shard_map/ppermute | solution.py:10
  93.3 0.5 reshape.107
  94.5 14.1 %all_to_all.27 = f32[16,1,1920]{2,1,0:T(1,128)S(1)} all-to-all(f32[16,1,1920]{2,1,0:T(1,128)S(1)} %reshape.132), channel_id=1, replica_groups=mesh['tm'=32,'rows'=16] {'rows'}, dimensions={0} | all-to-all | bytes 245760 | tf_op jit(solution)/shard_map/all_to_all | solution.py:50
  108.5 0.5 broadcast.93
  109.0 0.9 reduce.5
  110.5 0.6 fusion.28
  (52 shorter events, 6.2 us)
Async XLA Ops:
  28.7 1.0 copy-start.1
  28.7 1.1 copy-start.4
  35.2 10.0 %collective-permute-start = (f32[2,15360]{1,0:T(2,128)S(1)}, f32[2,15360]{1,0:T(2,128)S(1)}, u32[]{:S(2)}, u32[]{:S(2)}) collective-permute-start(f32[2,15360]{1,0:T(2,128)S(1)} %pad_maximum_fusion), channel_id=1, source_target_pairs={{0,16},{16,32},{32,48},{48,64},{64,80},{80,96},{96,112},{112,128},... | collective-permute-start | bytes 368648 | tf_op jit(solution)/shard_map/ppermute | solution.py:10
  39.1 12.0 %copy-start.2 = (bf16[24,3,3,3,384]{4,0,3,2,1:T(8,128)(2,1)S(1)}, bf16[24,3,3,3,384]{4,0,3,2,1:T(8,128)(2,1)}, u32[]{:S(2)}) copy-start(bf16[24,3,3,3,384]{4,0,3,2,1:T(8,128)(2,1)} %param.12) | copy-start | bytes 1492996
  46.9 12.1 %all-to-all-start = ((bf16[16,2,960]{2,1,0:T(2,128)(2,1)}), bf16[16,2,960]{2,1,0:T(2,128)(2,1)S(1)}, u32[]{:S(2)}, u32[]{:S(2)}) async-start(bf16[16,2,960]{2,1,0:T(2,128)(2,1)} %reshape.130), calls=%async_computation | async-start | bytes 131072 | tf_op jit(solution)/shard_map/all_to_all | solution.py:46
  51.1 8.4 %copy-start.3 = (f32[384]{0:T(512)S(1)}, f32[384]{0:T(512)}, u32[]{:S(2)}) copy-start(f32[384]{0:T(512)} %param.11) | copy-start | bytes 4612
  83.3 10.0 %collective-permute-start.1 = (f32[2,15360]{1,0:T(2,128)S(1)}, f32[2,15360]{1,0:T(2,128)S(1)}, u32[]{:S(2)}, u32[]{:S(2)}) collective-permute-start(f32[2,15360]{1,0:T(2,128)S(1)} %pad_maximum_fusion.1), channel_id=1, source_target_pairs={{0,16},{16,32},{32,48},{48,64},{64,80},{80,96},{96,112},{112,128},... | collective-permute-start | bytes 368648 | tf_op jit(solution)/shard_map/ppermute | solution.py:10
  94.4 16.0 %copy-start = (bf16[2,1,40,384]{3,2,1,0:T(8,128)(2,1)S(1)}, bf16[2,1,40,384]{3,2,1,0:T(8,128)(2,1)}, u32[]{:S(2)}) copy-start(bf16[2,1,40,384]{3,2,1,0:T(8,128)(2,1)} %param.7) | copy-start | bytes 184324

commit v7 on v6

--- a/solution.py
+++ b/solution.py
@@ -31,7 +31,8 @@
     tap = [product[..., a * part_width : (a + 1) * part_width] for a in range(3)]
     onward = jnp.stack([tap[0][0] + tap[1][1], tap[0][1]], 0)
     kept = jnp.stack([tap[2][0], tap[1][0] + tap[2][1]], 0)
-    arrived = passed_along(onward.reshape(onward.shape[0], -1), "tm", 1).reshape(onward.shape)
+    sent = onward.reshape(onward.shape[0], -1).astype(jnp.bfloat16)
+    arrived = passed_along(sent, "tm", 1).reshape(onward.shape).astype(jnp.float32)
     return kept + arrived + bias_part
 
 

time: 112 us -> 109 us (0.973)
  waiting for transfers between devices: 21.1 us -> 18.5 us
    ppermute x2, waiting for transfers between devices: 13.4 us -> 10.7 us  [passed_along(): return lax.ppermute(x, axis, pairs)]
    reshape x4 -> x0, local copies, waits for them, and re-layouts: 1.37 us -> none  [causal_conv(): passed_along(onward.reshape(onward.shape[0], -1), 'tm', 1)]
    convert_element_type x0 -> x4, local copies, waits for them, and re-layouts: none -> 1.25 us  [causal_conv(): passed_along(sent, 'tm', 1).reshape(onward.shape).astype(jnp.float32)]
where the time goes in v7:
time: 109 us; the launch traced here: 108 us
  blocking collectives  58.1 us (53%)
  waiting for transfers between devices  18.5 us (17%)
  local copies, waits for them, and re-layouts  10.4 us (10%)
  starting transfers between devices  9.3 us (9%)
  matrix products  6.94 us (6%)
  other arithmetic  4.75 us (4%)
    all_gather x1, blocking collectives, shards(): full_one = lax.all_gather(normed_one, 'rows', axis=1, tiled=True)  26.4 us
    all_gather x1, blocking collectives, shards(): full_two = lax.all_gather(normed_two, 'rows', axis=1, tiled=True)  17.6 us
    all_to_all x1, blocking collectives, shards(): lax.all_to_all(conv_two, 'rows', split_axis=1, concat_axis=3, tiled=True)  14.1 us
    ppermute x2, waiting for transfers between devices, passed_along(): return lax.ppermute(x, axis, pairs)  10.7 us
    all_to_all x1, waiting for transfers between devices, shards(): lax.all_to_all(conv_one, 'rows', split_axis=1, concat_axis=3, tiled=True)  7.76 us
    conv_general_dilated x2, matrix products, causal_conv(): lax.conv_general_dilated(own, stacked, window_strides=(1, 1), padding=((1...  6.94 us
    ppermute x2, starting transfers between devices, passed_along(): return lax.ppermute(x, axis, pairs)  5.05 us
    all_to_all x1, starting transfers between devices, shards(): lax.all_to_all(conv_one, 'rows', split_axis=1, concat_axis=3, tiled=True)  4.25 us
  transfers between devices with their start and end apart: 3, of which 3 were waited for; matrix products, arithmetic and copies ran while one was open for 1% of the time, Pallas kernels for 0%

profile of v7, /device:TPU:33, one launch (start us, length us, event | category | flops | bytes accessed | tf_op | source)
XLA Modules:
  0.0 108.4 jit_solution(14675186359571963938)
XLA Ops:
  0.0 0.9 fusion.22
  0.9 0.9 fusion.31
  1.9 26.4 %all_gather.6 = bf16[2,16,40,384]{3,2,0,1:T(8,128)(2,1)S(1)} all-gather(bf16[2,1,40,384]{3,2,0,1:T(8,128)(2,1)S(1)} %fusion.31), channel_id=1, replica_groups=mesh['tm'=32,'rows'=16] {'rows'}, dimensions={1}, use_global_device_ids=true | all-gather | bytes 1044480 | tf_op jit(solution)/shard_map/all_gather | solution.py:45
  28.9 0.8 copy-done.1
  29.8 3.5 %fusion.35 = (bf16[16,16,6,72]{3,1,2,0:T(8,128)(2,1)S(1)}, f32[16,16,6,72]{3,1,2,0:T(8,128)S(1)}) fusion(bf16[72,3,3,384]{3,0,2,1:T(8,128)(2,1)S(1)} %bitcast.86, bf16[16,2,8,8,384]{4,0,3,2,1:T(8,128)(2,1)S(1)} %fusion.2, pred[16,6]{0,1:T(8,128)(4,1)S(1)} %copy-done.4), kind=kOutput, calls=%fused_computation.52 | convolution fusion | flops 732782592 | bytes 2734176 | tf_op jit(solution)/shard_map/conv_general_dilated | solution.py:23
  33.3 0.5 copy.60
  35.3 3.1 %collective-permute-start = (bf16[2,15360]{1,0:T(2,128)(2,1)S(1)}, bf16[2,15360]{1,0:T(2,128)(2,1)S(1)}, u32[]{:S(2)}, u32[]{:S(2)}) collective-permute-start(bf16[2,15360]{1,0:T(2,128)(2,1)S(1)} %pad_maximum_fusion), channel_id=1, source_target_pairs={{0,16},{16,32},{32,48},{48,64},{64,80},{80,96},{96,112},{112,128},... | collective-permute-start | bytes 184328 | tf_op jit(solution)/shard_map/ppermute | solution.py:10
  38.4 0.8 dynamic_slice.6
  39.2 4.8 %collective-permute-done = bf16[2,15360]{1,0:T(2,128)(2,1)S(1)} collective-permute-done((bf16[2,15360]{1,0:T(2,128)(2,1)S(1)}, bf16[2,15360]{1,0:T(2,128)(2,1)S(1)}, u32[]{:S(2)}, u32[]{:S(2)}) %collective-permute-start) | collective-permute-done | bytes 61472 | tf_op jit(solution)/shard_map/ppermute | solution.py:10
  43.9 0.4 reshape.128
  44.7 0.9 reshape.140
  45.5 4.2 %all-to-all-start = ((bf16[16,2,960]{2,1,0:T(2,128)(2,1)}), bf16[16,2,960]{2,1,0:T(2,128)(2,1)S(1)}, u32[]{:S(2)}, u32[]{:S(2)}) async-start(bf16[16,2,960]{2,1,0:T(2,128)(2,1)} %reshape.140), calls=%async_computation | async-start | bytes 131072 | tf_op jit(solution)/shard_map/all_to_all | solution.py:47
  49.9 7.8 %all-to-all-done = bf16[16,2,960]{2,1,0:T(2,128)(2,1)S(1)} async-done(((bf16[16,2,960]{2,1,0:T(2,128)(2,1)}), bf16[16,2,960]{2,1,0:T(2,128)(2,1)S(1)}, u32[]{:S(2)}, u32[]{:S(2)}) %all-to-all-start) | async-done | bytes 61472 | tf_op jit(solution)/shard_map/all_to_all | solution.py:47
  58.3 17.6 %all_gather.7 = bf16[2,16,40,384]{3,2,0,1:T(8,128)(2,1)S(1)} all-gather(bf16[2,1,40,384]{3,2,0,1:T(8,128)(2,1)S(1)} %fusion.32), channel_id=1, replica_groups=mesh['tm'=32,'rows'=16] {'rows'}, dimensions={1}, use_global_device_ids=true | all-gather | bytes 1044480 | tf_op jit(solution)/shard_map/all_gather | solution.py:49
  76.5 3.5 %fusion.36 = (bf16[16,16,6,72]{3,1,2,0:T(8,128)(2,1)S(1)}, f32[16,16,6,72]{3,1,2,0:T(8,128)S(1)}) fusion(bf16[72,3,3,384]{3,0,2,1:T(8,128)(2,1)S(1)} %bitcast.85, bf16[16,2,8,8,384]{4,0,3,2,1:T(8,128)(2,1)S(1)} %fusion.3, pred[16,6]{0,1:T(8,128)(4,1)S(1)} %copy-done.4), kind=kOutput, calls=%fused_computation.53 | convolution fusion | flops 732782592 | bytes 2734176 | tf_op jit(solution)/shard_map/conv_general_dilated | solution.py:23
  80.0 0.5 copy.73
  82.0 1.9 %collective-permute-start.1 = (bf16[2,15360]{1,0:T(2,128)(2,1)S(1)}, bf16[2,15360]{1,0:T(2,128)(2,1)S(1)}, u32[]{:S(2)}, u32[]{:S(2)}) collective-permute-start(bf16[2,15360]{1,0:T(2,128)(2,1)S(1)} %pad_maximum_fusion.1), channel_id=1, source_target_pairs={{0,16},{16,32},{32,48},{48,64},{64,80},{80,96},{96,112},{112,128},... | collective-permute-start | bytes 184328 | tf_op jit(solution)/shard_map/ppermute | solution.py:10
  83.9 0.8 dynamic_slice.7
  84.7 6.0 %collective-permute-done.1 = bf16[2,15360]{1,0:T(2,128)(2,1)S(1)} collective-permute-done((bf16[2,15360]{1,0:T(2,128)(2,1)S(1)}, bf16[2,15360]{1,0:T(2,128)(2,1)S(1)}, u32[]{:S(2)}, u32[]{:S(2)}) %collective-permute-start.1) | collective-permute-done | bytes 61472 | tf_op jit(solution)/shard_map/ppermute | solution.py:10
  90.7 0.4 reshape.130
  91.8 14.1 %all_to_all.27 = f32[16,1,1920]{2,1,0:T(1,128)S(1)} all-to-all(f32[16,1,1920]{2,1,0:T(1,128)S(1)} %reshape.142), channel_id=1, replica_groups=mesh['tm'=32,'rows'=16] {'rows'}, dimensions={0} | all-to-all | bytes 245760 | tf_op jit(solution)/shard_map/all_to_all | solution.py:51
  105.8 0.5 broadcast.93
  106.4 0.9 reduce.5
  107.8 0.6 fusion.30
  (58 shorter events, 6.3 us)
Async XLA Ops:
  28.7 1.0 copy-start.1
  28.7 1.1 copy-start.4
  35.3 8.7 %collective-permute-start = (bf16[2,15360]{1,0:T(2,128)(2,1)S(1)}, bf16[2,15360]{1,0:T(2,128)(2,1)S(1)}, u32[]{:S(2)}, u32[]{:S(2)}) collective-permute-start(bf16[2,15360]{1,0:T(2,128)(2,1)S(1)} %pad_maximum_fusion), channel_id=1, source_target_pairs={{0,16},{16,32},{32,48},{48,64},{64,80},{80,96},{96,112},{112,128},... | collective-permute-start | bytes 184328 | tf_op jit(solution)/shard_map/ppermute | solution.py:10
  39.2 10.6 %copy-start.2 = (bf16[24,3,3,3,384]{4,0,3,2,1:T(8,128)(2,1)S(1)}, bf16[24,3,3,3,384]{4,0,3,2,1:T(8,128)(2,1)}, u32[]{:S(2)}) copy-start(bf16[24,3,3,3,384]{4,0,3,2,1:T(8,128)(2,1)} %param.12) | copy-start | bytes 1492996
  45.5 12.1 %all-to-all-start = ((bf16[16,2,960]{2,1,0:T(2,128)(2,1)}), bf16[16,2,960]{2,1,0:T(2,128)(2,1)S(1)}, u32[]{:S(2)}, u32[]{:S(2)}) async-start(bf16[16,2,960]{2,1,0:T(2,128)(2,1)} %reshape.140), calls=%async_computation | async-start | bytes 131072 | tf_op jit(solution)/shard_map/all_to_all | solution.py:47
  49.8 8.4 %copy-start.3 = (f32[384]{0:T(512)S(1)}, f32[384]{0:T(512)}, u32[]{:S(2)}) copy-start(f32[384]{0:T(512)} %param.11) | copy-start | bytes 4612
  82.0 8.7 %collective-permute-start.1 = (bf16[2,15360]{1,0:T(2,128)(2,1)S(1)}, bf16[2,15360]{1,0:T(2,128)(2,1)S(1)}, u32[]{:S(2)}, u32[]{:S(2)}) collective-permute-start(bf16[2,15360]{1,0:T(2,128)(2,1)S(1)} %pad_maximum_fusion.1), channel_id=1, source_target_pairs={{0,16},{16,32},{32,48},{48,64},{64,80},{80,96},{96,112},{112,128},... | collective-permute-start | bytes 184328 | tf_op jit(solution)/shard_map/ppermute | solution.py:10
  91.8 16.0 %copy-start = (bf16[2,1,40,384]{3,2,1,0:T(8,128)(2,1)S(1)}, bf16[2,1,40,384]{3,2,1,0:T(8,128)(2,1)}, u32[]{:S(2)}) copy-start(bf16[2,1,40,384]{3,2,1,0:T(8,128)(2,1)} %param.7) | copy-start | bytes 184324

commit v8 on v6

--- a/solution.py
+++ b/solution.py
@@ -47,8 +47,13 @@
     normed_two = norm_silu(own_rows, gain_two)
     full_two = lax.all_gather(normed_two, "rows", axis=1, tiled=True)
     conv_two = causal_conv(full_two, weight_two, bias_second)
-    returned = lax.all_to_all(conv_two, "rows", split_axis=1, concat_axis=3, tiled=True)
-    return (features.astype(jnp.float32) + returned).astype(jnp.bfloat16)
+    high = conv_two.astype(jnp.bfloat16)
+    low = (conv_two - high.astype(jnp.float32)).astype(jnp.bfloat16)
+    pair = jnp.concatenate([high, low], 0)
+    returned = lax.all_to_all(pair, "rows", split_axis=1, concat_axis=3, tiled=True).astype(jnp.float32)
+    frames = conv_two.shape[0]
+    total = returned[:frames] + returned[frames:]
+    return (features.astype(jnp.float32) + total).astype(jnp.bfloat16)
 
 
 def solution(mesh):

time: 112 us -> 111 us (level)
  no operation moved by 1% of the time
where the time goes in v8:
time: 111 us
  blocking collectives  58 us (52%)
  waiting for transfers between devices  21.1 us (19%)
  local copies, waits for them, and re-layouts  11 us (10%)
  starting transfers between devices  9.3 us (8%)
  matrix products  6.95 us (6%)
  other arithmetic  4 us (4%)
    all_gather x1, blocking collectives, shards(): full_one = lax.all_gather(normed_one, 'rows', axis=1, tiled=True)  26.4 us
    all_gather x1, blocking collectives, shards(): full_two = lax.all_gather(normed_two, 'rows', axis=1, tiled=True)  17.6 us
    all_to_all x1, blocking collectives, shards(): lax.all_to_all(pair, 'rows', split_axis=1, concat_axis=3, tiled=True)  13.9 us
    ppermute x2, waiting for transfers between devices, passed_along(): return lax.ppermute(x, axis, pairs)  13.4 us
    all_to_all x1, waiting for transfers between devices, shards(): lax.all_to_all(conv_one, 'rows', split_axis=1, concat_axis=3, tiled=True)  7.76 us
    conv_general_dilated x2, matrix products, causal_conv(): lax.conv_general_dilated(own, stacked, window_strides=(1, 1), padding=((1...  6.95 us
    ppermute x2, starting transfers between devices, passed_along(): return lax.ppermute(x, axis, pairs)  5.05 us
    unnamed x18, local copies, waits for them, and re-layouts  4.44 us
  transfers between devices with their start and end apart: 3, of which 3 were waited for; matrix products, arithmetic and copies ran while one was open for 1% of the time, Pallas kernels for 0%

profile of v8, /device:TPU:33, one launch (start us, length us, event | category | flops | bytes accessed | tf_op | source)
XLA Modules:
  0.0 110.8 jit_solution(4827505447209610484)
XLA Ops:
  0.0 0.9 fusion.20
  0.9 0.9 fusion.29
  1.9 26.4 %all_gather.6 = bf16[2,16,40,384]{3,2,0,1:T(8,128)(2,1)S(1)} all-gather(bf16[2,1,40,384]{3,2,0,1:T(8,128)(2,1)S(1)} %fusion.29), channel_id=1, replica_groups=mesh['tm'=32,'rows'=16] {'rows'}, dimensions={1}, use_global_device_ids=true | all-gather | bytes 1044480 | tf_op jit(solution)/shard_map/all_gather | solution.py:44
  28.9 0.8 copy-done.1
  29.8 3.5 %fusion.10 = f32[16,16,6,72]{3,1,2,0:T(8,128)S(1)} fusion(bf16[72,3,3,384]{3,0,2,1:T(8,128)(2,1)S(1)} %bitcast.75, bf16[16,2,8,8,384]{4,0,3,2,1:T(8,128)(2,1)S(1)} %fusion.2, pred[16,6]{0,1:T(8,128)(4,1)S(1)} %copy-done.4), kind=kOutput, calls=%fused_computation.11 | convolution fusion | flops 732672000 | bytes 2512992 | tf_op jit(solution)/shard_map/conv_general_dilated | solution.py:23
  33.3 0.5 copy.56
  35.2 3.1 %collective-permute-start = (f32[2,15360]{1,0:T(2,128)S(1)}, f32[2,15360]{1,0:T(2,128)S(1)}, u32[]{:S(2)}, u32[]{:S(2)}) collective-permute-start(f32[2,15360]{1,0:T(2,128)S(1)} %pad_maximum_fusion.1), channel_id=1, source_target_pairs={{0,16},{16,32},{32,48},{48,64},{64,80},{80,96},{96,112},{112,128},... | collective-permute-start | bytes 368648 | tf_op jit(solution)/shard_map/ppermute | solution.py:10
  38.4 0.8 dynamic_slice.6
  39.1 6.1 %collective-permute-done = f32[2,15360]{1,0:T(2,128)S(1)} collective-permute-done((f32[2,15360]{1,0:T(2,128)S(1)}, f32[2,15360]{1,0:T(2,128)S(1)}, u32[]{:S(2)}, u32[]{:S(2)}) %collective-permute-start) | collective-permute-done | bytes 122912 | tf_op jit(solution)/shard_map/ppermute | solution.py:10
  45.2 0.5 reshape.123
  46.0 0.9 reshape.149
  46.9 4.2 %all-to-all-start = ((bf16[16,2,960]{2,1,0:T(2,128)(2,1)}), bf16[16,2,960]{2,1,0:T(2,128)(2,1)S(1)}, u32[]{:S(2)}, u32[]{:S(2)}) async-start(bf16[16,2,960]{2,1,0:T(2,128)(2,1)} %reshape.149), calls=%async_computation | async-start | bytes 131072 | tf_op jit(solution)/shard_map/all_to_all | solution.py:46
  51.2 7.8 %all-to-all-done = bf16[16,2,960]{2,1,0:T(2,128)(2,1)S(1)} async-done(((bf16[16,2,960]{2,1,0:T(2,128)(2,1)}), bf16[16,2,960]{2,1,0:T(2,128)(2,1)S(1)}, u32[]{:S(2)}, u32[]{:S(2)}) %all-to-all-start) | async-done | bytes 61472 | tf_op jit(solution)/shard_map/all_to_all | solution.py:46
  59.6 17.6 %all_gather.7 = bf16[2,16,40,384]{3,2,0,1:T(8,128)(2,1)S(1)} all-gather(bf16[2,1,40,384]{3,2,0,1:T(8,128)(2,1)S(1)} %fusion.30), channel_id=1, replica_groups=mesh['tm'=32,'rows'=16] {'rows'}, dimensions={1}, use_global_device_ids=true | all-gather | bytes 1044480 | tf_op jit(solution)/shard_map/all_gather | solution.py:48
  77.9 3.5 %fusion.13 = f32[16,16,6,72]{3,1,2,0:T(8,128)S(1)} fusion(bf16[72,3,3,384]{3,0,2,1:T(8,128)(2,1)S(1)} %bitcast.74, bf16[16,2,8,8,384]{4,0,3,2,1:T(8,128)(2,1)S(1)} %fusion.3, pred[16,6]{0,1:T(8,128)(4,1)S(1)} %copy-done.4), kind=kOutput, calls=%fused_computation.12 | convolution fusion | flops 732672000 | bytes 2512992 | tf_op jit(solution)/shard_map/conv_general_dilated | solution.py:23
  83.3 1.9 %collective-permute-start.1 = (f32[2,15360]{1,0:T(2,128)S(1)}, f32[2,15360]{1,0:T(2,128)S(1)}, u32[]{:S(2)}, u32[]{:S(2)}) collective-permute-start(f32[2,15360]{1,0:T(2,128)S(1)} %pad_maximum_fusion.2), channel_id=1, source_target_pairs={{0,16},{16,32},{32,48},{48,64},{64,80},{80,96},{96,112},{112,128},... | collective-permute-start | bytes 368648 | tf_op jit(solution)/shard_map/ppermute | solution.py:10
  85.2 0.8 dynamic_slice.7
  86.0 7.3 %collective-permute-done.1 = f32[2,15360]{1,0:T(2,128)S(1)} collective-permute-done((f32[2,15360]{1,0:T(2,128)S(1)}, f32[2,15360]{1,0:T(2,128)S(1)}, u32[]{:S(2)}, u32[]{:S(2)}) %collective-permute-start.1) | collective-permute-done | bytes 122912 | tf_op jit(solution)/shard_map/ppermute | solution.py:10
  93.3 0.5 reshape.125
  94.2 0.5 reshape.151
  94.8 13.9 %all_to_all.8 = bf16[16,2,1920]{2,1,0:T(2,128)(2,1)S(1)} all-to-all(bf16[16,2,1920]{2,1,0:T(2,128)(2,1)S(1)} %reshape.151), channel_id=1, replica_groups=mesh['tm'=32,'rows'=16] {'rows'}, dimensions={0} | all-to-all | bytes 245760 | tf_op jit(solution)/shard_map/all_to_all | solution.py:53
  108.7 0.6 reshape.152
  109.6 0.5 copy-done
  110.2 0.6 fusion.28
  (52 shorter events, 6.3 us)
Async XLA Ops:
  28.7 1.0 copy-start.1
  28.7 1.1 copy-start.4
  35.2 10.0 %collective-permute-start = (f32[2,15360]{1,0:T(2,128)S(1)}, f32[2,15360]{1,0:T(2,128)S(1)}, u32[]{:S(2)}, u32[]{:S(2)}) collective-permute-start(f32[2,15360]{1,0:T(2,128)S(1)} %pad_maximum_fusion.1), channel_id=1, source_target_pairs={{0,16},{16,32},{32,48},{48,64},{64,80},{80,96},{96,112},{112,128},... | collective-permute-start | bytes 368648 | tf_op jit(solution)/shard_map/ppermute | solution.py:10
  39.1 12.0 %copy-start.2 = (bf16[24,3,3,3,384]{4,0,3,2,1:T(8,128)(2,1)S(1)}, bf16[24,3,3,3,384]{4,0,3,2,1:T(8,128)(2,1)}, u32[]{:S(2)}) copy-start(bf16[24,3,3,3,384]{4,0,3,2,1:T(8,128)(2,1)} %param.12) | copy-start | bytes 1492996
  46.9 12.1 %all-to-all-start = ((bf16[16,2,960]{2,1,0:T(2,128)(2,1)}), bf16[16,2,960]{2,1,0:T(2,128)(2,1)S(1)}, u32[]{:S(2)}, u32[]{:S(2)}) async-start(bf16[16,2,960]{2,1,0:T(2,128)(2,1)} %reshape.149), calls=%async_computation | async-start | bytes 131072 | tf_op jit(solution)/shard_map/all_to_all | solution.py:46
  51.1 8.4 %copy-start.3 = (f32[384]{0:T(512)S(1)}, f32[384]{0:T(512)}, u32[]{:S(2)}) copy-start(f32[384]{0:T(512)} %param.11) | copy-start | bytes 4612
  83.3 10.0 %collective-permute-start.1 = (f32[2,15360]{1,0:T(2,128)S(1)}, f32[2,15360]{1,0:T(2,128)S(1)}, u32[]{:S(2)}, u32[]{:S(2)}) collective-permute-start(f32[2,15360]{1,0:T(2,128)S(1)} %pad_maximum_fusion.2), channel_id=1, source_target_pairs={{0,16},{16,32},{32,48},{48,64},{64,80},{80,96},{96,112},{112,128},... | collective-permute-start | bytes 368648 | tf_op jit(solution)/shard_map/ppermute | solution.py:10
  109.3 0.8 copy-start

commit v9 on v3

--- a/solution.py
+++ b/solution.py
@@ -19,6 +19,7 @@
 
 def causal_conv(own, kernel, bias_part):
     part_width = kernel.shape[0]
+    frames, height, columns, _ = own.shape
     stacked = jnp.transpose(kernel, (1, 0, 2, 3, 4)).reshape(3 * part_width, 3, 3, kernel.shape[4])
     product = lax.conv_general_dilated(
         own,
@@ -29,25 +30,36 @@
         preferred_element_type=jnp.float32,
     )
     tap = [product[..., a * part_width : (a + 1) * part_width] for a in range(3)]
-    onward = jnp.stack([tap[0][0] + tap[1][1], tap[0][1]], 0)
-    kept = jnp.stack([tap[2][0], tap[1][0] + tap[2][1]], 0)
+
+    def rows_first(pair):
+        return jnp.transpose(jnp.stack(pair, 0), (1, 0, 2, 3)).reshape(height, -1)
+
+    onward = rows_first([tap[0][0] + tap[1][1], tap[0][1]])
+    kept = rows_first([tap[2][0], tap[1][0] + tap[2][1]])
     arrived = passed_along(onward, "tm", 1)
-    return kept + arrived + bias_part
+    return kept + arrived + jnp.tile(bias_part, frames * columns)
+
+
+def own_row(laid, frames, columns):
+    sources = lax.all_to_all(laid, "rows", split_axis=0, concat_axis=0, tiled=True)
+    sources = sources.reshape(sources.shape[0], frames, columns, -1)
+    return jnp.transpose(sources, (1, 2, 0, 3)).reshape(frames, 1, columns, -1)
 
 
 def shards(features, gain_one, weight_one, bias_one, gain_two, weight_two, bias_two):
     part_width = weight_one.shape[0]
+    frames, _, columns, _ = features.shape
     offset = lax.axis_index("rows") * part_width
     bias_first = lax.dynamic_slice_in_dim(bias_one, offset, part_width, 0)
     bias_second = lax.dynamic_slice_in_dim(bias_two, offset, part_width, 0)
     normed_one = norm_silu(features, gain_one)
     full_one = lax.all_gather(normed_one, "rows", axis=1, tiled=True)
     conv_one = causal_conv(full_one, weight_one, bias_first).astype(jnp.bfloat16)
-    own_rows = lax.all_to_all(conv_one, "rows", split_axis=1, concat_axis=3, tiled=True)
+    own_rows = own_row(conv_one, frames, columns)
     normed_two = norm_silu(own_rows, gain_two)
     full_two = lax.all_gather(normed_two, "rows", axis=1, tiled=True)
     conv_two = causal_conv(full_two, weight_two, bias_second)
-    returned = lax.all_to_all(conv_two, "rows", split_axis=1, concat_axis=3, tiled=True)
+    returned = own_row(conv_two, frames, columns)
     return (features.astype(jnp.float32) + returned).astype(jnp.bfloat16)
 
 

time: 120 us -> 110 us (0.917)
  waiting for transfers between devices: 32.7 us -> 19.8 us
  local copies, waits for them, and re-layouts: 7.49 us -> 9.58 us
    ppermute x2, waiting for transfers between devices: 25 us -> 12.9 us  [passed_along(): return lax.ppermute(x, axis, pairs)]
    reshape x0 -> x6, local copies, waits for them, and re-layouts: none -> 1.8 us  [the longest x4 1.24 us: rows_first(): return jnp.transpose(jnp.stack(pair, 0), (1, 0, 2, 3)).reshape(height, -1)]
    unnamed x18 -> x14, local copies, waits for them, and re-layouts: 3.39 us -> 1.78 us
  transfers between devices with their start and end apart: 3 -> 3, of which waited for: 3 -> 3; matrix products, arithmetic and copies ran while one was open for 1% -> 3% of each run, Pallas kernels for 0% -> 0%
where the time goes in v9:
time: 110 us
  blocking collectives  58 us (53%)
  waiting for transfers between devices  19.8 us (18%)
  local copies, waits for them, and re-layouts  9.58 us (9%)
  starting transfers between devices  9.43 us (9%)
  matrix products  6.93 us (6%)
  other arithmetic  5.56 us (5%)
    all_gather x1, blocking collectives, shards(): full_one = lax.all_gather(normed_one, 'rows', axis=1, tiled=True)  26.4 us
    all_gather x1, blocking collectives, shards(): full_two = lax.all_gather(normed_two, 'rows', axis=1, tiled=True)  17.6 us
    all_to_all x1, blocking collectives, own_row(): lax.all_to_all(laid, 'rows', split_axis=0, concat_axis=0, tiled=True)  14 us
    ppermute x2, waiting for transfers between devices, passed_along(): return lax.ppermute(x, axis, pairs)  12.9 us
    conv_general_dilated x2, matrix products, causal_conv(): lax.conv_general_dilated(own, stacked, window_strides=(1, 1), padding=((1...  6.93 us
    all_to_all x1, waiting for transfers between devices, own_row(): lax.all_to_all(laid, 'rows', split_axis=0, concat_axis=0, tiled=True)  6.9 us
    ppermute x2, starting transfers between devices, passed_along(): return lax.ppermute(x, axis, pairs)  5.18 us
    all_to_all x1, starting transfers between devices, own_row(): lax.all_to_all(laid, 'rows', split_axis=0, concat_axis=0, tiled=True)  4.25 us
  transfers between devices with their start and end apart: 3, of which 3 were waited for; matrix products, arithmetic and copies ran while one was open for 3% of the time, Pallas kernels for 0%

profile of v9, /device:TPU:33, one launch (start us, length us, event | category | flops | bytes accessed | tf_op | source)
XLA Modules:
  0.0 109.7 jit_solution(5831686985401706546)
XLA Ops:
  0.0 0.9 fusion.16
  0.9 0.9 fusion.27
  1.9 26.4 %all_gather.6 = bf16[2,16,40,384]{3,2,0,1:T(8,128)(2,1)S(1)} all-gather(bf16[2,1,40,384]{3,2,0,1:T(8,128)(2,1)S(1)} %fusion.27), channel_id=1, replica_groups=mesh['tm'=32,'rows'=16] {'rows'}, dimensions={1}, use_global_device_ids=true | all-gather | bytes 1044480 | tf_op jit(solution)/shard_map/all_gather | solution.py:56
  28.9 0.8 copy-done.1
  29.8 3.5 %fusion.10 = f32[16,16,6,72]{3,1,2,0:T(8,128)S(1)} fusion(bf16[72,3,3,384]{3,0,2,1:T(8,128)(2,1)S(1)} %bitcast.73, bf16[16,2,8,8,384]{4,0,3,2,1:T(8,128)(2,1)S(1)} %fusion.2, pred[16,6]{0,1:T(8,128)(4,1)S(1)} %copy-done.4), kind=kOutput, calls=%fused_computation.11 | convolution fusion | flops 732672000 | bytes 2512992 | tf_op jit(solution)/shard_map/conv_general_dilated | solution.py:24
  33.3 0.5 copy.52
  33.8 0.4 slice_add_fusion.2
  34.8 3.3 %collective-permute-start = (f32[16,1920]{1,0:T(8,128)S(1)}, f32[16,1920]{1,0:T(8,128)S(1)}, u32[]{:S(2)}, u32[]{:S(2)}) collective-permute-start(f32[16,1920]{1,0:T(8,128)S(1)} %reshape.123), channel_id=1, source_target_pairs={{0,16},{16,32},{32,48},{48,64},{64,80},{80,96},{96,112},{112,128},... | collective-permute-start | bytes 368648 | tf_op jit(solution)/shard_map/ppermute | solution.py:10
  38.7 0.8 dynamic_slice.6
  39.5 5.5 %collective-permute-done = f32[16,1920]{1,0:T(8,128)S(1)} collective-permute-done((f32[16,1920]{1,0:T(8,128)S(1)}, f32[16,1920]{1,0:T(8,128)S(1)}, u32[]{:S(2)}, u32[]{:S(2)}) %collective-permute-start) | collective-permute-done | bytes 122912 | tf_op jit(solution)/shard_map/ppermute | solution.py:10
  45.0 0.5 broadcast.95
  45.5 0.7 reduce.8
  46.2 0.8 reshape.153
  46.9 4.2 %all-to-all-start = ((bf16[16,2,960]{2,1,0:T(2,128)(2,1)}), bf16[16,2,960]{2,1,0:T(2,128)(2,1)S(1)}, u32[]{:S(2)}, u32[]{:S(2)}) async-start(bf16[16,2,960]{2,1,0:T(2,128)(2,1)} %reshape.153), calls=%async_computation | async-start | bytes 131072 | tf_op jit(solution)/shard_map/all_to_all | solution.py:44
  51.2 0.8 dynamic_slice.7
  52.1 6.9 %all-to-all-done = bf16[16,2,960]{2,1,0:T(2,128)(2,1)S(1)} async-done(((bf16[16,2,960]{2,1,0:T(2,128)(2,1)}), bf16[16,2,960]{2,1,0:T(2,128)(2,1)S(1)}, u32[]{:S(2)}, u32[]{:S(2)}) %all-to-all-start) | async-done | bytes 61472 | tf_op jit(solution)/shard_map/all_to_all | solution.py:44
  60.6 17.6 %all_gather.7 = bf16[2,16,40,384]{3,2,0,1:T(8,128)(2,1)S(1)} all-gather(bf16[2,1,40,384]{3,2,0,1:T(8,128)(2,1)S(1)} %fusion.28), channel_id=1, replica_groups=mesh['tm'=32,'rows'=16] {'rows'}, dimensions={1}, use_global_device_ids=true | all-gather | bytes 1044480 | tf_op jit(solution)/shard_map/all_gather | solution.py:60
  78.9 3.5 %fusion.13 = f32[16,16,6,72]{3,1,2,0:T(8,128)S(1)} fusion(bf16[72,3,3,384]{3,0,2,1:T(8,128)(2,1)S(1)} %bitcast.72, bf16[16,2,8,8,384]{4,0,3,2,1:T(8,128)(2,1)S(1)} %fusion.3, pred[16,6]{0,1:T(8,128)(4,1)S(1)} %copy-done.4), kind=kOutput, calls=%fused_computation.12 | convolution fusion | flops 732672000 | bytes 2512992 | tf_op jit(solution)/shard_map/conv_general_dilated | solution.py:24
  82.4 0.5 copy.62
  82.9 0.4 slice_add_fusion
  83.9 1.9 %collective-permute-start.1 = (f32[16,1920]{1,0:T(8,128)S(1)}, f32[16,1920]{1,0:T(8,128)S(1)}, u32[]{:S(2)}, u32[]{:S(2)}) collective-permute-start(f32[16,1920]{1,0:T(8,128)S(1)} %reshape.126), channel_id=1, source_target_pairs={{0,16},{16,32},{32,48},{48,64},{64,80},{80,96},{96,112},{112,128},... | collective-permute-start | bytes 368648 | tf_op jit(solution)/shard_map/ppermute | solution.py:10
  86.4 7.5 %collective-permute-done.1 = f32[16,1920]{1,0:T(8,128)S(1)} collective-permute-done((f32[16,1920]{1,0:T(8,128)S(1)}, f32[16,1920]{1,0:T(8,128)S(1)}, u32[]{:S(2)}, u32[]{:S(2)}) %collective-permute-start.1) | collective-permute-done | bytes 122912 | tf_op jit(solution)/shard_map/ppermute | solution.py:10
  94.0 14.0 %all_to_all.18 = f32[16,1,1920]{2,1,0:T(1,128)S(1)} all-to-all(f32[16,1,1920]{2,1,0:T(1,128)S(1)} %copy.65), channel_id=1, replica_groups=mesh['tm'=32,'rows'=16] {'rows'}, dimensions={0} | all-to-all | bytes 245760 | tf_op jit(solution)/shard_map/all_to_all | solution.py:44
  109.1 0.6 fusion.24
  (53 shorter events, 6.7 us)
Async XLA Ops:
  28.7 1.0 copy-start.1
  28.7 1.1 copy-start.4
  34.8 16.3 %copy-start.2 = (bf16[24,3,3,3,384]{4,0,3,2,1:T(8,128)(2,1)S(1)}, bf16[24,3,3,3,384]{4,0,3,2,1:T(8,128)(2,1)}, u32[]{:S(2)}) copy-start(bf16[24,3,3,3,384]{4,0,3,2,1:T(8,128)(2,1)} %param.12) | copy-start | bytes 1492996
  34.8 10.1 %collective-permute-start = (f32[16,1920]{1,0:T(8,128)S(1)}, f32[16,1920]{1,0:T(8,128)S(1)}, u32[]{:S(2)}, u32[]{:S(2)}) collective-permute-start(f32[16,1920]{1,0:T(8,128)S(1)} %reshape.123), channel_id=1, source_target_pairs={{0,16},{16,32},{32,48},{48,64},{64,80},{80,96},{96,112},{112,128},... | collective-permute-start | bytes 368648 | tf_op jit(solution)/shard_map/ppermute | solution.py:10
  46.9 12.1 %all-to-all-start = ((bf16[16,2,960]{2,1,0:T(2,128)(2,1)}), bf16[16,2,960]{2,1,0:T(2,128)(2,1)S(1)}, u32[]{:S(2)}, u32[]{:S(2)}) async-start(bf16[16,2,960]{2,1,0:T(2,128)(2,1)} %reshape.153), calls=%async_computation | async-start | bytes 131072 | tf_op jit(solution)/shard_map/all_to_all | solution.py:44
  51.2 9.3 %copy-start.3 = (f32[384]{0:T(512)S(1)}, f32[384]{0:T(512)}, u32[]{:S(2)}) copy-start(f32[384]{0:T(512)} %param.11) | copy-start | bytes 4612
  83.9 10.0 %collective-permute-start.1 = (f32[16,1920]{1,0:T(8,128)S(1)}, f32[16,1920]{1,0:T(8,128)S(1)}, u32[]{:S(2)}, u32[]{:S(2)}) collective-permute-start(f32[16,1920]{1,0:T(8,128)S(1)} %reshape.126), channel_id=1, source_target_pairs={{0,16},{16,32},{32,48},{48,64},{64,80},{80,96},{96,112},{112,128},... | collective-permute-start | bytes 368648 | tf_op jit(solution)/shard_map/ppermute | solution.py:10
  93.9 15.2 %copy-start = (bf16[2,1,40,384]{3,2,1,0:T(8,128)(2,1)S(1)}, bf16[2,1,40,384]{3,2,1,0:T(8,128)(2,1)}, u32[]{:S(2)}) copy-start(bf16[2,1,40,384]{3,2,1,0:T(8,128)(2,1)} %param.7) | copy-start | bytes 184324

commit v10 on v9

--- a/solution.py
+++ b/solution.py
@@ -20,16 +20,23 @@
 def causal_conv(own, kernel, bias_part):
     part_width = kernel.shape[0]
     frames, height, columns, _ = own.shape
-    stacked = jnp.transpose(kernel, (1, 0, 2, 3, 4)).reshape(3 * part_width, 3, 3, kernel.shape[4])
+    stacked = jnp.transpose(kernel, (1, 2, 0, 3, 4)).reshape(9 * part_width, 1, 3, kernel.shape[4])
     product = lax.conv_general_dilated(
         own,
         stacked,
         window_strides=(1, 1),
-        padding=((1, 1), (1, 1)),
+        padding=((0, 0), (1, 1)),
         dimension_numbers=("NHWC", "OHWI", "NHWC"),
         preferred_element_type=jnp.float32,
     )
-    tap = [product[..., a * part_width : (a + 1) * part_width] for a in range(3)]
+    padded = jnp.pad(product, ((0, 0), (1, 1), (0, 0), (0, 0)))
+    tap = []
+    for a in range(3):
+        summed = 0
+        for b in range(3):
+            at = (a * 3 + b) * part_width
+            summed = summed + padded[:, b : b + height, :, at : at + part_width]
+        tap.append(summed)
 
     def rows_first(pair):
         return jnp.transpose(jnp.stack(pair, 0), (1, 0, 2, 3)).reshape(height, -1)

time: 110 us -> 113 us (1.027)
  other arithmetic: 5.56 us -> 8.25 us
  matrix products: 6.93 us -> 4.53 us
  local copies, waits for them, and re-layouts: 9.58 us -> 11.6 us
    add x0 -> x2, other arithmetic: none -> 3.24 us  [causal_conv(): summed = summed + padded[:, b:b + height, :, at:at + part_width]]
    add x0 -> x12, local copies, waits for them, and re-layouts: none -> 3.03 us  [causal_conv(): summed = summed + padded[:, b:b + height, :, at:at + part_width]]
    conv_general_dilated x2, matrix products: 6.93 us -> 4.53 us  [causal_conv(): lax.conv_general_dilated(own, stacked, window_strides=(1, 1), padding=((0...]
where the time goes in v10:
time: 113 us; the launch traced here: 112 us
  blocking collectives  58 us (51%)
  waiting for transfers between devices  19.8 us (18%)
  local copies, waits for them, and re-layouts  11.6 us (10%)
  starting transfers between devices  9.42 us (8%)
  other arithmetic  8.25 us (7%)
  matrix products  4.53 us (4%)
    all_gather x1, blocking collectives, shards(): full_one = lax.all_gather(normed_one, 'rows', axis=1, tiled=True)  26.4 us
    all_gather x1, blocking collectives, shards(): full_two = lax.all_gather(normed_two, 'rows', axis=1, tiled=True)  17.6 us
    all_to_all x1, blocking collectives, own_row(): lax.all_to_all(laid, 'rows', split_axis=0, concat_axis=0, tiled=True)  13.9 us
    ppermute x2, waiting for transfers between devices, passed_along(): return lax.ppermute(x, axis, pairs)  12.9 us
    all_to_all x1, waiting for transfers between devices, own_row(): lax.all_to_all(laid, 'rows', split_axis=0, concat_axis=0, tiled=True)  6.9 us
    ppermute x2, starting transfers between devices, passed_along(): return lax.ppermute(x, axis, pairs)  5.17 us
    conv_general_dilated x2, matrix products, causal_conv(): lax.conv_general_dilated(own, stacked, window_strides=(1, 1), padding=((0...  4.53 us
    all_to_all x1, starting transfers between devices, own_row(): lax.all_to_all(laid, 'rows', split_axis=0, concat_axis=0, tiled=True)  4.24 us
  transfers between devices with their start and end apart: 3, of which 3 were waited for; matrix products, arithmetic and copies ran while one was open for 3% of the time, Pallas kernels for 0%

profile of v10, /device:TPU:33, one launch (start us, length us, event | category | flops | bytes accessed | tf_op | source)
XLA Modules:
  0.0 112.1 jit_solution(17153708330535037837)
XLA Ops:
  0.0 0.9 fusion.28
  0.9 0.9 fusion.39
  1.9 26.4 %all_gather.6 = bf16[2,16,40,384]{3,2,0,1:T(8,128)(2,1)S(1)} all-gather(bf16[2,1,40,384]{3,2,0,1:T(8,128)(2,1)S(1)} %fusion.39), channel_id=1, replica_groups=mesh['tm'=32,'rows'=16] {'rows'}, dimensions={1}, use_global_device_ids=true | all-gather | bytes 1044480 | tf_op jit(solution)/shard_map/all_gather | solution.py:63
  28.9 0.8 copy-done.1
  29.8 2.3 %fusion.10 = f32[16,16,6,216]{3,1,2,0:T(8,128)S(1)} fusion(bf16[216,1,3,384]{3,0,2,1:T(8,128)(2,1)S(1)} %bitcast.89, bf16[16,2,8,8,384]{4,0,3,2,1:T(8,128)(2,1)S(1)} %fusion.2, pred[16,6]{0,1:T(8,128)(4,1)S(1)} %copy-done.4), kind=kOutput, calls=%fused_computation.23 | convolution fusion | flops 764743680 | bytes 3397728 | tf_op jit(solution)/shard_map/conv_general_dilated | solution.py:24
  32.1 1.6 %fusion.21 = (f32[16,16,6,24]{3,1,2,0:T(8,128)S(1)}, f32[16,16,6,24]{3,1,2,0:T(8,128)S(1)}, f32[16,16,6,24]{3,1,2,0:T(8,128)S(1)}) fusion(f32[16,16,6,216]{3,1,2,0:T(8,128)S(1)} %fusion.10), kind=kLoop, calls=%fused_computation.32 | loop fusion | flops 221184 | bytes 4374528 | tf_op jit(solution)/shard_map/add | solution.py:38
  33.7 0.5 copy.63
  36.0 3.3 %collective-permute-start = (f32[16,1920]{1,0:T(8,128)S(1)}, f32[16,1920]{1,0:T(8,128)S(1)}, u32[]{:S(2)}, u32[]{:S(2)}) collective-permute-start(f32[16,1920]{1,0:T(8,128)S(1)} %reshape.123), channel_id=1, source_target_pairs={{0,16},{16,32},{32,48},{48,64},{64,80},{80,96},{96,112},{112,128},... | collective-permute-start | bytes 368648 | tf_op jit(solution)/shard_map/ppermute | solution.py:10
  39.8 0.8 dynamic_slice.6
  40.7 5.5 %collective-permute-done = f32[16,1920]{1,0:T(8,128)S(1)} collective-permute-done((f32[16,1920]{1,0:T(8,128)S(1)}, f32[16,1920]{1,0:T(8,128)S(1)}, u32[]{:S(2)}, u32[]{:S(2)}) %collective-permute-start) | collective-permute-done | bytes 122912 | tf_op jit(solution)/shard_map/ppermute | solution.py:10
  46.2 0.5 broadcast.99
  46.7 0.7 reduce.8
  47.4 0.8 reshape.165
  48.1 4.2 %all-to-all-start = ((bf16[16,2,960]{2,1,0:T(2,128)(2,1)}), bf16[16,2,960]{2,1,0:T(2,128)(2,1)S(1)}, u32[]{:S(2)}, u32[]{:S(2)}) async-start(bf16[16,2,960]{2,1,0:T(2,128)(2,1)} %reshape.165), calls=%async_computation | async-start | bytes 131072 | tf_op jit(solution)/shard_map/all_to_all | solution.py:51
  52.4 0.8 dynamic_slice.7
  53.3 6.9 %all-to-all-done = bf16[16,2,960]{2,1,0:T(2,128)(2,1)S(1)} async-done(((bf16[16,2,960]{2,1,0:T(2,128)(2,1)}), bf16[16,2,960]{2,1,0:T(2,128)(2,1)S(1)}, u32[]{:S(2)}, u32[]{:S(2)}) %all-to-all-start) | async-done | bytes 61472 | tf_op jit(solution)/shard_map/all_to_all | solution.py:51
  61.8 17.6 %all_gather.7 = bf16[2,16,40,384]{3,2,0,1:T(8,128)(2,1)S(1)} all-gather(bf16[2,1,40,384]{3,2,0,1:T(8,128)(2,1)S(1)} %fusion.40), channel_id=1, replica_groups=mesh['tm'=32,'rows'=16] {'rows'}, dimensions={1}, use_global_device_ids=true | all-gather | bytes 1044480 | tf_op jit(solution)/shard_map/all_gather | solution.py:67
  80.1 2.3 %fusion.13 = f32[16,16,6,216]{3,1,2,0:T(8,128)S(1)} fusion(bf16[216,1,3,384]{3,0,2,1:T(8,128)(2,1)S(1)} %bitcast.88, bf16[16,2,8,8,384]{4,0,3,2,1:T(8,128)(2,1)S(1)} %fusion.3, pred[16,6]{0,1:T(8,128)(4,1)S(1)} %copy-done.4), kind=kOutput, calls=%fused_computation.24 | convolution fusion | flops 764743680 | bytes 3397728 | tf_op jit(solution)/shard_map/conv_general_dilated | solution.py:24
  82.4 1.6 %fusion.27 = (f32[16,16,6,24]{3,1,2,0:T(8,128)S(1)}, f32[16,16,6,24]{3,1,2,0:T(8,128)S(1)}, f32[16,16,6,24]{3,1,2,0:T(8,128)S(1)}) fusion(f32[16,16,6,216]{3,1,2,0:T(8,128)S(1)} %fusion.13), kind=kLoop, calls=%fused_computation.38 | loop fusion | flops 221184 | bytes 4374528 | tf_op jit(solution)/shard_map/add | solution.py:38
  84.0 0.5 copy.75
  86.3 1.9 %collective-permute-start.1 = (f32[16,1920]{1,0:T(8,128)S(1)}, f32[16,1920]{1,0:T(8,128)S(1)}, u32[]{:S(2)}, u32[]{:S(2)}) collective-permute-start(f32[16,1920]{1,0:T(8,128)S(1)} %reshape.126), channel_id=1, source_target_pairs={{0,16},{16,32},{32,48},{48,64},{64,80},{80,96},{96,112},{112,128},... | collective-permute-start | bytes 368648 | tf_op jit(solution)/shard_map/ppermute | solution.py:10
  88.8 7.5 %collective-permute-done.1 = f32[16,1920]{1,0:T(8,128)S(1)} collective-permute-done((f32[16,1920]{1,0:T(8,128)S(1)}, f32[16,1920]{1,0:T(8,128)S(1)}, u32[]{:S(2)}, u32[]{:S(2)}) %collective-permute-start.1) | collective-permute-done | bytes 122912 | tf_op jit(solution)/shard_map/ppermute | solution.py:10
  96.4 13.9 %all_to_all.18 = f32[16,1,1920]{2,1,0:T(1,128)S(1)} all-to-all(f32[16,1,1920]{2,1,0:T(1,128)S(1)} %copy.77), channel_id=1, replica_groups=mesh['tm'=32,'rows'=16] {'rows'}, dimensions={0} | all-to-all | bytes 245760 | tf_op jit(solution)/shard_map/all_to_all | solution.py:51
  111.4 0.6 fusion.36
  (63 shorter events, 9.0 us)
Async XLA Ops:
  28.7 1.0 copy-start.1
  28.7 1.1 copy-start.4
  36.0 16.3 %copy-start.2 = (bf16[24,3,3,3,384]{4,0,3,2,1:T(8,128)(2,1)S(1)}, bf16[24,3,3,3,384]{4,0,3,2,1:T(8,128)(2,1)}, u32[]{:S(2)}) copy-start(bf16[24,3,3,3,384]{4,0,3,2,1:T(8,128)(2,1)} %param.12) | copy-start | bytes 1492996
  36.0 10.1 %collective-permute-start = (f32[16,1920]{1,0:T(8,128)S(1)}, f32[16,1920]{1,0:T(8,128)S(1)}, u32[]{:S(2)}, u32[]{:S(2)}) collective-permute-start(f32[16,1920]{1,0:T(8,128)S(1)} %reshape.123), channel_id=1, source_target_pairs={{0,16},{16,32},{32,48},{48,64},{64,80},{80,96},{96,112},{112,128},... | collective-permute-start | bytes 368648 | tf_op jit(solution)/shard_map/ppermute | solution.py:10
  48.1 12.1 %all-to-all-start = ((bf16[16,2,960]{2,1,0:T(2,128)(2,1)}), bf16[16,2,960]{2,1,0:T(2,128)(2,1)S(1)}, u32[]{:S(2)}, u32[]{:S(2)}) async-start(bf16[16,2,960]{2,1,0:T(2,128)(2,1)} %reshape.165), calls=%async_computation | async-start | bytes 131072 | tf_op jit(solution)/shard_map/all_to_all | solution.py:51
  52.4 9.3 %copy-start.3 = (f32[384]{0:T(512)S(1)}, f32[384]{0:T(512)}, u32[]{:S(2)}) copy-start(f32[384]{0:T(512)} %param.11) | copy-start | bytes 4612
  86.3 10.0 %collective-permute-start.1 = (f32[16,1920]{1,0:T(8,128)S(1)}, f32[16,1920]{1,0:T(8,128)S(1)}, u32[]{:S(2)}, u32[]{:S(2)}) collective-permute-start(f32[16,1920]{1,0:T(8,128)S(1)} %reshape.126), channel_id=1, source_target_pairs={{0,16},{16,32},{32,48},{48,64},{64,80},{80,96},{96,112},{112,128},... | collective-permute-start | bytes 368648 | tf_op jit(solution)/shard_map/ppermute | solution.py:10
  96.3 15.2 %copy-start = (bf16[2,1,40,384]{3,2,1,0:T(8,128)(2,1)S(1)}, bf16[2,1,40,384]{3,2,1,0:T(8,128)(2,1)}, u32[]{:S(2)}) copy-start(bf16[2,1,40,384]{3,2,1,0:T(8,128)(2,1)} %param.7) | copy-start | bytes 184324

commit v11 on v9

--- a/solution.py
+++ b/solution.py
@@ -52,8 +52,7 @@
     offset = lax.axis_index("rows") * part_width
     bias_first = lax.dynamic_slice_in_dim(bias_one, offset, part_width, 0)
     bias_second = lax.dynamic_slice_in_dim(bias_two, offset, part_width, 0)
-    normed_one = norm_silu(features, gain_one)
-    full_one = lax.all_gather(normed_one, "rows", axis=1, tiled=True)
+    full_one = norm_silu(lax.all_gather(features, "rows", axis=1, tiled=True), gain_one)
     conv_one = causal_conv(full_one, weight_one, bias_first).astype(jnp.bfloat16)
     own_rows = own_row(conv_one, frames, columns)
     normed_two = norm_silu(own_rows, gain_two)

time: 110 us -> 109 us (level)
  no operation moved by 1% of the time
where the time goes in v11:
time: 109 us
  blocking collectives  58.4 us (54%)
  waiting for transfers between devices  19.8 us (18%)
  starting transfers between devices  9.43 us (9%)
  local copies, waits for them, and re-layouts  9.38 us (9%)
  matrix products  6.93 us (6%)
  other arithmetic  4.65 us (4%)
    all_gather x1, blocking collectives, shards(): lax.all_gather(features, 'rows', axis=1, tiled=True)  26.8 us
    all_gather x1, blocking collectives, shards(): full_two = lax.all_gather(normed_two, 'rows', axis=1, tiled=True)  17.6 us
    all_to_all x1, blocking collectives, own_row(): lax.all_to_all(laid, 'rows', split_axis=0, concat_axis=0, tiled=True)  14 us
    ppermute x2, waiting for transfers between devices, passed_along(): return lax.ppermute(x, axis, pairs)  12.9 us
    conv_general_dilated x2, matrix products, causal_conv(): lax.conv_general_dilated(own, stacked, window_strides=(1, 1), padding=((1...  6.93 us
    all_to_all x1, waiting for transfers between devices, own_row(): lax.all_to_all(laid, 'rows', split_axis=0, concat_axis=0, tiled=True)  6.9 us
    ppermute x2, starting transfers between devices, passed_along(): return lax.ppermute(x, axis, pairs)  5.18 us
    all_to_all x1, starting transfers between devices, own_row(): lax.all_to_all(laid, 'rows', split_axis=0, concat_axis=0, tiled=True)  4.25 us
  transfers between devices with their start and end apart: 3, of which 3 were waited for; matrix products, arithmetic and copies ran while one was open for 3% of the time, Pallas kernels for 0%

profile of v11, /device:TPU:33, one launch (start us, length us, event | category | flops | bytes accessed | tf_op | source)
XLA Modules:
  0.0 109.0 jit_solution(10529067866014810498)
XLA Ops:
  0.0 26.8 %all_gather.6 = bf16[2,16,40,384]{3,2,0,1:T(8,128)(2,1)S(1)} all-gather(bf16[2,1,40,384]{3,2,0,1:T(8,128)(2,1)} %bitcast.71), channel_id=1, replica_groups=mesh['tm'=32,'rows'=16] {'rows'}, dimensions={1}, use_global_device_ids=true | all-gather | bytes 1044480 | tf_op jit(solution)/shard_map/all_gather | solution.py:55
  27.1 0.7 fusion.24
  28.2 0.8 copy-done
  29.0 3.5 %fusion.18 = f32[16,16,6,72]{3,1,2,0:T(8,128)S(1)} fusion(bf16[72,3,3,384]{3,0,2,1:T(8,128)(2,1)S(1)} %bitcast.70, bf16[16,2,8,8,384]{4,0,3,2,1:T(8,128)(2,1)S(1)} %fusion.10, pred[16,6]{0,1:T(8,128)(4,1)S(1)} %copy-done.5), kind=kOutput, calls=%fused_computation.21 | convolution fusion | flops 732672000 | bytes 2512992 | tf_op jit(solution)/shard_map/conv_general_dilated | solution.py:24
  32.5 0.5 copy.50
  33.0 0.4 slice_add_fusion.2
  34.1 3.3 %collective-permute-start = (f32[16,1920]{1,0:T(8,128)S(1)}, f32[16,1920]{1,0:T(8,128)S(1)}, u32[]{:S(2)}, u32[]{:S(2)}) collective-permute-start(f32[16,1920]{1,0:T(8,128)S(1)} %reshape.116), channel_id=1, source_target_pairs={{0,16},{16,32},{32,48},{48,64},{64,80},{80,96},{96,112},{112,128},... | collective-permute-start | bytes 368648 | tf_op jit(solution)/shard_map/ppermute | solution.py:10
  37.9 0.8 dynamic_slice.6
  38.8 5.5 %collective-permute-done = f32[16,1920]{1,0:T(8,128)S(1)} collective-permute-done((f32[16,1920]{1,0:T(8,128)S(1)}, f32[16,1920]{1,0:T(8,128)S(1)}, u32[]{:S(2)}, u32[]{:S(2)}) %collective-permute-start) | collective-permute-done | bytes 122912 | tf_op jit(solution)/shard_map/ppermute | solution.py:10
  44.2 0.5 broadcast.82
  44.8 0.7 reduce.7
  45.4 0.8 reshape.146
  46.2 4.2 %all-to-all-start = ((bf16[16,2,960]{2,1,0:T(2,128)(2,1)}), bf16[16,2,960]{2,1,0:T(2,128)(2,1)S(1)}, u32[]{:S(2)}, u32[]{:S(2)}) async-start(bf16[16,2,960]{2,1,0:T(2,128)(2,1)} %reshape.146), calls=%async_computation | async-start | bytes 131072 | tf_op jit(solution)/shard_map/all_to_all | solution.py:44
  50.5 0.8 dynamic_slice.7
  51.4 6.9 %all-to-all-done = bf16[16,2,960]{2,1,0:T(2,128)(2,1)S(1)} async-done(((bf16[16,2,960]{2,1,0:T(2,128)(2,1)}), bf16[16,2,960]{2,1,0:T(2,128)(2,1)S(1)}, u32[]{:S(2)}, u32[]{:S(2)}) %all-to-all-start) | async-done | bytes 61472 | tf_op jit(solution)/shard_map/all_to_all | solution.py:44
  58.8 0.4 reshape.143
  59.9 17.6 %all_gather.7 = bf16[2,16,40,384]{3,2,0,1:T(8,128)(2,1)S(1)} all-gather(bf16[2,1,40,384]{3,2,0,1:T(8,128)(2,1)S(1)} %fusion.27), channel_id=1, replica_groups=mesh['tm'=32,'rows'=16] {'rows'}, dimensions={1}, use_global_device_ids=true | all-gather | bytes 1044480 | tf_op jit(solution)/shard_map/all_gather | solution.py:59
  78.2 3.5 %fusion.21 = f32[16,16,6,72]{3,1,2,0:T(8,128)S(1)} fusion(bf16[72,3,3,384]{3,0,2,1:T(8,128)(2,1)S(1)} %bitcast.69, bf16[16,2,8,8,384]{4,0,3,2,1:T(8,128)(2,1)S(1)} %fusion.11, pred[16,6]{0,1:T(8,128)(4,1)S(1)} %copy-done.5), kind=kOutput, calls=%fused_computation.22 | convolution fusion | flops 732672000 | bytes 2512992 | tf_op jit(solution)/shard_map/conv_general_dilated | solution.py:24
  81.6 0.5 copy.60
  82.1 0.4 slice_add_fusion
  83.1 1.9 %collective-permute-start.1 = (f32[16,1920]{1,0:T(8,128)S(1)}, f32[16,1920]{1,0:T(8,128)S(1)}, u32[]{:S(2)}, u32[]{:S(2)}) collective-permute-start(f32[16,1920]{1,0:T(8,128)S(1)} %reshape.119), channel_id=1, source_target_pairs={{0,16},{16,32},{32,48},{48,64},{64,80},{80,96},{96,112},{112,128},... | collective-permute-start | bytes 368648 | tf_op jit(solution)/shard_map/ppermute | solution.py:10
  85.6 7.5 %collective-permute-done.1 = f32[16,1920]{1,0:T(8,128)S(1)} collective-permute-done((f32[16,1920]{1,0:T(8,128)S(1)}, f32[16,1920]{1,0:T(8,128)S(1)}, u32[]{:S(2)}, u32[]{:S(2)}) %collective-permute-start.1) | collective-permute-done | bytes 122912 | tf_op jit(solution)/shard_map/ppermute | solution.py:10
  93.3 14.0 %all_to_all.18 = f32[16,1,1920]{2,1,0:T(1,128)S(1)} all-to-all(f32[16,1,1920]{2,1,0:T(1,128)S(1)} %copy.63), channel_id=1, replica_groups=mesh['tm'=32,'rows'=16] {'rows'}, dimensions={0} | all-to-all | bytes 245760 | tf_op jit(solution)/shard_map/all_to_all | solution.py:44
  108.3 0.6 add_convert_fusion
  (54 shorter events, 6.4 us)
Async XLA Ops:
  0.0 27.1 %copy-start.3 = (f32[384]{0:T(512)S(1)}, f32[384]{0:T(512)}, u32[]{:S(2)}) copy-start(f32[384]{0:T(512)} %param.8) | copy-start | bytes 4612
  27.9 1.0 copy-start
  28.0 1.1 copy-start.5
  34.1 16.3 %copy-start.1 = (bf16[24,3,3,3,384]{4,0,3,2,1:T(8,128)(2,1)S(1)}, bf16[24,3,3,3,384]{4,0,3,2,1:T(8,128)(2,1)}, u32[]{:S(2)}) copy-start(bf16[24,3,3,3,384]{4,0,3,2,1:T(8,128)(2,1)} %param.12) | copy-start | bytes 1492996
  34.1 10.1 %collective-permute-start = (f32[16,1920]{1,0:T(8,128)S(1)}, f32[16,1920]{1,0:T(8,128)S(1)}, u32[]{:S(2)}, u32[]{:S(2)}) collective-permute-start(f32[16,1920]{1,0:T(8,128)S(1)} %reshape.116), channel_id=1, source_target_pairs={{0,16},{16,32},{32,48},{48,64},{64,80},{80,96},{96,112},{112,128},... | collective-permute-start | bytes 368648 | tf_op jit(solution)/shard_map/ppermute | solution.py:10
  46.2 12.1 %all-to-all-start = ((bf16[16,2,960]{2,1,0:T(2,128)(2,1)}), bf16[16,2,960]{2,1,0:T(2,128)(2,1)S(1)}, u32[]{:S(2)}, u32[]{:S(2)}) async-start(bf16[16,2,960]{2,1,0:T(2,128)(2,1)} %reshape.146), calls=%async_computation | async-start | bytes 131072 | tf_op jit(solution)/shard_map/all_to_all | solution.py:44
  50.5 9.3 %copy-start.4 = (f32[384]{0:T(512)S(1)}, f32[384]{0:T(512)}, u32[]{:S(2)}) copy-start(f32[384]{0:T(512)} %param.11) | copy-start | bytes 4612
  83.1 10.0 %collective-permute-start.1 = (f32[16,1920]{1,0:T(8,128)S(1)}, f32[16,1920]{1,0:T(8,128)S(1)}, u32[]{:S(2)}, u32[]{:S(2)}) collective-permute-start(f32[16,1920]{1,0:T(8,128)S(1)} %reshape.119), channel_id=1, source_target_pairs={{0,16},{16,32},{32,48},{48,64},{64,80},{80,96},{96,112},{112,128},... | collective-permute-start | bytes 368648 | tf_op jit(solution)/shard_map/ppermute | solution.py:10
  93.1 15.2 %copy-start.2 = (bf16[2,1,40,384]{3,2,1,0:T(8,128)(2,1)S(1)}, bf16[2,1,40,384]{3,2,1,0:T(8,128)(2,1)}, u32[]{:S(2)}) copy-start(bf16[2,1,40,384]{3,2,1,0:T(8,128)(2,1)} %param.7) | copy-start | bytes 184324

commit v12 on v11

--- a/solution.py
+++ b/solution.py
@@ -52,14 +52,17 @@
     offset = lax.axis_index("rows") * part_width
     bias_first = lax.dynamic_slice_in_dim(bias_one, offset, part_width, 0)
     bias_second = lax.dynamic_slice_in_dim(bias_two, offset, part_width, 0)
-    full_one = norm_silu(lax.all_gather(features, "rows", axis=1, tiled=True), gain_one)
+    every_row = lax.all_gather(features, "rows", axis=1, tiled=True)
+    full_one = norm_silu(every_row, gain_one)
+    residual = lax.dynamic_slice_in_dim(every_row, offset, part_width, 3)
+    residual = jnp.transpose(residual, (1, 0, 2, 3)).reshape(residual.shape[1], -1)
     conv_one = causal_conv(full_one, weight_one, bias_first).astype(jnp.bfloat16)
     own_rows = own_row(conv_one, frames, columns)
     normed_two = norm_silu(own_rows, gain_two)
     full_two = lax.all_gather(normed_two, "rows", axis=1, tiled=True)
     conv_two = causal_conv(full_two, weight_two, bias_second)
-    returned = own_row(conv_two, frames, columns)
-    return (features.astype(jnp.float32) + returned).astype(jnp.bfloat16)
+    block_out = (residual.astype(jnp.float32) + conv_two).astype(jnp.bfloat16)
+    return own_row(block_out, frames, columns)
 
 
 def solution(mesh):

time: 109 us -> 109 us (level)
  blocking collectives: 58.4 us -> 57.2 us
    all_to_all x1, blocking collectives: 14 us -> 12.7 us  [own_row(): lax.all_to_all(laid, 'rows', split_axis=0, concat_axis=0, tiled=True)]
where the time goes in v12:
time: 109 us; the launch traced here: 108 us
  blocking collectives  57.2 us (52%)
  waiting for transfers between devices  19.3 us (18%)
  local copies, waits for them, and re-layouts  10.4 us (10%)
  starting transfers between devices  9.29 us (9%)
  matrix products  6.96 us (6%)
  other arithmetic  4.9 us (4%)
    all_gather x1, blocking collectives, shards(): every_row = lax.all_gather(features, 'rows', axis=1, tiled=True)  26.8 us
    all_gather x1, blocking collectives, shards(): full_two = lax.all_gather(normed_two, 'rows', axis=1, tiled=True)  17.6 us
    ppermute x2, waiting for transfers between devices, passed_along(): return lax.ppermute(x, axis, pairs)  12.8 us
    all_to_all x1, blocking collectives, own_row(): lax.all_to_all(laid, 'rows', split_axis=0, concat_axis=0, tiled=True)  12.7 us
    conv_general_dilated x2, matrix products, causal_conv(): lax.conv_general_dilated(own, stacked, window_strides=(1, 1), padding=((1...  6.96 us
    all_to_all x1, waiting for transfers between devices, own_row(): lax.all_to_all(laid, 'rows', split_axis=0, concat_axis=0, tiled=True)  6.49 us
    ppermute x2, starting transfers between devices, passed_along(): return lax.ppermute(x, axis, pairs)  5.04 us
    all_to_all x1, starting transfers between devices, own_row(): lax.all_to_all(laid, 'rows', split_axis=0, concat_axis=0, tiled=True)  4.25 us
  transfers between devices with their start and end apart: 3, of which 3 were waited for; matrix products, arithmetic and copies ran while one was open for 3% of the time, Pallas kernels for 0%

profile of v12, /device:TPU:33, one launch (start us, length us, event | category | flops | bytes accessed | tf_op | source)
XLA Modules:
  0.0 108.4 jit_solution(544741570580881418)
XLA Ops:
  0.0 26.8 %all_gather.6 = bf16[2,16,40,384]{3,2,0,1:T(8,128)(2,1)S(1)} all-gather(bf16[2,1,40,384]{3,2,0,1:T(8,128)(2,1)} %bitcast.75), channel_id=1, replica_groups=mesh['tm'=32,'rows'=16] {'rows'}, dimensions={1}, use_global_device_ids=true | all-gather | bytes 1044480 | tf_op jit(solution)/shard_map/all_gather | solution.py:55
  27.1 0.7 fusion.24
  28.2 0.8 copy-done
  29.0 3.5 %fusion.18 = f32[16,16,6,72]{3,1,2,0:T(8,128)S(1)} fusion(bf16[72,3,3,384]{3,0,2,1:T(8,128)(2,1)S(1)} %bitcast.74, bf16[16,2,8,8,384]{4,0,3,2,1:T(8,128)(2,1)S(1)} %fusion.10, pred[16,6]{0,1:T(8,128)(4,1)S(1)} %copy-done.4), kind=kOutput, calls=%fused_computation.21 | convolution fusion | flops 732672000 | bytes 2512992 | tf_op jit(solution)/shard_map/conv_general_dilated | solution.py:24
  32.5 0.5 copy.49
  33.0 0.4 slice_add_fusion.2
  34.1 3.1 %collective-permute-start = (f32[16,1920]{1,0:T(8,128)S(1)}, f32[16,1920]{1,0:T(8,128)S(1)}, u32[]{:S(2)}, u32[]{:S(2)}) collective-permute-start(f32[16,1920]{1,0:T(8,128)S(1)} %reshape.119), channel_id=1, source_target_pairs={{0,16},{16,32},{32,48},{48,64},{64,80},{80,96},{96,112},{112,128},... | collective-permute-start | bytes 368648 | tf_op jit(solution)/shard_map/ppermute | solution.py:10
  37.8 0.8 dynamic_slice.10
  38.7 5.4 %collective-permute-done = f32[16,1920]{1,0:T(8,128)S(1)} collective-permute-done((f32[16,1920]{1,0:T(8,128)S(1)}, f32[16,1920]{1,0:T(8,128)S(1)}, u32[]{:S(2)}, u32[]{:S(2)}) %collective-permute-start) | collective-permute-done | bytes 122912 | tf_op jit(solution)/shard_map/ppermute | solution.py:10
  44.1 0.5 broadcast.82
  44.6 0.7 reduce.7
  45.3 0.8 reshape.150
  46.0 4.2 %all-to-all-start = ((bf16[16,2,960]{2,1,0:T(2,128)(2,1)}), bf16[16,2,960]{2,1,0:T(2,128)(2,1)S(1)}, u32[]{:S(2)}, u32[]{:S(2)}) async-start(bf16[16,2,960]{2,1,0:T(2,128)(2,1)} %reshape.150), calls=%async_computation | async-start | bytes 131072 | tf_op jit(solution)/shard_map/all_to_all | solution.py:44
  50.8 0.8 dynamic_slice.11
  51.6 6.5 %all-to-all-done = bf16[16,2,960]{2,1,0:T(2,128)(2,1)S(1)} async-done(((bf16[16,2,960]{2,1,0:T(2,128)(2,1)}), bf16[16,2,960]{2,1,0:T(2,128)(2,1)S(1)}, u32[]{:S(2)}, u32[]{:S(2)}) %all-to-all-start) | async-done | bytes 61472 | tf_op jit(solution)/shard_map/all_to_all | solution.py:44
  59.8 17.6 %all_gather.7 = bf16[2,16,40,384]{3,2,0,1:T(8,128)(2,1)S(1)} all-gather(bf16[2,1,40,384]{3,2,0,1:T(8,128)(2,1)S(1)} %fusion.28), channel_id=1, replica_groups=mesh['tm'=32,'rows'=16] {'rows'}, dimensions={1}, use_global_device_ids=true | all-gather | bytes 1044480 | tf_op jit(solution)/shard_map/all_gather | solution.py:62
  78.0 3.5 %fusion.21 = f32[16,16,6,72]{3,1,2,0:T(8,128)S(1)} fusion(bf16[72,3,3,384]{3,0,2,1:T(8,128)(2,1)S(1)} %bitcast.73, bf16[16,2,8,8,384]{4,0,3,2,1:T(8,128)(2,1)S(1)} %fusion.11, pred[16,6]{0,1:T(8,128)(4,1)S(1)} %copy-done.4), kind=kOutput, calls=%fused_computation.22 | convolution fusion | flops 732672000 | bytes 2512992 | tf_op jit(solution)/shard_map/conv_general_dilated | solution.py:24
  81.5 0.5 copy.59
  83.0 1.9 %collective-permute-start.1 = (f32[16,1920]{1,0:T(8,128)S(1)}, f32[16,1920]{1,0:T(8,128)S(1)}, u32[]{:S(2)}, u32[]{:S(2)}) collective-permute-start(f32[16,1920]{1,0:T(8,128)S(1)} %reshape.122), channel_id=1, source_target_pairs={{0,16},{16,32},{32,48},{48,64},{64,80},{80,96},{96,112},{112,128},... | collective-permute-start | bytes 368648 | tf_op jit(solution)/shard_map/ppermute | solution.py:10
  85.5 7.5 %collective-permute-done.1 = f32[16,1920]{1,0:T(8,128)S(1)} collective-permute-done((f32[16,1920]{1,0:T(8,128)S(1)}, f32[16,1920]{1,0:T(8,128)S(1)}, u32[]{:S(2)}, u32[]{:S(2)}) %collective-permute-start.1) | collective-permute-done | bytes 122912 | tf_op jit(solution)/shard_map/ppermute | solution.py:10
  93.0 0.7 reduce.8
  93.8 12.7 %all_to_all.18 = bf16[16,2,960]{2,1,0:T(2,128)(2,1)S(1)} all-to-all(bf16[16,2,960]{2,1,0:T(2,128)(2,1)S(1)} %reshape.152), channel_id=1, replica_groups=mesh['tm'=32,'rows'=16] {'rows'}, dimensions={0} | all-to-all | bytes 122880 | tf_op jit(solution)/shard_map/all_to_all | solution.py:44
  107.0 0.4 reshape.123
  107.7 0.8 copy.64
  (55 shorter events, 7.2 us)
Async XLA Ops:
  0.0 27.1 %copy-start.2 = (f32[384]{0:T(512)S(1)}, f32[384]{0:T(512)}, u32[]{:S(2)}) copy-start(f32[384]{0:T(512)} %param.8) | copy-start | bytes 4612
  27.9 1.0 copy-start
  28.0 1.1 copy-start.4
  33.8 4.9 %copy-start.1 = (bf16[24,3,3,3,384]{4,0,3,2,1:T(8,128)(2,1)S(1)}, bf16[24,3,3,3,384]{4,0,3,2,1:T(8,128)(2,1)}, u32[]{:S(2)}) copy-start(bf16[24,3,3,3,384]{4,0,3,2,1:T(8,128)(2,1)} %param.12) | copy-start | bytes 1492996
  34.1 10.0 %collective-permute-start = (f32[16,1920]{1,0:T(8,128)S(1)}, f32[16,1920]{1,0:T(8,128)S(1)}, u32[]{:S(2)}, u32[]{:S(2)}) collective-permute-start(f32[16,1920]{1,0:T(8,128)S(1)} %reshape.119), channel_id=1, source_target_pairs={{0,16},{16,32},{32,48},{48,64},{64,80},{80,96},{96,112},{112,128},... | collective-permute-start | bytes 368648 | tf_op jit(solution)/shard_map/ppermute | solution.py:10
  46.0 12.1 %all-to-all-start = ((bf16[16,2,960]{2,1,0:T(2,128)(2,1)}), bf16[16,2,960]{2,1,0:T(2,128)(2,1)S(1)}, u32[]{:S(2)}, u32[]{:S(2)}) async-start(bf16[16,2,960]{2,1,0:T(2,128)(2,1)} %reshape.150), calls=%async_computation | async-start | bytes 131072 | tf_op jit(solution)/shard_map/all_to_all | solution.py:44
  50.8 8.9 %copy-start.3 = (f32[384]{0:T(512)S(1)}, f32[384]{0:T(512)}, u32[]{:S(2)}) copy-start(f32[384]{0:T(512)} %param.11) | copy-start | bytes 4612
  83.0 10.0 %collective-permute-start.1 = (f32[16,1920]{1,0:T(8,128)S(1)}, f32[16,1920]{1,0:T(8,128)S(1)}, u32[]{:S(2)}, u32[]{:S(2)}) collective-permute-start(f32[16,1920]{1,0:T(8,128)S(1)} %reshape.122), channel_id=1, source_target_pairs={{0,16},{16,32},{32,48},{48,64},{64,80},{80,96},{96,112},{112,128},... | collective-permute-start | bytes 368648 | tf_op jit(solution)/shard_map/ppermute | solution.py:10

commit v13 on v12

--- a/solution.py
+++ b/solution.py
@@ -32,12 +32,12 @@
     tap = [product[..., a * part_width : (a + 1) * part_width] for a in range(3)]
 
     def rows_first(pair):
-        return jnp.transpose(jnp.stack(pair, 0), (1, 0, 2, 3)).reshape(height, -1)
+        return jnp.transpose(jnp.stack(pair, 0), (1, 0, 2, 3)).reshape(height, frames, -1)
 
     onward = rows_first([tap[0][0] + tap[1][1], tap[0][1]])
     kept = rows_first([tap[2][0], tap[1][0] + tap[2][1]])
-    arrived = passed_along(onward, "tm", 1)
-    return kept + arrived + jnp.tile(bias_part, frames * columns)
+    arrived = passed_along(onward.reshape(height, -1), "tm", 1).reshape(kept.shape)
+    return kept + arrived + jnp.tile(bias_part, columns)
 
 
 def own_row(laid, frames, columns):
@@ -55,7 +55,7 @@
     every_row = lax.all_gather(features, "rows", axis=1, tiled=True)
     full_one = norm_silu(every_row, gain_one)
     residual = lax.dynamic_slice_in_dim(every_row, offset, part_width, 3)
-    residual = jnp.transpose(residual, (1, 0, 2, 3)).reshape(residual.shape[1], -1)
+    residual = jnp.transpose(residual, (1, 0, 2, 3)).reshape(residual.shape[1], frames, -1)
     conv_one = causal_conv(full_one, weight_one, bias_first).astype(jnp.bfloat16)
     own_rows = own_row(conv_one, frames, columns)
     normed_two = norm_silu(own_rows, gain_two)

time: 109 us -> 106 us (0.972)
  other arithmetic: 4.9 us -> 2.99 us
    all_to_all x5 -> x0, other arithmetic: 1.71 us -> none  [own_row(): lax.all_to_all(laid, 'rows', split_axis=0, concat_axis=0, tiled=True)]
    unnamed x16 -> x12, local copies, waits for them, and re-layouts: 2.03 us -> 0.91 us
where the time goes in v13:
time: 106 us
  blocking collectives  57.2 us (54%)
  waiting for transfers between devices  19.4 us (18%)
  local copies, waits for them, and re-layouts  9.42 us (9%)
  starting transfers between devices  9.28 us (9%)
  matrix products  6.93 us (7%)
  other arithmetic  2.99 us (3%)
    all_gather x1, blocking collectives, shards(): every_row = lax.all_gather(features, 'rows', axis=1, tiled=True)  26.8 us
    all_gather x1, blocking collectives, shards(): full_two = lax.all_gather(normed_two, 'rows', axis=1, tiled=True)  17.6 us
    ppermute x2, waiting for transfers between devices, passed_along(): return lax.ppermute(x, axis, pairs)  13 us
    all_to_all x1, blocking collectives, own_row(): lax.all_to_all(laid, 'rows', split_axis=0, concat_axis=0, tiled=True)  12.8 us
    conv_general_dilated x2, matrix products, causal_conv(): lax.conv_general_dilated(own, stacked, window_strides=(1, 1), padding=((1...  6.93 us
    all_to_all x1, waiting for transfers between devices, own_row(): lax.all_to_all(laid, 'rows', split_axis=0, concat_axis=0, tiled=True)  6.38 us
    ppermute x2, starting transfers between devices, passed_along(): return lax.ppermute(x, axis, pairs)  5.04 us
    all_to_all x1, starting transfers between devices, own_row(): lax.all_to_all(laid, 'rows', split_axis=0, concat_axis=0, tiled=True)  4.24 us
  transfers between devices with their start and end apart: 3, of which 3 were waited for; matrix products, arithmetic and copies ran while one was open for 3% of the time, Pallas kernels for 0%

profile of v13, /device:TPU:33, one launch (start us, length us, event | category | flops | bytes accessed | tf_op | source)
XLA Modules:
  0.0 105.6 jit_solution(10138521436737265294)
XLA Ops:
  0.0 26.8 %all_gather.6 = bf16[2,16,40,384]{3,2,0,1:T(8,128)(2,1)S(1)} all-gather(bf16[2,1,40,384]{3,2,0,1:T(8,128)(2,1)} %bitcast.79), channel_id=1, replica_groups=mesh['tm'=32,'rows'=16] {'rows'}, dimensions={1}, use_global_device_ids=true | all-gather | bytes 1044480 | tf_op jit(solution)/shard_map/all_gather | solution.py:55
  27.1 0.7 fusion.24
  28.2 0.8 copy-done
  29.0 3.5 %fusion.18 = f32[16,16,6,72]{3,1,2,0:T(8,128)S(1)} fusion(bf16[72,3,3,384]{3,0,2,1:T(8,128)(2,1)S(1)} %bitcast.78, bf16[16,2,8,8,384]{4,0,3,2,1:T(8,128)(2,1)S(1)} %fusion.10, pred[16,6]{0,1:T(8,128)(4,1)S(1)} %copy-done.4), kind=kOutput, calls=%fused_computation.21 | convolution fusion | flops 732672000 | bytes 2512992 | tf_op jit(solution)/shard_map/conv_general_dilated | solution.py:24
  32.5 0.5 copy.74
  33.0 0.4 slice_add_fusion.2
  33.8 0.3 reshape_reshape.6
  34.1 3.1 %collective-permute-start = (f32[16,1920]{1,0:T(8,128)S(1)}, f32[16,1920]{1,0:T(8,128)S(1)}, u32[]{:S(2)}, u32[]{:S(2)}) collective-permute-start(f32[16,1920]{1,0:T(8,128)S(1)} %reshape_reshape.6), channel_id=1, source_target_pairs={{0,16},{16,32},{32,48},{48,64},{64,80},{80,96},{96,112},{112,128},... | collective-permute-start | bytes 368648 | tf_op jit(solution)/shard_map/ppermute | solution.py:10
  37.7 0.8 dynamic_slice.10
  38.6 5.5 %collective-permute-done = f32[16,1920]{1,0:T(8,128)S(1)} collective-permute-done((f32[16,1920]{1,0:T(8,128)S(1)}, f32[16,1920]{1,0:T(8,128)S(1)}, u32[]{:S(2)}, u32[]{:S(2)}) %collective-permute-start) | collective-permute-done | bytes 122912 | tf_op jit(solution)/shard_map/ppermute | solution.py:10
  44.3 0.7 copy.78
  45.0 4.2 %all-to-all-start = ((bf16[16,2,960]{2,1,0:T(2,128)(2,1)}), bf16[16,2,960]{2,1,0:T(2,128)(2,1)S(1)}, u32[]{:S(2)}, u32[]{:S(2)}) async-start(bf16[16,2,960]{2,1,0:T(2,128)(2,1)} %copy.78), calls=%async_computation | async-start | bytes 131072 | tf_op jit(solution)/shard_map/all_to_all | solution.py:44
  49.4 0.4 reshape.142
  49.8 0.8 dynamic_slice.11
  50.7 6.4 %all-to-all-done = bf16[16,2,960]{2,1,0:T(2,128)(2,1)S(1)} async-done(((bf16[16,2,960]{2,1,0:T(2,128)(2,1)}), bf16[16,2,960]{2,1,0:T(2,128)(2,1)S(1)}, u32[]{:S(2)}, u32[]{:S(2)}) %all-to-all-start) | async-done | bytes 61472 | tf_op jit(solution)/shard_map/all_to_all | solution.py:44
  58.1 17.6 %all_gather.7 = bf16[2,16,40,384]{3,2,0,1:T(8,128)(2,1)S(1)} all-gather(bf16[2,1,40,384]{3,2,0,1:T(8,128)(2,1)S(1)} %fusion.29), channel_id=1, replica_groups=mesh['tm'=32,'rows'=16] {'rows'}, dimensions={1}, use_global_device_ids=true | all-gather | bytes 1044480 | tf_op jit(solution)/shard_map/all_gather | solution.py:62
  76.3 3.5 %fusion.21 = f32[16,16,6,72]{3,1,2,0:T(8,128)S(1)} fusion(bf16[72,3,3,384]{3,0,2,1:T(8,128)(2,1)S(1)} %bitcast.77, bf16[16,2,8,8,384]{4,0,3,2,1:T(8,128)(2,1)S(1)} %fusion.11, pred[16,6]{0,1:T(8,128)(4,1)S(1)} %copy-done.4), kind=kOutput, calls=%fused_computation.22 | convolution fusion | flops 732672000 | bytes 2512992 | tf_op jit(solution)/shard_map/conv_general_dilated | solution.py:24
  79.8 0.5 copy.86
  80.3 0.4 slice_add_fusion
  81.0 0.3 reshape_reshape.7
  81.3 1.9 %collective-permute-start.1 = (f32[16,1920]{1,0:T(8,128)S(1)}, f32[16,1920]{1,0:T(8,128)S(1)}, u32[]{:S(2)}, u32[]{:S(2)}) collective-permute-start(f32[16,1920]{1,0:T(8,128)S(1)} %reshape_reshape.7), channel_id=1, source_target_pairs={{0,16},{16,32},{32,48},{48,64},{64,80},{80,96},{96,112},{112,128},... | collective-permute-start | bytes 368648 | tf_op jit(solution)/shard_map/ppermute | solution.py:10
  83.7 7.5 %collective-permute-done.1 = f32[16,1920]{1,0:T(8,128)S(1)} collective-permute-done((f32[16,1920]{1,0:T(8,128)S(1)}, f32[16,1920]{1,0:T(8,128)S(1)}, u32[]{:S(2)}, u32[]{:S(2)}) %collective-permute-start.1) | collective-permute-done | bytes 122912 | tf_op jit(solution)/shard_map/ppermute | solution.py:10
  91.6 12.8 %all_to_all.10 = bf16[16,2,960]{2,1,0:T(2,128)(2,1)S(1)} all-to-all(bf16[16,2,960]{2,1,0:T(2,128)(2,1)S(1)} %copy.90), channel_id=1, replica_groups=mesh['tm'=32,'rows'=16] {'rows'}, dimensions={0} | all-to-all | bytes 122880 | tf_op jit(solution)/shard_map/all_to_all | solution.py:44
  104.9 0.7 copy.93
  (53 shorter events, 5.3 us)
Async XLA Ops:
  0.0 27.1 %copy-start.2 = (f32[384]{0:T(512)S(1)}, f32[384]{0:T(512)}, u32[]{:S(2)}) copy-start(f32[384]{0:T(512)} %param.8) | copy-start | bytes 4612
  27.9 1.0 copy-start
  28.0 1.1 %copy-start.4 = (pred[16,6]{0,1:T(8,128)(4,1)S(1)}, pred[16,6]{0,1:T(8,128)(4,1)}, u32[]{:S(2)}) copy-start(pred[16,6]{0,1:T(8,128)(4,1)} %constant.36) | copy-start | bytes 292
  33.8 4.8 %copy-start.1 = (bf16[24,3,3,3,384]{4,0,3,2,1:T(8,128)(2,1)S(1)}, bf16[24,3,3,3,384]{4,0,3,2,1:T(8,128)(2,1)}, u32[]{:S(2)}) copy-start(bf16[24,3,3,3,384]{4,0,3,2,1:T(8,128)(2,1)} %param.12) | copy-start | bytes 1492996
  34.1 10.0 %collective-permute-start = (f32[16,1920]{1,0:T(8,128)S(1)}, f32[16,1920]{1,0:T(8,128)S(1)}, u32[]{:S(2)}, u32[]{:S(2)}) collective-permute-start(f32[16,1920]{1,0:T(8,128)S(1)} %reshape_reshape.6), channel_id=1, source_target_pairs={{0,16},{16,32},{32,48},{48,64},{64,80},{80,96},{96,112},{112,128},... | collective-permute-start | bytes 368648 | tf_op jit(solution)/shard_map/ppermute | solution.py:10
  45.0 12.1 %all-to-all-start = ((bf16[16,2,960]{2,1,0:T(2,128)(2,1)}), bf16[16,2,960]{2,1,0:T(2,128)(2,1)S(1)}, u32[]{:S(2)}, u32[]{:S(2)}) async-start(bf16[16,2,960]{2,1,0:T(2,128)(2,1)} %copy.78), calls=%async_computation | async-start | bytes 131072 | tf_op jit(solution)/shard_map/all_to_all | solution.py:44
  49.8 8.2 %copy-start.3 = (f32[384]{0:T(512)S(1)}, f32[384]{0:T(512)}, u32[]{:S(2)}) copy-start(f32[384]{0:T(512)} %param.11) | copy-start | bytes 4612
  81.3 10.0 %collective-permute-start.1 = (f32[16,1920]{1,0:T(8,128)S(1)}, f32[16,1920]{1,0:T(8,128)S(1)}, u32[]{:S(2)}, u32[]{:S(2)}) collective-permute-start(f32[16,1920]{1,0:T(8,128)S(1)} %reshape_reshape.7), channel_id=1, source_target_pairs={{0,16},{16,32},{32,48},{48,64},{64,80},{80,96},{96,112},{112,128},... | collective-permute-start | bytes 368648 | tf_op jit(solution)/shard_map/ppermute | solution.py:10

commit v14 on v13

--- a/solution.py
+++ b/solution.py
@@ -26,16 +26,16 @@
         stacked,
         window_strides=(1, 1),
         padding=((1, 1), (1, 1)),
-        dimension_numbers=("NHWC", "OHWI", "NHWC"),
+        dimension_numbers=("NHWC", "OHWI", "HNWC"),
         preferred_element_type=jnp.float32,
     )
     tap = [product[..., a * part_width : (a + 1) * part_width] for a in range(3)]
 
     def rows_first(pair):
-        return jnp.transpose(jnp.stack(pair, 0), (1, 0, 2, 3)).reshape(height, frames, -1)
+        return jnp.stack(pair, 1).reshape(height, frames, -1)
 
-    onward = rows_first([tap[0][0] + tap[1][1], tap[0][1]])
-    kept = rows_first([tap[2][0], tap[1][0] + tap[2][1]])
+    onward = rows_first([tap[0][:, 0] + tap[1][:, 1], tap[0][:, 1]])
+    kept = rows_first([tap[2][:, 0], tap[1][:, 0] + tap[2][:, 1]])
     arrived = passed_along(onward.reshape(height, -1), "tm", 1).reshape(kept.shape)
     return kept + arrived + jnp.tile(bias_part, columns)
 

time: 106 us -> 106 us (level)
    ppermute x2, waiting for transfers between devices: 13 us -> 11.5 us  [passed_along(): return lax.ppermute(x, axis, pairs)]
    all_to_all x1, waiting for transfers between devices: 6.38 us -> 7.76 us  [own_row(): lax.all_to_all(laid, 'rows', split_axis=0, concat_axis=0, tiled=True)]
where the time goes in v14:
time: 106 us
  blocking collectives  57.2 us (54%)
  waiting for transfers between devices  19.3 us (18%)
  local copies, waits for them, and re-layouts  9.48 us (9%)
  starting transfers between devices  9.42 us (9%)
  matrix products  6.93 us (7%)
  other arithmetic  2.9 us (3%)
    all_gather x1, blocking collectives, shards(): every_row = lax.all_gather(features, 'rows', axis=1, tiled=True)  26.8 us
    all_gather x1, blocking collectives, shards(): full_two = lax.all_gather(normed_two, 'rows', axis=1, tiled=True)  17.6 us
    all_to_all x1, blocking collectives, own_row(): lax.all_to_all(laid, 'rows', split_axis=0, concat_axis=0, tiled=True)  12.8 us
    ppermute x2, waiting for transfers between devices, passed_along(): return lax.ppermute(x, axis, pairs)  11.5 us
    all_to_all x1, waiting for transfers between devices, own_row(): lax.all_to_all(laid, 'rows', split_axis=0, concat_axis=0, tiled=True)  7.76 us
    conv_general_dilated x2, matrix products, causal_conv(): lax.conv_general_dilated(own, stacked, window_strides=(1, 1), padding=((1...  6.93 us
    ppermute x2, starting transfers between devices, passed_along(): return lax.ppermute(x, axis, pairs)  5.18 us
    all_to_all x1, starting transfers between devices, own_row(): lax.all_to_all(laid, 'rows', split_axis=0, concat_axis=0, tiled=True)  4.25 us
  transfers between devices with their start and end apart: 3, of which 3 were waited for; matrix products, arithmetic and copies ran while one was open for 3% of the time, Pallas kernels for 0%

profile of v14, /device:TPU:33, one launch (start us, length us, event | category | flops | bytes accessed | tf_op | source)
XLA Modules:
  0.0 105.6 jit_solution(2151371085866886302)
XLA Ops:
  0.0 26.8 %all_gather.6 = bf16[2,16,40,384]{3,2,0,1:T(8,128)(2,1)S(1)} all-gather(bf16[2,1,40,384]{3,2,0,1:T(8,128)(2,1)} %bitcast.75), channel_id=1, replica_groups=mesh['tm'=32,'rows'=16] {'rows'}, dimensions={1}, use_global_device_ids=true | all-gather | bytes 1044480 | tf_op jit(solution)/shard_map/all_gather | solution.py:55
  27.1 0.7 fusion.24
  28.2 0.8 copy-done
  29.0 3.5 %fusion.18 = f32[16,16,6,72]{3,1,2,0:T(8,128)S(1)} fusion(bf16[72,3,3,384]{3,0,2,1:T(8,128)(2,1)S(1)} %bitcast.74, bf16[16,2,8,8,384]{4,0,3,2,1:T(8,128)(2,1)S(1)} %fusion.10, pred[16,6]{0,1:T(8,128)(4,1)S(1)} %copy-done.4), kind=kOutput, calls=%fused_computation.21 | convolution fusion | flops 732672000 | bytes 2512992 | tf_op jit(solution)/shard_map/conv_general_dilated | solution.py:24
  32.5 0.5 copy.81
  33.0 0.4 slice_add_fusion.2
  33.7 0.3 reshape_reshape.6
  34.0 3.3 %collective-permute-start = (f32[16,1920]{1,0:T(8,128)S(1)}, f32[16,1920]{1,0:T(8,128)S(1)}, u32[]{:S(2)}, u32[]{:S(2)}) collective-permute-start(f32[16,1920]{1,0:T(8,128)S(1)} %reshape_reshape.6), channel_id=1, source_target_pairs={{0,16},{16,32},{32,48},{48,64},{64,80},{80,96},{96,112},{112,128},... | collective-permute-start | bytes 368648 | tf_op jit(solution)/shard_map/ppermute | solution.py:10
  37.8 0.8 dynamic_slice.10
  38.7 5.4 %collective-permute-done = f32[16,1920]{1,0:T(8,128)S(1)} collective-permute-done((f32[16,1920]{1,0:T(8,128)S(1)}, f32[16,1920]{1,0:T(8,128)S(1)}, u32[]{:S(2)}, u32[]{:S(2)}) %collective-permute-start) | collective-permute-done | bytes 122912 | tf_op jit(solution)/shard_map/ppermute | solution.py:10
  44.3 0.7 copy.86
  45.0 4.2 %all-to-all-start = ((bf16[16,2,960]{2,1,0:T(2,128)(2,1)}), bf16[16,2,960]{2,1,0:T(2,128)(2,1)S(1)}, u32[]{:S(2)}, u32[]{:S(2)}) async-start(bf16[16,2,960]{2,1,0:T(2,128)(2,1)} %copy.86), calls=%async_computation | async-start | bytes 131072 | tf_op jit(solution)/shard_map/all_to_all | solution.py:44
  49.3 7.8 %all-to-all-done = bf16[16,2,960]{2,1,0:T(2,128)(2,1)S(1)} async-done(((bf16[16,2,960]{2,1,0:T(2,128)(2,1)}), bf16[16,2,960]{2,1,0:T(2,128)(2,1)S(1)}, u32[]{:S(2)}, u32[]{:S(2)}) %all-to-all-start) | async-done | bytes 61472 | tf_op jit(solution)/shard_map/all_to_all | solution.py:44
  58.1 17.6 %all_gather.7 = bf16[2,16,40,384]{3,2,0,1:T(8,128)(2,1)S(1)} all-gather(bf16[2,1,40,384]{3,2,0,1:T(8,128)(2,1)S(1)} %fusion.30), channel_id=1, replica_groups=mesh['tm'=32,'rows'=16] {'rows'}, dimensions={1}, use_global_device_ids=true | all-gather | bytes 1044480 | tf_op jit(solution)/shard_map/all_gather | solution.py:62
  76.4 3.5 %fusion.21 = f32[16,16,6,72]{3,1,2,0:T(8,128)S(1)} fusion(bf16[72,3,3,384]{3,0,2,1:T(8,128)(2,1)S(1)} %bitcast.73, bf16[16,2,8,8,384]{4,0,3,2,1:T(8,128)(2,1)S(1)} %fusion.11, pred[16,6]{0,1:T(8,128)(4,1)S(1)} %copy-done.4), kind=kOutput, calls=%fused_computation.22 | convolution fusion | flops 732672000 | bytes 2512992 | tf_op jit(solution)/shard_map/conv_general_dilated | solution.py:24
  79.8 0.5 copy.94
  80.3 0.4 slice_add_fusion
  81.0 0.3 reshape_reshape.7
  81.3 1.9 %collective-permute-start.1 = (f32[16,1920]{1,0:T(8,128)S(1)}, f32[16,1920]{1,0:T(8,128)S(1)}, u32[]{:S(2)}, u32[]{:S(2)}) collective-permute-start(f32[16,1920]{1,0:T(8,128)S(1)} %reshape_reshape.7), channel_id=1, source_target_pairs={{0,16},{16,32},{32,48},{48,64},{64,80},{80,96},{96,112},{112,128},... | collective-permute-start | bytes 368648 | tf_op jit(solution)/shard_map/ppermute | solution.py:10
  83.4 0.4 reshape.140
  83.8 0.8 dynamic_slice.11
  85.2 6.1 %collective-permute-done.1 = f32[16,1920]{1,0:T(8,128)S(1)} collective-permute-done((f32[16,1920]{1,0:T(8,128)S(1)}, f32[16,1920]{1,0:T(8,128)S(1)}, u32[]{:S(2)}, u32[]{:S(2)}) %collective-permute-start.1) | collective-permute-done | bytes 122912 | tf_op jit(solution)/shard_map/ppermute | solution.py:10
  91.6 12.8 %all_to_all.10 = bf16[16,2,960]{2,1,0:T(2,128)(2,1)S(1)} all-to-all(bf16[16,2,960]{2,1,0:T(2,128)(2,1)S(1)} %copy.99), channel_id=1, replica_groups=mesh['tm'=32,'rows'=16] {'rows'}, dimensions={0} | all-to-all | bytes 122880 | tf_op jit(solution)/shard_map/all_to_all | solution.py:44
  104.9 0.7 copy.102
  (54 shorter events, 5.2 us)
Async XLA Ops:
  0.0 27.1 %copy-start.2 = (f32[384]{0:T(512)S(1)}, f32[384]{0:T(512)}, u32[]{:S(2)}) copy-start(f32[384]{0:T(512)} %param.8) | copy-start | bytes 4612
  27.9 1.0 copy-start
  28.0 1.1 %copy-start.4 = (pred[16,6]{0,1:T(8,128)(4,1)S(1)}, pred[16,6]{0,1:T(8,128)(4,1)}, u32[]{:S(2)}) copy-start(pred[16,6]{0,1:T(8,128)(4,1)} %constant.36) | copy-start | bytes 292
  34.0 15.3 %copy-start.1 = (bf16[24,3,3,3,384]{4,0,3,2,1:T(8,128)(2,1)S(1)}, bf16[24,3,3,3,384]{4,0,3,2,1:T(8,128)(2,1)}, u32[]{:S(2)}) copy-start(bf16[24,3,3,3,384]{4,0,3,2,1:T(8,128)(2,1)} %param.12) | copy-start | bytes 1492996
  34.0 10.1 %collective-permute-start = (f32[16,1920]{1,0:T(8,128)S(1)}, f32[16,1920]{1,0:T(8,128)S(1)}, u32[]{:S(2)}, u32[]{:S(2)}) collective-permute-start(f32[16,1920]{1,0:T(8,128)S(1)} %reshape_reshape.6), channel_id=1, source_target_pairs={{0,16},{16,32},{32,48},{48,64},{64,80},{80,96},{96,112},{112,128},... | collective-permute-start | bytes 368648 | tf_op jit(solution)/shard_map/ppermute | solution.py:10
  45.0 12.1 %all-to-all-start = ((bf16[16,2,960]{2,1,0:T(2,128)(2,1)}), bf16[16,2,960]{2,1,0:T(2,128)(2,1)S(1)}, u32[]{:S(2)}, u32[]{:S(2)}) async-start(bf16[16,2,960]{2,1,0:T(2,128)(2,1)} %copy.86), calls=%async_computation | async-start | bytes 131072 | tf_op jit(solution)/shard_map/all_to_all | solution.py:44
  49.3 8.7 %copy-start.3 = (f32[384]{0:T(512)S(1)}, f32[384]{0:T(512)}, u32[]{:S(2)}) copy-start(f32[384]{0:T(512)} %param.11) | copy-start | bytes 4612
  81.3 10.0 %collective-permute-start.1 = (f32[16,1920]{1,0:T(8,128)S(1)}, f32[16,1920]{1,0:T(8,128)S(1)}, u32[]{:S(2)}, u32[]{:S(2)}) collective-permute-start(f32[16,1920]{1,0:T(8,128)S(1)} %reshape_reshape.7), channel_id=1, source_target_pairs={{0,16},{16,32},{32,48},{48,64},{64,80},{80,96},{96,112},{112,128},... | collective-permute-start | bytes 368648 | tf_op jit(solution)/shard_map/ppermute | solution.py:10

commit v15 on v13

--- a/solution.py
+++ b/solution.py
@@ -41,9 +41,9 @@
 
 
 def own_row(laid, frames, columns):
-    sources = lax.all_to_all(laid, "rows", split_axis=0, concat_axis=0, tiled=True)
-    sources = sources.reshape(sources.shape[0], frames, columns, -1)
-    return jnp.transpose(sources, (1, 2, 0, 3)).reshape(frames, 1, columns, -1)
+    pieces = laid.reshape(laid.shape[0], frames, columns, -1)
+    placed = lax.all_to_all(pieces, "rows", split_axis=0, concat_axis=3, tiled=True)
+    return placed.reshape(frames, 1, columns, -1)
 
 
 def shards(features, gain_one, weight_one, bias_one, gain_two, weight_two, bias_two):

time: 106 us -> 107 us (level)
  waiting for transfers between devices: 19.4 us -> 20.8 us
    unnamed x12 -> x19, local copies, waits for them, and re-layouts: 0.91 us -> 3.47 us
    all_to_all x1, waiting for transfers between devices: 6.38 us -> 7.76 us  [own_row(): lax.all_to_all(pieces, 'rows', split_axis=0, concat_axis=3, tiled=True)]
    convert_element_type x3 -> x0, local copies, waits for them, and re-layouts: 1.17 us -> none  [the longest x1 0.68 us: shards(): causal_conv(full_one, weight_one, bias_first).astype(jnp.bfloat16)]
  transfers between devices with their start and end apart: 3 -> 3, of which waited for: 3 -> 3; matrix products, arithmetic and copies ran while one was open for 3% -> 2% of each run, Pallas kernels for 0% -> 0%
where the time goes in v15:
time: 107 us
  blocking collectives  57.2 us (53%)
  waiting for transfers between devices  20.8 us (19%)
  local copies, waits for them, and re-layouts  9.99 us (9%)
  starting transfers between devices  9.3 us (9%)
  matrix products  6.96 us (7%)
  other arithmetic  2.08 us (2%)
    all_gather x1, blocking collectives, shards(): every_row = lax.all_gather(features, 'rows', axis=1, tiled=True)  26.8 us
    all_gather x1, blocking collectives, shards(): full_two = lax.all_gather(normed_two, 'rows', axis=1, tiled=True)  17.6 us
    ppermute x2, waiting for transfers between devices, passed_along(): return lax.ppermute(x, axis, pairs)  13 us
    all_to_all x1, blocking collectives, own_row(): lax.all_to_all(pieces, 'rows', split_axis=0, concat_axis=3, tiled=True)  12.7 us
    all_to_all x1, waiting for transfers between devices, own_row(): lax.all_to_all(pieces, 'rows', split_axis=0, concat_axis=3, tiled=True)  7.76 us
    conv_general_dilated x2, matrix products, causal_conv(): lax.conv_general_dilated(own, stacked, window_strides=(1, 1), padding=((1...  6.96 us
    ppermute x2, starting transfers between devices, passed_along(): return lax.ppermute(x, axis, pairs)  5.05 us
    all_to_all x1, starting transfers between devices, own_row(): lax.all_to_all(pieces, 'rows', split_axis=0, concat_axis=3, tiled=True)  4.25 us
  transfers between devices with their start and end apart: 3, of which 3 were waited for; matrix products, arithmetic and copies ran while one was open for 2% of the time, Pallas kernels for 0%

profile of v15, /device:TPU:33, one launch (start us, length us, event | category | flops | bytes accessed | tf_op | source)
XLA Modules:
  0.0 106.6 jit_solution(15017528950291777764)
XLA Ops:
  0.0 26.8 %all_gather.6 = bf16[2,16,40,384]{3,2,0,1:T(8,128)(2,1)S(1)} all-gather(bf16[2,1,40,384]{3,2,0,1:T(8,128)(2,1)} %bitcast.98), channel_id=1, replica_groups=mesh['tm'=32,'rows'=16] {'rows'}, dimensions={1}, use_global_device_ids=true | all-gather | bytes 1044480 | tf_op jit(solution)/shard_map/all_gather | solution.py:55
  27.1 0.7 fusion.24
  28.2 0.8 copy-done
  29.0 3.5 %fusion.18 = f32[16,16,6,72]{3,1,2,0:T(8,128)S(1)} fusion(bf16[72,3,3,384]{3,0,2,1:T(8,128)(2,1)S(1)} %bitcast.97, bf16[16,2,8,8,384]{4,0,3,2,1:T(8,128)(2,1)S(1)} %fusion.10, pred[16,6]{0,1:T(8,128)(4,1)S(1)} %copy-done.4), kind=kOutput, calls=%fused_computation.21 | convolution fusion | flops 732672000 | bytes 2512992 | tf_op jit(solution)/shard_map/conv_general_dilated | solution.py:24
  32.5 0.5 copy.51
  33.0 0.4 copy.68
  33.8 0.3 reshape_reshape.6
  34.2 3.1 %collective-permute-start = (f32[16,1920]{1,0:T(8,128)S(1)}, f32[16,1920]{1,0:T(8,128)S(1)}, u32[]{:S(2)}, u32[]{:S(2)}) collective-permute-start(f32[16,1920]{1,0:T(8,128)S(1)} %reshape_reshape.6), channel_id=1, source_target_pairs={{0,16},{16,32},{32,48},{48,64},{64,80},{80,96},{96,112},{112,128},... | collective-permute-start | bytes 368648 | tf_op jit(solution)/shard_map/ppermute | solution.py:10
  37.3 0.8 dynamic_slice.10
  38.1 6.1 %collective-permute-done = f32[16,1920]{1,0:T(8,128)S(1)} collective-permute-done((f32[16,1920]{1,0:T(8,128)S(1)}, f32[16,1920]{1,0:T(8,128)S(1)}, u32[]{:S(2)}, u32[]{:S(2)}) %collective-permute-start) | collective-permute-done | bytes 122912 | tf_op jit(solution)/shard_map/ppermute | solution.py:10
  44.1 0.4 reshape.111
  44.9 0.9 reshape.137
  45.7 4.3 %all-to-all-start = ((bf16[16,2,960]{2,1,0:T(2,128)(2,1)}), bf16[16,2,960]{2,1,0:T(2,128)(2,1)S(1)}, u32[]{:S(2)}, u32[]{:S(2)}) async-start(bf16[16,2,960]{2,1,0:T(2,128)(2,1)} %reshape.137), calls=%async_computation | async-start | bytes 131072 | tf_op jit(solution)/shard_map/all_to_all | solution.py:45
  50.1 7.8 %all-to-all-done = bf16[16,2,960]{2,1,0:T(2,128)(2,1)S(1)} async-done(((bf16[16,2,960]{2,1,0:T(2,128)(2,1)}), bf16[16,2,960]{2,1,0:T(2,128)(2,1)S(1)}, u32[]{:S(2)}, u32[]{:S(2)}) %all-to-all-start) | async-done | bytes 61472 | tf_op jit(solution)/shard_map/all_to_all | solution.py:45
  58.5 17.6 %all_gather.7 = bf16[2,16,40,384]{3,2,0,1:T(8,128)(2,1)S(1)} all-gather(bf16[2,1,40,384]{3,2,0,1:T(8,128)(2,1)S(1)} %fusion.33), channel_id=1, replica_groups=mesh['tm'=32,'rows'=16] {'rows'}, dimensions={1}, use_global_device_ids=true | all-gather | bytes 1044480 | tf_op jit(solution)/shard_map/all_gather | solution.py:62
  76.7 3.5 %fusion.21 = f32[16,16,6,72]{3,1,2,0:T(8,128)S(1)} fusion(bf16[72,3,3,384]{3,0,2,1:T(8,128)(2,1)S(1)} %bitcast.96, bf16[16,2,8,8,384]{4,0,3,2,1:T(8,128)(2,1)S(1)} %fusion.11, pred[16,6]{0,1:T(8,128)(4,1)S(1)} %copy-done.4), kind=kOutput, calls=%fused_computation.22 | convolution fusion | flops 732672000 | bytes 2512992 | tf_op jit(solution)/shard_map/conv_general_dilated | solution.py:24
  80.2 0.5 copy.61
  80.7 0.4 copy.69
  81.9 1.9 %collective-permute-start.1 = (f32[16,1920]{1,0:T(8,128)S(1)}, f32[16,1920]{1,0:T(8,128)S(1)}, u32[]{:S(2)}, u32[]{:S(2)}) collective-permute-start(f32[16,1920]{1,0:T(8,128)S(1)} %reshape_reshape.7), channel_id=1, source_target_pairs={{0,16},{16,32},{32,48},{48,64},{64,80},{80,96},{96,112},{112,128},... | collective-permute-start | bytes 368648 | tf_op jit(solution)/shard_map/ppermute | solution.py:10
  84.1 0.8 dynamic_slice.11
  84.9 6.9 %collective-permute-done.1 = f32[16,1920]{1,0:T(8,128)S(1)} collective-permute-done((f32[16,1920]{1,0:T(8,128)S(1)}, f32[16,1920]{1,0:T(8,128)S(1)}, u32[]{:S(2)}, u32[]{:S(2)}) %collective-permute-start.1) | collective-permute-done | bytes 122912 | tf_op jit(solution)/shard_map/ppermute | solution.py:10
  91.8 0.4 reshape.113
  92.9 12.7 %all_to_all.24 = bf16[16,2,960]{2,1,0:T(2,128)(2,1)S(1)} all-to-all(bf16[16,2,960]{2,1,0:T(2,128)(2,1)S(1)} %reshape.139), channel_id=1, replica_groups=mesh['tm'=32,'rows'=16] {'rows'}, dimensions={0} | all-to-all | bytes 122880 | tf_op jit(solution)/shard_map/all_to_all | solution.py:45
  105.9 0.7 copy.66
  (46 shorter events, 4.6 us)
Async XLA Ops:
  0.0 27.1 %copy-start.2 = (f32[384]{0:T(512)S(1)}, f32[384]{0:T(512)}, u32[]{:S(2)}) copy-start(f32[384]{0:T(512)} %param.8) | copy-start | bytes 4612
  27.9 1.0 copy-start
  28.0 1.1 %copy-start.4 = (pred[16,6]{0,1:T(8,128)(4,1)S(1)}, pred[16,6]{0,1:T(8,128)(4,1)}, u32[]{:S(2)}) copy-start(pred[16,6]{0,1:T(8,128)(4,1)} %constant.36) | copy-start | bytes 292
  34.2 10.0 %collective-permute-start = (f32[16,1920]{1,0:T(8,128)S(1)}, f32[16,1920]{1,0:T(8,128)S(1)}, u32[]{:S(2)}, u32[]{:S(2)}) collective-permute-start(f32[16,1920]{1,0:T(8,128)S(1)} %reshape_reshape.6), channel_id=1, source_target_pairs={{0,16},{16,32},{32,48},{48,64},{64,80},{80,96},{96,112},{112,128},... | collective-permute-start | bytes 368648 | tf_op jit(solution)/shard_map/ppermute | solution.py:10
  38.1 11.9 %copy-start.1 = (bf16[24,3,3,3,384]{4,0,3,2,1:T(8,128)(2,1)S(1)}, bf16[24,3,3,3,384]{4,0,3,2,1:T(8,128)(2,1)}, u32[]{:S(2)}) copy-start(bf16[24,3,3,3,384]{4,0,3,2,1:T(8,128)(2,1)} %param.12) | copy-start | bytes 1492996
  45.7 12.1 %all-to-all-start = ((bf16[16,2,960]{2,1,0:T(2,128)(2,1)}), bf16[16,2,960]{2,1,0:T(2,128)(2,1)S(1)}, u32[]{:S(2)}, u32[]{:S(2)}) async-start(bf16[16,2,960]{2,1,0:T(2,128)(2,1)} %reshape.137), calls=%async_computation | async-start | bytes 131072 | tf_op jit(solution)/shard_map/all_to_all | solution.py:45
  50.0 8.4 %copy-start.3 = (f32[384]{0:T(512)S(1)}, f32[384]{0:T(512)}, u32[]{:S(2)}) copy-start(f32[384]{0:T(512)} %param.11) | copy-start | bytes 4612
  81.9 10.0 %collective-permute-start.1 = (f32[16,1920]{1,0:T(8,128)S(1)}, f32[16,1920]{1,0:T(8,128)S(1)}, u32[]{:S(2)}, u32[]{:S(2)}) collective-permute-start(f32[16,1920]{1,0:T(8,128)S(1)} %reshape_reshape.7), channel_id=1, source_target_pairs={{0,16},{16,32},{32,48},{48,64},{64,80},{80,96},{96,112},{112,128},... | collective-permute-start | bytes 368648 | tf_op jit(solution)/shard_map/ppermute | solution.py:10

commit v16 on v13

--- a/solution.py
+++ b/solution.py
@@ -62,7 +62,9 @@
     full_two = lax.all_gather(normed_two, "rows", axis=1, tiled=True)
     conv_two = causal_conv(full_two, weight_two, bias_second)
     block_out = (residual.astype(jnp.float32) + conv_two).astype(jnp.bfloat16)
-    return own_row(block_out, frames, columns)
+    pieces = block_out.reshape(block_out.shape[0], frames, columns, -1)
+    placed = lax.all_to_all(pieces, "rows", split_axis=0, concat_axis=3, tiled=True)
+    return placed.reshape(frames, 1, columns, -1)
 
 
 def solution(mesh):

time: 106 us -> 107 us (level)
    all_to_all x1, waiting for transfers between devices: 6.38 us -> 7.76 us  [own_row(): lax.all_to_all(laid, 'rows', split_axis=0, concat_axis=0, tiled=True)]
  transfers between devices with their start and end apart: 3 -> 3, of which waited for: 3 -> 3; matrix products, arithmetic and copies ran while one was open for 3% -> 2% of each run, Pallas kernels for 0% -> 0%
where the time goes in v16:
time: 107 us; the launch traced here: 106 us
  blocking collectives  57.1 us (53%)
  waiting for transfers between devices  20.3 us (19%)
  local copies, waits for them, and re-layouts  9.72 us (9%)
  starting transfers between devices  9.42 us (9%)
  matrix products  6.95 us (6%)
  other arithmetic  2.48 us (2%)
    all_gather x1, blocking collectives, shards(): every_row = lax.all_gather(features, 'rows', axis=1, tiled=True)  26.8 us
    all_gather x1, blocking collectives, shards(): full_two = lax.all_gather(normed_two, 'rows', axis=1, tiled=True)  17.6 us
    all_to_all x1, blocking collectives, shards(): lax.all_to_all(pieces, 'rows', split_axis=0, concat_axis=3, tiled=True)  12.7 us
    ppermute x2, waiting for transfers between devices, passed_along(): return lax.ppermute(x, axis, pairs)  12.5 us
    all_to_all x1, waiting for transfers between devices, own_row(): lax.all_to_all(laid, 'rows', split_axis=0, concat_axis=0, tiled=True)  7.76 us
    conv_general_dilated x2, matrix products, causal_conv(): lax.conv_general_dilated(own, stacked, window_strides=(1, 1), padding=((1...  6.95 us
    ppermute x2, starting transfers between devices, passed_along(): return lax.ppermute(x, axis, pairs)  5.18 us
    all_to_all x1, starting transfers between devices, own_row(): lax.all_to_all(laid, 'rows', split_axis=0, concat_axis=0, tiled=True)  4.24 us
  transfers between devices with their start and end apart: 3, of which 3 were waited for; matrix products, arithmetic and copies ran while one was open for 2% of the time, Pallas kernels for 0%

profile of v16, /device:TPU:33, one launch (start us, length us, event | category | flops | bytes accessed | tf_op | source)
XLA Modules:
  0.0 106.3 jit_solution(15659367038536221899)
XLA Ops:
  0.0 26.8 %all_gather.6 = bf16[2,16,40,384]{3,2,0,1:T(8,128)(2,1)S(1)} all-gather(bf16[2,1,40,384]{3,2,0,1:T(8,128)(2,1)} %bitcast.89), channel_id=1, replica_groups=mesh['tm'=32,'rows'=16] {'rows'}, dimensions={1}, use_global_device_ids=true | all-gather | bytes 1044480 | tf_op jit(solution)/shard_map/all_gather | solution.py:55
  27.1 0.7 fusion.24
  28.2 0.8 copy-done
  29.0 3.5 %fusion.18 = f32[16,16,6,72]{3,1,2,0:T(8,128)S(1)} fusion(bf16[72,3,3,384]{3,0,2,1:T(8,128)(2,1)S(1)} %bitcast.88, bf16[16,2,8,8,384]{4,0,3,2,1:T(8,128)(2,1)S(1)} %fusion.10, pred[16,6]{0,1:T(8,128)(4,1)S(1)} %copy-done.4), kind=kOutput, calls=%fused_computation.21 | convolution fusion | flops 732672000 | bytes 2512992 | tf_op jit(solution)/shard_map/conv_general_dilated | solution.py:24
  32.5 0.5 copy.69
  33.0 0.4 slice_add_fusion
  33.8 0.3 reshape_reshape.6
  34.1 3.3 %collective-permute-start = (f32[16,1920]{1,0:T(8,128)S(1)}, f32[16,1920]{1,0:T(8,128)S(1)}, u32[]{:S(2)}, u32[]{:S(2)}) collective-permute-start(f32[16,1920]{1,0:T(8,128)S(1)} %reshape_reshape.6), channel_id=1, source_target_pairs={{0,16},{16,32},{32,48},{48,64},{64,80},{80,96},{96,112},{112,128},... | collective-permute-start | bytes 368648 | tf_op jit(solution)/shard_map/ppermute | solution.py:10
  37.8 0.8 dynamic_slice.10
  38.7 5.5 %collective-permute-done = f32[16,1920]{1,0:T(8,128)S(1)} collective-permute-done((f32[16,1920]{1,0:T(8,128)S(1)}, f32[16,1920]{1,0:T(8,128)S(1)}, u32[]{:S(2)}, u32[]{:S(2)}) %collective-permute-start) | collective-permute-done | bytes 122912 | tf_op jit(solution)/shard_map/ppermute | solution.py:10
  44.4 0.7 copy.73
  45.1 4.2 %all-to-all-start = ((bf16[16,2,960]{2,1,0:T(2,128)(2,1)}), bf16[16,2,960]{2,1,0:T(2,128)(2,1)S(1)}, u32[]{:S(2)}, u32[]{:S(2)}) async-start(bf16[16,2,960]{2,1,0:T(2,128)(2,1)} %copy.73), calls=%async_computation | async-start | bytes 131072 | tf_op jit(solution)/shard_map/all_to_all | solution.py:44
  49.4 7.8 %all-to-all-done = bf16[16,2,960]{2,1,0:T(2,128)(2,1)S(1)} async-done(((bf16[16,2,960]{2,1,0:T(2,128)(2,1)}), bf16[16,2,960]{2,1,0:T(2,128)(2,1)S(1)}, u32[]{:S(2)}, u32[]{:S(2)}) %all-to-all-start) | async-done | bytes 61472 | tf_op jit(solution)/shard_map/all_to_all | solution.py:44
  58.2 17.6 %all_gather.7 = bf16[2,16,40,384]{3,2,0,1:T(8,128)(2,1)S(1)} all-gather(bf16[2,1,40,384]{3,2,0,1:T(8,128)(2,1)S(1)} %fusion.31), channel_id=1, replica_groups=mesh['tm'=32,'rows'=16] {'rows'}, dimensions={1}, use_global_device_ids=true | all-gather | bytes 1044480 | tf_op jit(solution)/shard_map/all_gather | solution.py:62
  76.5 3.5 %fusion.21 = f32[16,16,6,72]{3,1,2,0:T(8,128)S(1)} fusion(bf16[72,3,3,384]{3,0,2,1:T(8,128)(2,1)S(1)} %bitcast.87, bf16[16,2,8,8,384]{4,0,3,2,1:T(8,128)(2,1)S(1)} %fusion.11, pred[16,6]{0,1:T(8,128)(4,1)S(1)} %copy-done.4), kind=kOutput, calls=%fused_computation.22 | convolution fusion | flops 732672000 | bytes 2512992 | tf_op jit(solution)/shard_map/conv_general_dilated | solution.py:24
  80.0 0.5 copy.81
  80.5 0.4 copy.88
  81.3 0.3 reshape_reshape.7
  81.6 1.9 %collective-permute-start.1 = (f32[16,1920]{1,0:T(8,128)S(1)}, f32[16,1920]{1,0:T(8,128)S(1)}, u32[]{:S(2)}, u32[]{:S(2)}) collective-permute-start(f32[16,1920]{1,0:T(8,128)S(1)} %reshape_reshape.7), channel_id=1, source_target_pairs={{0,16},{16,32},{32,48},{48,64},{64,80},{80,96},{96,112},{112,128},... | collective-permute-start | bytes 368648 | tf_op jit(solution)/shard_map/ppermute | solution.py:10
  83.9 0.8 dynamic_slice.11
  84.6 7.0 %collective-permute-done.1 = f32[16,1920]{1,0:T(8,128)S(1)} collective-permute-done((f32[16,1920]{1,0:T(8,128)S(1)}, f32[16,1920]{1,0:T(8,128)S(1)}, u32[]{:S(2)}, u32[]{:S(2)}) %collective-permute-start.1) | collective-permute-done | bytes 122912 | tf_op jit(solution)/shard_map/ppermute | solution.py:10
  91.6 0.4 reshape.113
  92.6 12.7 %all_to_all.20 = bf16[16,2,960]{2,1,0:T(2,128)(2,1)S(1)} all-to-all(bf16[16,2,960]{2,1,0:T(2,128)(2,1)S(1)} %reshape.137), channel_id=1, replica_groups=mesh['tm'=32,'rows'=16] {'rows'}, dimensions={0} | all-to-all | bytes 122880 | tf_op jit(solution)/shard_map/all_to_all | solution.py:66
  105.6 0.7 copy.86
  (50 shorter events, 5.0 us)
Async XLA Ops:
  0.0 27.1 %copy-start.2 = (f32[384]{0:T(512)S(1)}, f32[384]{0:T(512)}, u32[]{:S(2)}) copy-start(f32[384]{0:T(512)} %param.8) | copy-start | bytes 4612
  27.9 1.0 copy-start
  28.0 1.1 %copy-start.4 = (pred[16,6]{0,1:T(8,128)(4,1)S(1)}, pred[16,6]{0,1:T(8,128)(4,1)}, u32[]{:S(2)}) copy-start(pred[16,6]{0,1:T(8,128)(4,1)} %constant.36) | copy-start | bytes 292
  34.1 15.3 %copy-start.1 = (bf16[24,3,3,3,384]{4,0,3,2,1:T(8,128)(2,1)S(1)}, bf16[24,3,3,3,384]{4,0,3,2,1:T(8,128)(2,1)}, u32[]{:S(2)}) copy-start(bf16[24,3,3,3,384]{4,0,3,2,1:T(8,128)(2,1)} %param.12) | copy-start | bytes 1492996
  34.1 10.1 %collective-permute-start = (f32[16,1920]{1,0:T(8,128)S(1)}, f32[16,1920]{1,0:T(8,128)S(1)}, u32[]{:S(2)}, u32[]{:S(2)}) collective-permute-start(f32[16,1920]{1,0:T(8,128)S(1)} %reshape_reshape.6), channel_id=1, source_target_pairs={{0,16},{16,32},{32,48},{48,64},{64,80},{80,96},{96,112},{112,128},... | collective-permute-start | bytes 368648 | tf_op jit(solution)/shard_map/ppermute | solution.py:10
  45.1 12.1 %all-to-all-start = ((bf16[16,2,960]{2,1,0:T(2,128)(2,1)}), bf16[16,2,960]{2,1,0:T(2,128)(2,1)S(1)}, u32[]{:S(2)}, u32[]{:S(2)}) async-start(bf16[16,2,960]{2,1,0:T(2,128)(2,1)} %copy.73), calls=%async_computation | async-start | bytes 131072 | tf_op jit(solution)/shard_map/all_to_all | solution.py:44
  49.4 8.7 %copy-start.3 = (f32[384]{0:T(512)S(1)}, f32[384]{0:T(512)}, u32[]{:S(2)}) copy-start(f32[384]{0:T(512)} %param.11) | copy-start | bytes 4612
  81.6 10.0 %collective-permute-start.1 = (f32[16,1920]{1,0:T(8,128)S(1)}, f32[16,1920]{1,0:T(8,128)S(1)}, u32[]{:S(2)}, u32[]{:S(2)}) collective-permute-start(f32[16,1920]{1,0:T(8,128)S(1)} %reshape_reshape.7), channel_id=1, source_target_pairs={{0,16},{16,32},{32,48},{48,64},{64,80},{80,96},{96,112},{112,128},... | collective-permute-start | bytes 368648 | tf_op jit(solution)/shard_map/ppermute | solution.py:10

commit v17 on v14

--- a/solution.py
+++ b/solution.py
@@ -20,16 +20,23 @@
 def causal_conv(own, kernel, bias_part):
     part_width = kernel.shape[0]
     frames, height, columns, _ = own.shape
-    stacked = jnp.transpose(kernel, (1, 0, 2, 3, 4)).reshape(3 * part_width, 3, 3, kernel.shape[4])
+    stacked = jnp.transpose(kernel, (1, 2, 0, 3, 4)).reshape(9 * part_width, 1, 3, kernel.shape[4])
     product = lax.conv_general_dilated(
         own,
         stacked,
         window_strides=(1, 1),
-        padding=((1, 1), (1, 1)),
+        padding=((0, 0), (1, 1)),
         dimension_numbers=("NHWC", "OHWI", "HNWC"),
         preferred_element_type=jnp.float32,
     )
-    tap = [product[..., a * part_width : (a + 1) * part_width] for a in range(3)]
+    padded = jnp.pad(product, ((1, 1), (0, 0), (0, 0), (0, 0)))
+    tap = []
+    for a in range(3):
+        summed = 0
+        for b in range(3):
+            at = (a * 3 + b) * part_width
+            summed = summed + padded[b : b + height, :, :, at : at + part_width]
+        tap.append(summed)
 
     def rows_first(pair):
         return jnp.stack(pair, 1).reshape(height, frames, -1)

time: 106 us -> 109 us (1.028)
  other arithmetic: 2.9 us -> 5.59 us
  local copies, waits for them, and re-layouts: 9.48 us -> 12 us
  matrix products: 6.93 us -> 4.51 us
    add x0 -> x2, other arithmetic: none -> 3.24 us  [causal_conv(): summed = summed + padded[b:b + height, :, :, at:at + part_width]]
    add x0 -> x6, local copies, waits for them, and re-layouts: none -> 2.76 us  [causal_conv(): summed = summed + padded[b:b + height, :, :, at:at + part_width]]
    conv_general_dilated x2, matrix products: 6.93 us -> 4.51 us  [causal_conv(): lax.conv_general_dilated(own, stacked, window_strides=(1, 1), padding=((0...]
where the time goes in v17:
time: 109 us; the launch traced here: 108 us
  blocking collectives  57.1 us (52%)
  waiting for transfers between devices  19.3 us (18%)
  local copies, waits for them, and re-layouts  12 us (11%)
  starting transfers between devices  9.4 us (9%)
  other arithmetic  5.59 us (5%)
  matrix products  4.51 us (4%)
    all_gather x1, blocking collectives, shards(): every_row = lax.all_gather(features, 'rows', axis=1, tiled=True)  26.7 us
    all_gather x1, blocking collectives, shards(): full_two = lax.all_gather(normed_two, 'rows', axis=1, tiled=True)  17.6 us
    all_to_all x1, blocking collectives, own_row(): lax.all_to_all(laid, 'rows', split_axis=0, concat_axis=0, tiled=True)  12.7 us
    ppermute x2, waiting for transfers between devices, passed_along(): return lax.ppermute(x, axis, pairs)  12.4 us
    all_to_all x1, waiting for transfers between devices, own_row(): lax.all_to_all(laid, 'rows', split_axis=0, concat_axis=0, tiled=True)  6.91 us
    ppermute x2, starting transfers between devices, passed_along(): return lax.ppermute(x, axis, pairs)  5.16 us
    conv_general_dilated x2, matrix products, causal_conv(): lax.conv_general_dilated(own, stacked, window_strides=(1, 1), padding=((0...  4.51 us
    all_to_all x1, starting transfers between devices, own_row(): lax.all_to_all(laid, 'rows', split_axis=0, concat_axis=0, tiled=True)  4.24 us
  transfers between devices with their start and end apart: 3, of which 3 were waited for; matrix products, arithmetic and copies ran while one was open for 3% of the time, Pallas kernels for 0%

profile of v17, /device:TPU:33, one launch (start us, length us, event | category | flops | bytes accessed | tf_op | source)
XLA Modules:
  0.0 108.3 jit_solution(13752607532250116121)
XLA Ops:
  0.0 1.1 %copy.68 = bf16[24,3,3,3,384]{4,0,2,1,3:T(8,128)(2,1)S(1)} copy(bf16[24,3,3,3,384]{4,0,3,2,1:T(8,128)(2,1)} %param.9) | data formatting | bytes 995328 | tf_op args[2]
  1.1 26.7 %all_gather.6 = bf16[2,16,40,384]{3,2,0,1:T(8,128)(2,1)S(1)} all-gather(bf16[2,1,40,384]{3,2,0,1:T(8,128)(2,1)} %bitcast.83), channel_id=1, replica_groups=mesh['tm'=32,'rows'=16] {'rows'}, dimensions={1}, use_global_device_ids=true | all-gather | bytes 1044480 | tf_op jit(solution)/shard_map/all_gather | solution.py:62
  28.1 0.7 fusion.24
  29.6 2.3 %fusion.18 = f32[16,16,6,216]{3,1,2,0:T(8,128)S(1)} fusion(bf16[216,1,3,384]{3,0,2,1:T(8,128)(2,1)S(1)} %bitcast.82, bf16[16,2,8,8,384]{4,0,3,2,1:T(8,128)(2,1)S(1)} %fusion.10, pred[16,6]{0,1:T(8,128)(4,1)S(1)} %copy-done.3), kind=kOutput, calls=%fused_computation.33 | convolution fusion | flops 764743680 | bytes 3397728 | tf_op jit(solution)/shard_map/conv_general_dilated | solution.py:24
  31.9 1.6 %fusion.30 = (f32[16,16,6,24]{3,1,2,0:T(8,128)S(1)}, f32[16,16,6,24]{3,1,2,0:T(8,128)S(1)}, f32[16,16,6,24]{3,1,2,0:T(8,128)S(1)}) fusion(f32[16,16,6,216]{3,1,2,0:T(8,128)S(1)} %fusion.18), kind=kLoop, calls=%fused_computation.42 | loop fusion | flops 221184 | bytes 4374528 | tf_op jit(solution)/shard_map/add | solution.py:38
  33.5 0.5 copy.73
  34.0 0.5 copy.71
  34.4 0.5 copy.69
  35.6 3.2 %collective-permute-start = (f32[16,1920]{1,0:T(8,128)S(1)}, f32[16,1920]{1,0:T(8,128)S(1)}, u32[]{:S(2)}, u32[]{:S(2)}) collective-permute-start(f32[16,1920]{1,0:T(8,128)S(1)} %reshape_reshape.6), channel_id=1, source_target_pairs={{0,16},{16,32},{32,48},{48,64},{64,80},{80,96},{96,112},{112,128},... | collective-permute-start | bytes 368648 | tf_op jit(solution)/shard_map/ppermute | solution.py:10
  38.9 0.8 dynamic_slice.10
  40.3 5.5 %collective-permute-done = f32[16,1920]{1,0:T(8,128)S(1)} collective-permute-done((f32[16,1920]{1,0:T(8,128)S(1)}, f32[16,1920]{1,0:T(8,128)S(1)}, u32[]{:S(2)}, u32[]{:S(2)}) %collective-permute-start) | collective-permute-done | bytes 122912 | tf_op jit(solution)/shard_map/ppermute | solution.py:10
  46.0 0.7 copy.76
  46.7 4.2 %all-to-all-start = ((bf16[16,2,960]{2,1,0:T(2,128)(2,1)}), bf16[16,2,960]{2,1,0:T(2,128)(2,1)S(1)}, u32[]{:S(2)}, u32[]{:S(2)}) async-start(bf16[16,2,960]{2,1,0:T(2,128)(2,1)} %copy.76), calls=%async_computation | async-start | bytes 131072 | tf_op jit(solution)/shard_map/all_to_all | solution.py:51
  50.9 0.8 dynamic_slice.11
  51.8 6.9 %all-to-all-done = bf16[16,2,960]{2,1,0:T(2,128)(2,1)S(1)} async-done(((bf16[16,2,960]{2,1,0:T(2,128)(2,1)}), bf16[16,2,960]{2,1,0:T(2,128)(2,1)S(1)}, u32[]{:S(2)}, u32[]{:S(2)}) %all-to-all-start) | async-done | bytes 61472 | tf_op jit(solution)/shard_map/all_to_all | solution.py:51
  59.8 17.6 %all_gather.7 = bf16[2,16,40,384]{3,2,0,1:T(8,128)(2,1)S(1)} all-gather(bf16[2,1,40,384]{3,2,0,1:T(8,128)(2,1)S(1)} %fusion.42), channel_id=1, replica_groups=mesh['tm'=32,'rows'=16] {'rows'}, dimensions={1}, use_global_device_ids=true | all-gather | bytes 1044480 | tf_op jit(solution)/shard_map/all_gather | solution.py:69
  78.0 2.3 %fusion.21 = f32[16,16,6,216]{3,1,2,0:T(8,128)S(1)} fusion(bf16[216,1,3,384]{3,0,2,1:T(8,128)(2,1)S(1)} %bitcast.81, bf16[16,2,8,8,384]{4,0,3,2,1:T(8,128)(2,1)S(1)} %fusion.11, pred[16,6]{0,1:T(8,128)(4,1)S(1)} %copy-done.3), kind=kOutput, calls=%fused_computation.34 | convolution fusion | flops 764743680 | bytes 3397728 | tf_op jit(solution)/shard_map/conv_general_dilated | solution.py:24
  80.3 1.6 %fusion.36 = (f32[16,16,6,24]{3,1,2,0:T(8,128)S(1)}, f32[16,16,6,24]{3,1,2,0:T(8,128)S(1)}, f32[16,16,6,24]{3,1,2,0:T(8,128)S(1)}) fusion(f32[16,16,6,216]{3,1,2,0:T(8,128)S(1)} %fusion.21), kind=kLoop, calls=%fused_computation.48 | loop fusion | flops 221184 | bytes 4374528 | tf_op jit(solution)/shard_map/add | solution.py:38
  81.9 0.5 copy.88
  82.4 0.5 copy.86
  84.0 1.9 %collective-permute-start.1 = (f32[16,1920]{1,0:T(8,128)S(1)}, f32[16,1920]{1,0:T(8,128)S(1)}, u32[]{:S(2)}, u32[]{:S(2)}) collective-permute-start(f32[16,1920]{1,0:T(8,128)S(1)} %reshape_reshape.7), channel_id=1, source_target_pairs={{0,16},{16,32},{32,48},{48,64},{64,80},{80,96},{96,112},{112,128},... | collective-permute-start | bytes 368648 | tf_op jit(solution)/shard_map/ppermute | solution.py:10
  87.1 6.9 %collective-permute-done.1 = f32[16,1920]{1,0:T(8,128)S(1)} collective-permute-done((f32[16,1920]{1,0:T(8,128)S(1)}, f32[16,1920]{1,0:T(8,128)S(1)}, u32[]{:S(2)}, u32[]{:S(2)}) %collective-permute-start.1) | collective-permute-done | bytes 122912 | tf_op jit(solution)/shard_map/ppermute | solution.py:10
  94.3 12.7 %all_to_all.10 = bf16[16,2,960]{2,1,0:T(2,128)(2,1)S(1)} all-to-all(bf16[16,2,960]{2,1,0:T(2,128)(2,1)S(1)} %copy.91), channel_id=1, replica_groups=mesh['tm'=32,'rows'=16] {'rows'}, dimensions={0} | all-to-all | bytes 122880 | tf_op jit(solution)/shard_map/all_to_all | solution.py:51
  107.6 0.7 copy.94
  (58 shorter events, 7.4 us)
Async XLA Ops:
  0.0 28.1 %copy-start.1 = (f32[384]{0:T(512)S(1)}, f32[384]{0:T(512)}, u32[]{:S(2)}) copy-start(f32[384]{0:T(512)} %param.8) | copy-start | bytes 4612
  28.9 0.7 copy-start.3
  35.6 16.1 %copy-start = (bf16[24,3,3,3,384]{4,0,3,2,1:T(8,128)(2,1)S(1)}, bf16[24,3,3,3,384]{4,0,3,2,1:T(8,128)(2,1)}, u32[]{:S(2)}) copy-start(bf16[24,3,3,3,384]{4,0,3,2,1:T(8,128)(2,1)} %param.12) | copy-start | bytes 1492996
  35.6 10.1 %collective-permute-start = (f32[16,1920]{1,0:T(8,128)S(1)}, f32[16,1920]{1,0:T(8,128)S(1)}, u32[]{:S(2)}, u32[]{:S(2)}) collective-permute-start(f32[16,1920]{1,0:T(8,128)S(1)} %reshape_reshape.6), channel_id=1, source_target_pairs={{0,16},{16,32},{32,48},{48,64},{64,80},{80,96},{96,112},{112,128},... | collective-permute-start | bytes 368648 | tf_op jit(solution)/shard_map/ppermute | solution.py:10
  46.7 12.1 %all-to-all-start = ((bf16[16,2,960]{2,1,0:T(2,128)(2,1)}), bf16[16,2,960]{2,1,0:T(2,128)(2,1)S(1)}, u32[]{:S(2)}, u32[]{:S(2)}) async-start(bf16[16,2,960]{2,1,0:T(2,128)(2,1)} %copy.76), calls=%async_computation | async-start | bytes 131072 | tf_op jit(solution)/shard_map/all_to_all | solution.py:51
  51.8 7.8 %copy-start.2 = (f32[384]{0:T(512)S(1)}, f32[384]{0:T(512)}, u32[]{:S(2)}) copy-start(f32[384]{0:T(512)} %param.11) | copy-start | bytes 4612
  84.0 10.0 %collective-permute-start.1 = (f32[16,1920]{1,0:T(8,128)S(1)}, f32[16,1920]{1,0:T(8,128)S(1)}, u32[]{:S(2)}, u32[]{:S(2)}) collective-permute-start(f32[16,1920]{1,0:T(8,128)S(1)} %reshape_reshape.7), channel_id=1, source_target_pairs={{0,16},{16,32},{32,48},{48,64},{64,80},{80,96},{96,112},{112,128},... | collective-permute-start | bytes 368648 | tf_op jit(solution)/shard_map/ppermute | solution.py:10

commit v18 on v13

--- a/solution.py
+++ b/solution.py
@@ -17,10 +17,13 @@
     return jax.nn.silu(scaled).astype(jnp.bfloat16)
 
 
-def causal_conv(own, kernel, bias_part):
-    part_width = kernel.shape[0]
+def stack_taps(kernel):
+    return jnp.transpose(kernel, (1, 0, 2, 3, 4)).reshape(3 * kernel.shape[0], 3, 3, kernel.shape[4])
+
+
+def causal_conv(own, stacked, bias_part):
+    part_width = stacked.shape[0] // 3
     frames, height, columns, _ = own.shape
-    stacked = jnp.transpose(kernel, (1, 0, 2, 3, 4)).reshape(3 * part_width, 3, 3, kernel.shape[4])
     product = lax.conv_general_dilated(
         own,
         stacked,
@@ -52,15 +55,17 @@
     offset = lax.axis_index("rows") * part_width
     bias_first = lax.dynamic_slice_in_dim(bias_one, offset, part_width, 0)
     bias_second = lax.dynamic_slice_in_dim(bias_two, offset, part_width, 0)
+    stacked_one = stack_taps(weight_one)
+    features, stacked_one = lax.optimization_barrier((features, stacked_one))
     every_row = lax.all_gather(features, "rows", axis=1, tiled=True)
     full_one = norm_silu(every_row, gain_one)
     residual = lax.dynamic_slice_in_dim(every_row, offset, part_width, 3)
     residual = jnp.transpose(residual, (1, 0, 2, 3)).reshape(residual.shape[1], frames, -1)
-    conv_one = causal_conv(full_one, weight_one, bias_first).astype(jnp.bfloat16)
+    conv_one = causal_conv(full_one, stacked_one, bias_first).astype(jnp.bfloat16)
     own_rows = own_row(conv_one, frames, columns)
     normed_two = norm_silu(own_rows, gain_two)
     full_two = lax.all_gather(normed_two, "rows", axis=1, tiled=True)
-    conv_two = causal_conv(full_two, weight_two, bias_second)
+    conv_two = causal_conv(full_two, stack_taps(weight_two), bias_second)
     block_out = (residual.astype(jnp.float32) + conv_two).astype(jnp.bfloat16)
     return own_row(block_out, frames, columns)
 

time: 106 us -> 106 us (level)
  no operation moved by 1% of the time
where the time goes in v18:
time: 106 us
  blocking collectives  57.1 us (54%)
  waiting for transfers between devices  19.4 us (18%)
  local copies, waits for them, and re-layouts  10.1 us (10%)
  starting transfers between devices  9.29 us (9%)
  matrix products  6.93 us (7%)
  other arithmetic  2.99 us (3%)
    all_gather x1, blocking collectives, shards(): every_row = lax.all_gather(features, 'rows', axis=1, tiled=True)  26.7 us
    all_gather x1, blocking collectives, shards(): full_two = lax.all_gather(normed_two, 'rows', axis=1, tiled=True)  17.6 us
    ppermute x2, waiting for transfers between devices, passed_along(): return lax.ppermute(x, axis, pairs)  13.1 us
    all_to_all x1, blocking collectives, own_row(): lax.all_to_all(laid, 'rows', split_axis=0, concat_axis=0, tiled=True)  12.7 us
    conv_general_dilated x2, matrix products, causal_conv(): lax.conv_general_dilated(own, stacked, window_strides=(1, 1), padding=((1...  6.93 us
    all_to_all x1, waiting for transfers between devices, own_row(): lax.all_to_all(laid, 'rows', split_axis=0, concat_axis=0, tiled=True)  6.31 us
    ppermute x2, starting transfers between devices, passed_along(): return lax.ppermute(x, axis, pairs)  5.03 us
    all_to_all x1, starting transfers between devices, own_row(): lax.all_to_all(laid, 'rows', split_axis=0, concat_axis=0, tiled=True)  4.26 us
  transfers between devices with their start and end apart: 3, of which 3 were waited for; matrix products, arithmetic and copies ran while one was open for 3% of the time, Pallas kernels for 0%

profile of v18, /device:TPU:33, one launch (start us, length us, event | category | flops | bytes accessed | tf_op | source)
XLA Modules:
  0.0 106.2 jit_solution(15077377978590975277)
XLA Ops:
  0.0 1.1 %copy.69 = bf16[24,3,3,3,384]{4,0,1,3,2:T(8,128)(2,1)S(1)} copy(bf16[24,3,3,3,384]{4,0,3,2,1:T(8,128)(2,1)} %param.9) | data formatting | bytes 995328 | tf_op args[2]
  1.1 26.7 %all_gather.6 = bf16[2,16,40,384]{3,2,0,1:T(8,128)(2,1)S(1)} all-gather(bf16[2,1,40,384]{3,2,0,1:T(8,128)(2,1)} %bitcast.79), channel_id=1, replica_groups=mesh['tm'=32,'rows'=16] {'rows'}, dimensions={1}, use_global_device_ids=true | all-gather | bytes 1044480 | tf_op jit(solution)/shard_map/all_gather | solution.py:60
  28.1 0.7 fusion.24
  29.2 0.4 copy-done.3
  29.6 3.5 %fusion.18 = f32[16,16,6,72]{3,1,2,0:T(8,128)S(1)} fusion(bf16[72,3,3,384]{3,0,2,1:T(8,128)(2,1)S(1)} %bitcast.78, bf16[16,2,8,8,384]{4,0,3,2,1:T(8,128)(2,1)S(1)} %fusion.10, pred[16,6]{0,1:T(8,128)(4,1)S(1)} %copy-done.3), kind=kOutput, calls=%fused_computation.21 | convolution fusion | flops 732672000 | bytes 2512992 | tf_op jit(solution)/shard_map/conv_general_dilated | solution.py:27
  33.1 0.5 copy.74
  33.6 0.4 slice_add_fusion.2
  34.6 3.1 %collective-permute-start = (f32[16,1920]{1,0:T(8,128)S(1)}, f32[16,1920]{1,0:T(8,128)S(1)}, u32[]{:S(2)}, u32[]{:S(2)}) collective-permute-start(f32[16,1920]{1,0:T(8,128)S(1)} %reshape_reshape.6), channel_id=1, source_target_pairs={{0,16},{16,32},{32,48},{48,64},{64,80},{80,96},{96,112},{112,128},... | collective-permute-start | bytes 368648 | tf_op jit(solution)/shard_map/ppermute | solution.py:10
  38.2 0.8 dynamic_slice.10
  39.1 5.5 %collective-permute-done = f32[16,1920]{1,0:T(8,128)S(1)} collective-permute-done((f32[16,1920]{1,0:T(8,128)S(1)}, f32[16,1920]{1,0:T(8,128)S(1)}, u32[]{:S(2)}, u32[]{:S(2)}) %collective-permute-start) | collective-permute-done | bytes 122912 | tf_op jit(solution)/shard_map/ppermute | solution.py:10
  44.8 0.7 copy.78
  45.5 4.3 %all-to-all-start = ((bf16[16,2,960]{2,1,0:T(2,128)(2,1)}), bf16[16,2,960]{2,1,0:T(2,128)(2,1)S(1)}, u32[]{:S(2)}, u32[]{:S(2)}) async-start(bf16[16,2,960]{2,1,0:T(2,128)(2,1)} %copy.78), calls=%async_computation | async-start | bytes 131072 | tf_op jit(solution)/shard_map/all_to_all | solution.py:47
  49.9 0.4 reshape.142
  50.4 0.8 dynamic_slice.11
  51.3 6.3 %all-to-all-done = bf16[16,2,960]{2,1,0:T(2,128)(2,1)S(1)} async-done(((bf16[16,2,960]{2,1,0:T(2,128)(2,1)}), bf16[16,2,960]{2,1,0:T(2,128)(2,1)S(1)}, u32[]{:S(2)}, u32[]{:S(2)}) %all-to-all-start) | async-done | bytes 61472 | tf_op jit(solution)/shard_map/all_to_all | solution.py:47
  58.6 17.6 %all_gather.7 = bf16[2,16,40,384]{3,2,0,1:T(8,128)(2,1)S(1)} all-gather(bf16[2,1,40,384]{3,2,0,1:T(8,128)(2,1)S(1)} %fusion.29), channel_id=1, replica_groups=mesh['tm'=32,'rows'=16] {'rows'}, dimensions={1}, use_global_device_ids=true | all-gather | bytes 1044480 | tf_op jit(solution)/shard_map/all_gather | solution.py:67
  76.9 3.5 %fusion.21 = f32[16,16,6,72]{3,1,2,0:T(8,128)S(1)} fusion(bf16[72,3,3,384]{3,0,2,1:T(8,128)(2,1)S(1)} %bitcast.77, bf16[16,2,8,8,384]{4,0,3,2,1:T(8,128)(2,1)S(1)} %fusion.11, pred[16,6]{0,1:T(8,128)(4,1)S(1)} %copy-done.3), kind=kOutput, calls=%fused_computation.22 | convolution fusion | flops 732672000 | bytes 2512992 | tf_op jit(solution)/shard_map/conv_general_dilated | solution.py:27
  80.4 0.5 copy.86
  80.9 0.4 slice_add_fusion
  81.6 0.3 reshape_reshape.7
  81.9 1.9 %collective-permute-start.1 = (f32[16,1920]{1,0:T(8,128)S(1)}, f32[16,1920]{1,0:T(8,128)S(1)}, u32[]{:S(2)}, u32[]{:S(2)}) collective-permute-start(f32[16,1920]{1,0:T(8,128)S(1)} %reshape_reshape.7), channel_id=1, source_target_pairs={{0,16},{16,32},{32,48},{48,64},{64,80},{80,96},{96,112},{112,128},... | collective-permute-start | bytes 368648 | tf_op jit(solution)/shard_map/ppermute | solution.py:10
  84.3 7.6 %collective-permute-done.1 = f32[16,1920]{1,0:T(8,128)S(1)} collective-permute-done((f32[16,1920]{1,0:T(8,128)S(1)}, f32[16,1920]{1,0:T(8,128)S(1)}, u32[]{:S(2)}, u32[]{:S(2)}) %collective-permute-start.1) | collective-permute-done | bytes 122912 | tf_op jit(solution)/shard_map/ppermute | solution.py:10
  92.2 12.7 %all_to_all.10 = bf16[16,2,960]{2,1,0:T(2,128)(2,1)S(1)} all-to-all(bf16[16,2,960]{2,1,0:T(2,128)(2,1)S(1)} %copy.90), channel_id=1, replica_groups=mesh['tm'=32,'rows'=16] {'rows'}, dimensions={0} | all-to-all | bytes 122880 | tf_op jit(solution)/shard_map/all_to_all | solution.py:47
  105.4 0.7 copy.93
  (51 shorter events, 5.5 us)
Async XLA Ops:
  0.0 28.1 %copy-start.1 = (f32[384]{0:T(512)S(1)}, f32[384]{0:T(512)}, u32[]{:S(2)}) copy-start(f32[384]{0:T(512)} %param.8) | copy-start | bytes 4612
  28.9 0.7 copy-start.3
  34.6 10.0 %collective-permute-start = (f32[16,1920]{1,0:T(8,128)S(1)}, f32[16,1920]{1,0:T(8,128)S(1)}, u32[]{:S(2)}, u32[]{:S(2)}) collective-permute-start(f32[16,1920]{1,0:T(8,128)S(1)} %reshape_reshape.6), channel_id=1, source_target_pairs={{0,16},{16,32},{32,48},{48,64},{64,80},{80,96},{96,112},{112,128},... | collective-permute-start | bytes 368648 | tf_op jit(solution)/shard_map/ppermute | solution.py:10
  38.0 12.4 %copy-start = (bf16[24,3,3,3,384]{4,0,3,2,1:T(8,128)(2,1)S(1)}, bf16[24,3,3,3,384]{4,0,3,2,1:T(8,128)(2,1)}, u32[]{:S(2)}) copy-start(bf16[24,3,3,3,384]{4,0,3,2,1:T(8,128)(2,1)} %param.12) | copy-start | bytes 1492996
  45.5 12.1 %all-to-all-start = ((bf16[16,2,960]{2,1,0:T(2,128)(2,1)}), bf16[16,2,960]{2,1,0:T(2,128)(2,1)S(1)}, u32[]{:S(2)}, u32[]{:S(2)}) async-start(bf16[16,2,960]{2,1,0:T(2,128)(2,1)} %copy.78), calls=%async_computation | async-start | bytes 131072 | tf_op jit(solution)/shard_map/all_to_all | solution.py:47
  50.4 8.1 %copy-start.2 = (f32[384]{0:T(512)S(1)}, f32[384]{0:T(512)}, u32[]{:S(2)}) copy-start(f32[384]{0:T(512)} %param.11) | copy-start | bytes 4612
  81.9 10.0 %collective-permute-start.1 = (f32[16,1920]{1,0:T(8,128)S(1)}, f32[16,1920]{1,0:T(8,128)S(1)}, u32[]{:S(2)}, u32[]{:S(2)}) collective-permute-start(f32[16,1920]{1,0:T(8,128)S(1)} %reshape_reshape.7), channel_id=1, source_target_pairs={{0,16},{16,32},{32,48},{48,64},{64,80},{80,96},{96,112},{112,128},... | collective-permute-start | bytes 368648 | tf_op jit(solution)/shard_map/ppermute | solution.py:10

commit v19 on v13

--- a/solution.py
+++ b/solution.py
@@ -35,9 +35,10 @@
         return jnp.transpose(jnp.stack(pair, 0), (1, 0, 2, 3)).reshape(height, frames, -1)
 
     onward = rows_first([tap[0][0] + tap[1][1], tap[0][1]])
-    kept = rows_first([tap[2][0], tap[1][0] + tap[2][1]])
+    kept = rows_first([tap[2][0], tap[1][0] + tap[2][1]]) + jnp.tile(bias_part, columns)
+    kept = lax.optimization_barrier(kept)
     arrived = passed_along(onward.reshape(height, -1), "tm", 1).reshape(kept.shape)
-    return kept + arrived + jnp.tile(bias_part, columns)
+    return kept + arrived
 
 
 def own_row(laid, frames, columns):

time: 106 us -> 106 us (level)
  no operation moved by 1% of the time
where the time goes in v19:
time: 106 us
  blocking collectives  57.1 us (54%)
  waiting for transfers between devices  19.4 us (18%)
  local copies, waits for them, and re-layouts  9.42 us (9%)
  starting transfers between devices  9.28 us (9%)
  matrix products  6.95 us (7%)
  other arithmetic  3.01 us (3%)
    all_gather x1, blocking collectives, shards(): every_row = lax.all_gather(features, 'rows', axis=1, tiled=True)  26.8 us
    all_gather x1, blocking collectives, shards(): full_two = lax.all_gather(normed_two, 'rows', axis=1, tiled=True)  17.6 us
    all_to_all x1, blocking collectives, own_row(): lax.all_to_all(laid, 'rows', split_axis=0, concat_axis=0, tiled=True)  12.7 us
    ppermute x2, waiting for transfers between devices, passed_along(): return lax.ppermute(x, axis, pairs)  12.1 us
    all_to_all x1, waiting for transfers between devices, own_row(): lax.all_to_all(laid, 'rows', split_axis=0, concat_axis=0, tiled=True)  7.24 us
    conv_general_dilated x2, matrix products, causal_conv(): lax.conv_general_dilated(own, stacked, window_strides=(1, 1), padding=((1...  6.95 us
    ppermute x2, starting transfers between devices, passed_along(): return lax.ppermute(x, axis, pairs)  5.04 us
    all_to_all x1, starting transfers between devices, own_row(): lax.all_to_all(laid, 'rows', split_axis=0, concat_axis=0, tiled=True)  4.24 us
  transfers between devices with their start and end apart: 3, of which 3 were waited for; matrix products, arithmetic and copies ran while one was open for 3% of the time, Pallas kernels for 0%

profile of v19, /device:TPU:33, one launch (start us, length us, event | category | flops | bytes accessed | tf_op | source)
XLA Modules:
  0.0 105.6 jit_solution(14117151031554257215)
XLA Ops:
  0.0 26.8 %all_gather.6 = bf16[2,16,40,384]{3,2,0,1:T(8,128)(2,1)S(1)} all-gather(bf16[2,1,40,384]{3,2,0,1:T(8,128)(2,1)} %bitcast.79), channel_id=1, replica_groups=mesh['tm'=32,'rows'=16] {'rows'}, dimensions={1}, use_global_device_ids=true | all-gather | bytes 1044480 | tf_op jit(solution)/shard_map/all_gather | solution.py:56
  27.1 0.7 fusion.24
  28.2 0.8 copy-done
  29.0 3.5 %fusion.18 = f32[16,16,6,72]{3,1,2,0:T(8,128)S(1)} fusion(bf16[72,3,3,384]{3,0,2,1:T(8,128)(2,1)S(1)} %bitcast.78, bf16[16,2,8,8,384]{4,0,3,2,1:T(8,128)(2,1)S(1)} %fusion.10, pred[16,6]{0,1:T(8,128)(4,1)S(1)} %copy-done.4), kind=kOutput, calls=%fused_computation.21 | convolution fusion | flops 732672000 | bytes 2512992 | tf_op jit(solution)/shard_map/conv_general_dilated | solution.py:24
  32.5 0.5 copy.74
  33.0 0.4 slice_add_fusion.2
  33.8 0.3 reshape_reshape.6
  34.1 3.1 %collective-permute-start = (f32[16,1920]{1,0:T(8,128)S(1)}, f32[16,1920]{1,0:T(8,128)S(1)}, u32[]{:S(2)}, u32[]{:S(2)}) collective-permute-start(f32[16,1920]{1,0:T(8,128)S(1)} %reshape_reshape.6), channel_id=1, source_target_pairs={{0,16},{16,32},{32,48},{48,64},{64,80},{80,96},{96,112},{112,128},... | collective-permute-start | bytes 368648 | tf_op jit(solution)/shard_map/ppermute | solution.py:10
  37.7 0.8 dynamic_slice.10
  38.6 0.8 dynamic_slice.11
  39.5 4.6 %collective-permute-done = f32[16,1920]{1,0:T(8,128)S(1)} collective-permute-done((f32[16,1920]{1,0:T(8,128)S(1)}, f32[16,1920]{1,0:T(8,128)S(1)}, u32[]{:S(2)}, u32[]{:S(2)}) %collective-permute-start) | collective-permute-done | bytes 122912 | tf_op jit(solution)/shard_map/ppermute | solution.py:10
  44.3 0.7 copy.78
  45.0 4.2 %all-to-all-start = ((bf16[16,2,960]{2,1,0:T(2,128)(2,1)}), bf16[16,2,960]{2,1,0:T(2,128)(2,1)S(1)}, u32[]{:S(2)}, u32[]{:S(2)}) async-start(bf16[16,2,960]{2,1,0:T(2,128)(2,1)} %copy.78), calls=%async_computation | async-start | bytes 131072 | tf_op jit(solution)/shard_map/all_to_all | solution.py:45
  49.4 0.4 reshape.142
  49.8 7.2 %all-to-all-done = bf16[16,2,960]{2,1,0:T(2,128)(2,1)S(1)} async-done(((bf16[16,2,960]{2,1,0:T(2,128)(2,1)}), bf16[16,2,960]{2,1,0:T(2,128)(2,1)S(1)}, u32[]{:S(2)}, u32[]{:S(2)}) %all-to-all-start) | async-done | bytes 61472 | tf_op jit(solution)/shard_map/all_to_all | solution.py:45
  58.1 17.6 %all_gather.7 = bf16[2,16,40,384]{3,2,0,1:T(8,128)(2,1)S(1)} all-gather(bf16[2,1,40,384]{3,2,0,1:T(8,128)(2,1)S(1)} %fusion.27), channel_id=1, replica_groups=mesh['tm'=32,'rows'=16] {'rows'}, dimensions={1}, use_global_device_ids=true | all-gather | bytes 1044480 | tf_op jit(solution)/shard_map/all_gather | solution.py:63
  76.3 3.5 %fusion.21 = f32[16,16,6,72]{3,1,2,0:T(8,128)S(1)} fusion(bf16[72,3,3,384]{3,0,2,1:T(8,128)(2,1)S(1)} %bitcast.77, bf16[16,2,8,8,384]{4,0,3,2,1:T(8,128)(2,1)S(1)} %fusion.11, pred[16,6]{0,1:T(8,128)(4,1)S(1)} %copy-done.4), kind=kOutput, calls=%fused_computation.22 | convolution fusion | flops 732672000 | bytes 2512992 | tf_op jit(solution)/shard_map/conv_general_dilated | solution.py:24
  79.8 0.5 copy.86
  80.3 0.4 slice_add_fusion
  81.0 0.3 reshape_reshape.7
  81.3 1.9 %collective-permute-start.1 = (f32[16,1920]{1,0:T(8,128)S(1)}, f32[16,1920]{1,0:T(8,128)S(1)}, u32[]{:S(2)}, u32[]{:S(2)}) collective-permute-start(f32[16,1920]{1,0:T(8,128)S(1)} %reshape_reshape.7), channel_id=1, source_target_pairs={{0,16},{16,32},{32,48},{48,64},{64,80},{80,96},{96,112},{112,128},... | collective-permute-start | bytes 368648 | tf_op jit(solution)/shard_map/ppermute | solution.py:10
  83.8 7.5 %collective-permute-done.1 = f32[16,1920]{1,0:T(8,128)S(1)} collective-permute-done((f32[16,1920]{1,0:T(8,128)S(1)}, f32[16,1920]{1,0:T(8,128)S(1)}, u32[]{:S(2)}, u32[]{:S(2)}) %collective-permute-start.1) | collective-permute-done | bytes 122912 | tf_op jit(solution)/shard_map/ppermute | solution.py:10
  91.6 12.7 %all_to_all.10 = bf16[16,2,960]{2,1,0:T(2,128)(2,1)S(1)} all-to-all(bf16[16,2,960]{2,1,0:T(2,128)(2,1)S(1)} %copy.90), channel_id=1, replica_groups=mesh['tm'=32,'rows'=16] {'rows'}, dimensions={0} | all-to-all | bytes 122880 | tf_op jit(solution)/shard_map/all_to_all | solution.py:45
  104.9 0.7 copy.93
  (55 shorter events, 5.3 us)
Async XLA Ops:
  0.0 27.1 %copy-start.2 = (f32[384]{0:T(512)S(1)}, f32[384]{0:T(512)}, u32[]{:S(2)}) copy-start(f32[384]{0:T(512)} %param.8) | copy-start | bytes 4612
  27.9 1.0 copy-start
  28.0 1.1 %copy-start.4 = (pred[16,6]{0,1:T(8,128)(4,1)S(1)}, pred[16,6]{0,1:T(8,128)(4,1)}, u32[]{:S(2)}) copy-start(pred[16,6]{0,1:T(8,128)(4,1)} %constant.36) | copy-start | bytes 292
  33.8 4.8 %copy-start.1 = (bf16[24,3,3,3,384]{4,0,3,2,1:T(8,128)(2,1)S(1)}, bf16[24,3,3,3,384]{4,0,3,2,1:T(8,128)(2,1)}, u32[]{:S(2)}) copy-start(bf16[24,3,3,3,384]{4,0,3,2,1:T(8,128)(2,1)} %param.12) | copy-start | bytes 1492996
  34.1 10.0 %collective-permute-start = (f32[16,1920]{1,0:T(8,128)S(1)}, f32[16,1920]{1,0:T(8,128)S(1)}, u32[]{:S(2)}, u32[]{:S(2)}) collective-permute-start(f32[16,1920]{1,0:T(8,128)S(1)} %reshape_reshape.6), channel_id=1, source_target_pairs={{0,16},{16,32},{32,48},{48,64},{64,80},{80,96},{96,112},{112,128},... | collective-permute-start | bytes 368648 | tf_op jit(solution)/shard_map/ppermute | solution.py:10
  45.0 12.1 %all-to-all-start = ((bf16[16,2,960]{2,1,0:T(2,128)(2,1)}), bf16[16,2,960]{2,1,0:T(2,128)(2,1)S(1)}, u32[]{:S(2)}, u32[]{:S(2)}) async-start(bf16[16,2,960]{2,1,0:T(2,128)(2,1)} %copy.78), calls=%async_computation | async-start | bytes 131072 | tf_op jit(solution)/shard_map/all_to_all | solution.py:45
  49.4 8.6 %copy-start.3 = (f32[384]{0:T(512)S(1)}, f32[384]{0:T(512)}, u32[]{:S(2)}) copy-start(f32[384]{0:T(512)} %param.11) | copy-start | bytes 4612
  81.3 10.0 %collective-permute-start.1 = (f32[16,1920]{1,0:T(8,128)S(1)}, f32[16,1920]{1,0:T(8,128)S(1)}, u32[]{:S(2)}, u32[]{:S(2)}) collective-permute-start(f32[16,1920]{1,0:T(8,128)S(1)} %reshape_reshape.7), channel_id=1, source_target_pairs={{0,16},{16,32},{32,48},{48,64},{64,80},{80,96},{96,112},{112,128},... | collective-permute-start | bytes 368648 | tf_op jit(solution)/shard_map/ppermute | solution.py:10
